TPU v7x, 128 devices: a whole 4x4x4 slice. The times are simulated.
128 devices in a mesh: grains: 128 (over z, x, y, core).
Axes of the slice: x: 4, y: 4, z: 4, core: 2. Of those that a mesh axis runs over, the one named last changes fastest.
Arguments:
- tangent: float32 [8192, 128, 128], P('grains'), may hold values from -48 to 48
- blocks: bfloat16 [8192, 8, 128, 128], P('grains'), may hold values from -0.1875 to 0.1875
- columns: int32 [8192, 8], P('grains'), may hold values from 0 to 95, as said below
- counts: int32 [128], P('grains'), may hold values from 32 to 64, as said below
- send_lists: int32 [128, 2, 16], P('grains'), may hold values from 0 to 63, as said below
Outputs:
- basis: float32 [8192, 128, 128], P('grains')
- r_factor: float32 [128, 128], replicated
Inputs may be any that keep to these rules, and one draw needn't show every extreme that they name: `counts`: some device has exactly 64 live block rows; every device has at least 32. Every entry of send_lists[d] is below counts[d]. For block row b of device d, columns[., 0] is b; every other entry is below counts[d] or lies in 64 to 64 + 2 * 16 - 1 (received rows). Entries of slots that are not live follow the same law.
All inputs are finite; a program needn't handle non-finite values.
Results may differ from a plain program's by a relative error of at most 0.0028.
Values may be sent and summed in bfloat16 or wider, within the bound.
No kernel may reach another device: no remote copies, remote signals or barrier semaphores. Data moves between devices by JAX's collectives and lax.ppermute only.
A program may use at most 128 MiB of HBM per device.

v0:
```python
import jax
import jax.numpy as jnp
from jax import lax
from jax.sharding import PartitionSpec as P

SUBSTEPS = 3


def passed_along(shard, axis, by):
    length = lax.axis_size(axis)
    return lax.ppermute(shard, axis, [(i, (i + by) % length) for i in range(length)])


def apply_inverse(matrix, lower):
    return lax.linalg.triangular_solve(lower, matrix, left_side=False, lower=True, transpose_a=True)


def local(tangent, blocks, columns, counts, send_lists):
    slots, width, vectors = tangent.shape
    live = (jnp.arange(slots, dtype=jnp.int32) < counts[0]).astype(jnp.float32)[:, None, None]
    state = tangent * live
    for step in range(SUBSTEPS):
        rounded = state.astype(jnp.bfloat16)
        to_lower = rounded[send_lists[0, 0]]
        to_upper = rounded[send_lists[0, 1]]
        from_lower = passed_along(to_upper, "grains", 1)
        from_upper = passed_along(to_lower, "grains", -1)
        extended = jnp.concatenate([rounded, from_lower, from_upper], axis=0)
        gathered = extended[columns]
        update = jnp.einsum("bkij,bkjv->biv", blocks, gathered, preferred_element_type=jnp.float32)
        state = state + update * live
    flat = state.reshape(slots * width, vectors)
    first_low = jnp.linalg.cholesky(
        lax.psum(jnp.einsum("rk,rv->kv", flat, flat, precision=lax.Precision.HIGHEST), "grains")
    )
    basis = apply_inverse(flat, first_low)
    r_factor = first_low.T
    return (basis.reshape(slots, width, vectors), r_factor)


def solution(mesh):
    in_specs = (
        P("grains", None, None),
        P("grains", None, None, None),
        P("grains", None),
        P("grains"),
        P("grains", None, None),
    )
    out_specs = (P("grains", None, None), P())
    return jax.shard_map(local, mesh=mesh, in_specs=in_specs, out_specs=out_specs, check_vma=False)
```

profile of v0, /device:TPU:0, one launch (start us, length us, event | category | flops | bytes accessed | tf_op | source)
XLA Modules:
  0.0 345.0 jit_solution(11176043454755930773)
XLA Ops:
  7.2 0.0 all-reduce.2.cloned.1.call-start
  7.9 0.8 fusion.4
  8.6 0.0 copy-start.4
  8.6 4.8 %fusion.6 = (bf16[64,128,128]{2,1,0:T(8,128)(2,1)S(1)}, f32[64,128,128]{2,1,0:T(8,128)}) fusion(f32[64,128,128]{2,1,0:T(8,128)} %param.5, f32[64]{0:T(128)S(1)} %compare_convert_fusion), kind=kLoop, calls=%fused_computation.40 | loop fusion | flops 2097152 | bytes 10486016 | tf_op jit(solution)/shard_map/convert_element_type | solution.py:23
  13.5 0.6 gather_fusion
  14.1 0.1 collective-permute-start
  14.2 1.4 gather_fusion.1
  15.6 8.2 %collective-permute-start.1 = (bf16[16,128,128]{2,1,0:T(8,128)(2,1)}, bf16[16,128,128]{2,1,0:T(8,128)(2,1)}, u32[]{:S(2)}, u32[]{:S(2)}) collective-permute-start(bf16[16,128,128]{2,1,0:T(8,128)(2,1)} %gather_fusion.1), channel_id=1, source_target_pairs={{0,127},{1,0},{2,1},{3,2},{4,3},{5,4},{6,5},{7,6},{8,7},{9,8},{10,... | collective-permute-start | bytes 1572872 | tf_op jit(solution)/shard_map/ppermute | solution.py:11
  23.9 0.1 copy.15
  24.0 0.1 reshape.96
  24.0 5.6 %copy.17 = f32[64,128,128]{1,2,0:T(8,128)} copy(f32[64,128,128]{2,1,0:T(8,128)} %get-tuple-element.7) | data formatting | bytes 8388608 | tf_op jit(solution)/shard_map/mul | solution.py:21
  29.7 0.0 collective-permute-done
  29.7 0.0 copy-start.3
  29.7 0.8 copy-done.3
  30.5 0.4 collective-permute-done.1
  30.9 2.1 pad_maximum_fusion
  33.0 13.9 %gather_fusion.2 = bf16[512,128,128]{2,1,0:T(8,128)(2,1)} fusion(bf16[96,128,128]{2,1,0:T(8,128)(2,1)S(1)} %pad_maximum_fusion, s32[1024]{0:T(1024)S(1)} %pad_clamp_fusion), kind=kCustom, calls=%fused_computation.2 | custom fusion | bytes 33556480 | tf_op jit(solution)/shard_map/gather | solution.py:29
  46.9 15.8 %fusion.7 = (bf16[64,128,128]{1,2,0:T(8,128)(2,1)S(1)}, f32[64,128,128]{1,2,0:T(8,128)}) fusion(f32[64,128,128]{1,2,0:T(8,128)} %copy.17, f32[64]{0:T(128)S(1)} %compare_convert_fusion, bf16[64,8,128,128]{3,2,1,0:T(8,128)(2,1)} %bitcast.59, bf16[64,8,128,128]{3,2,1,0:T(8,128)(2,1)} %param.6), kind=kOutput, calls=%fused_computation.41 | convolution fusion | flops 2150629376 | bytes 44040448 | tf_op jit(solution)/shard_map/bkij,bkjv->biv/dot_general | solution.py:30
  62.7 0.6 gather_fusion.4
  63.4 0.6 gather_fusion.3
  64.0 0.1 collective-permute-start.2
  64.1 7.6 %collective-permute-start.3 = (bf16[16,128,128]{1,2,0:T(8,128)(2,1)S(1)}, bf16[16,128,128]{1,2,0:T(8,128)(2,1)S(1)}, u32[]{:S(2)}, u32[]{:S(2)}) collective-permute-start(bf16[16,128,128]{1,2,0:T(8,128)(2,1)S(1)} %gather_fusion.4), channel_id=1, source_target_pairs={{0,127},{1,0},{2,1},{3,2},{4,3},{5,4},{6,5},{7,6},{8,7},{9,8},{10,... | collective-permute-start | bytes 1572872 | tf_op jit(solution)/shard_map/ppermute | solution.py:11
  71.7 6.6 %collective-permute-done.2 = bf16[16,128,128]{1,2,0:T(8,128)(2,1)S(1)} collective-permute-done((bf16[16,128,128]{1,2,0:T(8,128)(2,1)S(1)}, bf16[16,128,128]{1,2,0:T(8,128)(2,1)S(1)}, u32[]{:S(2)}, u32[]{:S(2)}) %collective-permute-start.2) | collective-permute-done | bytes 524320 | tf_op jit(solution)/shard_map/ppermute | solution.py:11
  78.3 0.1 collective-permute-done.3
  78.4 1.8 pad_maximum_fusion.1
  80.2 13.9 %gather_fusion.5 = bf16[512,128,128]{1,2,0:T(8,128)(2,1)} fusion(bf16[96,128,128]{1,2,0:T(8,128)(2,1)S(1)} %pad_maximum_fusion.1, s32[1024]{0:T(1024)S(1)} %pad_clamp_fusion), kind=kCustom, calls=%fused_computation.5 | custom fusion | bytes 33556480 | tf_op jit(solution)/shard_map/gather | solution.py:29
  94.1 15.6 %fusion.8 = (bf16[64,128,128]{1,2,0:T(8,128)(2,1)S(1)}, f32[64,128,128]{1,2,0:T(8,128)}) fusion(f32[64,128,128]{1,2,0:T(8,128)} %get-tuple-element.13, f32[64]{0:T(128)S(1)} %compare_convert_fusion, bf16[64,8,128,128]{2,3,1,0:T(8,128)(2,1)} %bitcast.60, bf16[64,8,128,128]{3,2,1,0:T(8,128)(2,1)} %param.6), kind=kOutput, calls=%fused_computation.42 | convolution fusion | flops 2150629376 | bytes 44040448 | tf_op jit(solution)/shard_map/bkij,bkjv->biv/dot_general | solution.py:30
  109.7 0.6 gather_fusion.7
  110.4 0.6 gather_fusion.6
  111.0 0.1 collective-permute-start.4
  111.1 7.4 %collective-permute-start.5 = (bf16[16,128,128]{1,2,0:T(8,128)(2,1)S(1)}, bf16[16,128,128]{1,2,0:T(8,128)(2,1)S(1)}, u32[]{:S(2)}, u32[]{:S(2)}) collective-permute-start(bf16[16,128,128]{1,2,0:T(8,128)(2,1)S(1)} %gather_fusion.7), channel_id=1, source_target_pairs={{0,127},{1,0},{2,1},{3,2},{4,3},{5,4},{6,5},{7,6},{8,7},{9,8},{10,... | collective-permute-start | bytes 1572872 | tf_op jit(solution)/shard_map/ppermute | solution.py:11
  118.5 6.8 %collective-permute-done.4 = bf16[16,128,128]{1,2,0:T(8,128)(2,1)S(1)} collective-permute-done((bf16[16,128,128]{1,2,0:T(8,128)(2,1)S(1)}, bf16[16,128,128]{1,2,0:T(8,128)(2,1)S(1)}, u32[]{:S(2)}, u32[]{:S(2)}) %collective-permute-start.4) | collective-permute-done | bytes 524320 | tf_op jit(solution)/shard_map/ppermute | solution.py:11
  125.3 0.0 copy-done.1
  125.3 0.0 collective-permute-done.5
  125.3 1.8 pad_maximum_fusion.2
  127.1 13.9 %gather_fusion.8 = bf16[512,128,128]{1,2,0:T(8,128)(2,1)} fusion(bf16[96,128,128]{1,2,0:T(8,128)(2,1)S(1)} %pad_maximum_fusion.2, s32[1024]{0:T(1024)S(1)} %pad_clamp_fusion), kind=kCustom, calls=%fused_computation.8 | custom fusion | bytes 33556480 | tf_op jit(solution)/shard_map/gather | solution.py:29
  141.0 16.2 %bitcast_add_fusion = f32[64,128,128]{1,2,0:T(8,128)} fusion(f32[64,128,128]{1,2,0:T(8,128)} %get-tuple-element.15, bf16[64,8,128,128]{2,3,1,0:T(8,128)(2,1)} %bitcast.58, bf16[64,8,128,128]{3,2,1,0:T(8,128)(2,1)} %param.6, f32[64]{0:T(128)S(1)} %compare_convert_fusion), kind=kOutput, calls=%fused_computation.9 | convolution fusion | flops 2149580800 | bytes 41943296 | tf_op jit(solution)/shard_map/bkij,bkjv->biv/dot_general | solution.py:30
  157.2 7.6 %convolution_bitcast_fusion = f32[128,128]{0,1:T(8,128)} fusion(f32[64,128,128]{1,2,0:T(8,128)} %bitcast_add_fusion), kind=kOutput, calls=%fused_computation.19 | convolution fusion | flops 1610612736 | bytes 4259840 | tf_op jit(solution)/shard_map/rk,rv->kv/dot_general | solution.py:34
  164.8 0.0 all-reduce.2.cloned.1.call-update
  164.8 137.9 %all-reduce.2.cloned.1.call-done = f32[128,128]{0,1:T(8,128)} async-done(((f32[128,128]{0,1:T(8,128)}), f32[128,128]{0,1:T(8,128)}) %all-reduce.2.cloned.1.call-update) | async-done | bytes 65552 | tf_op jit(solution)/shard_map/psum | solution.py:34
  302.7 0.9 copy.20
  303.6 0.9 fusion.2
  304.5 11.7 %cholesky.16 = f32[128,128]{1,0:T(8,128)S(1)} custom-call(f32[128,128]{1,0:T(8,128)S(1)} %fusion.2), custom_call_target="Cholesky" | custom-call | tf_op jit(solution)/shard_map/jit(cholesky)/cholesky | solution.py:33
  316.2 0.6 compare_reduce_fusion
  316.9 0.7 fusion.3
  317.6 0.7 copy.23
  318.3 9.8 %custom-call.6 = f32[1,128,128]{1,2,0:T(8,128)S(1)} custom-call(f32[1,128,128]{2,1,0:T(8,128)S(1)} %get-tuple-element.9), custom_call_target="InvertDiagBlocksLowerTriangular" | custom-call | tf_op jit(solution)/shard_map/triangular_solve | solution.py:15
  328.1 10.1 %fusion = f32[64,128,128]{2,1,0:T(8,128)} fusion(f32[64,128,128]{1,2,0:T(8,128)} %bitcast_add_fusion, f32[1,128,128]{1,2,0:T(8,128)S(1)} %custom-call.6), kind=kOutput, calls=%fused_computation.20 | convolution fusion | flops 1610612736 | bytes 8454144 | tf_op jit(solution)/shard_map/triangular_solve | solution.py:15
  (12 shorter events, 0.1 us)
Async XLA Ops:
  7.2 295.5 %all-reduce.2.cloned.1.call-start = ((), (), s32[]{:S(2)}) async-start(), calls=%async_computation | async-start | bytes 131072 | tf_op jit(solution)/shard_map/psum | solution.py:34
  8.6 15.2 %copy-start.4 = (s32[64,8]{0,1:T(8,128)S(1)}, s32[64,8]{0,1:T(8,128)}, u32[]{:S(2)}) copy-start(s32[64,8]{0,1:T(8,128)} %param.7) | copy-start | bytes 6148
  13.5 16.2 %copy-start.2 = (bf16[64,128,128]{2,1,0:T(8,128)(2,1)}, bf16[64,128,128]{2,1,0:T(8,128)(2,1)S(1)}, u32[]{:S(2)}) copy-start(bf16[64,128,128]{2,1,0:T(8,128)(2,1)S(1)} %get-tuple-element.6) | copy-start | bytes 6291460
  14.1 15.6 %collective-permute-start = (bf16[16,128,128]{2,1,0:T(8,128)(2,1)S(1)}, bf16[16,128,128]{2,1,0:T(8,128)(2,1)S(1)}, u32[]{:S(2)}, u32[]{:S(2)}) collective-permute-start(bf16[16,128,128]{2,1,0:T(8,128)(2,1)S(1)} %gather_fusion), channel_id=1, source_target_pairs={{0,1},{1,2},{2,3},{3,4},{4,5},{5,6},{6,7},{7,8},{8,9},{9,10},{10,1... | collective-permute-start | bytes 1572872 | tf_op jit(solution)/shard_map/ppermute | solution.py:11
  15.6 15.2 %collective-permute-start.1 = (bf16[16,128,128]{2,1,0:T(8,128)(2,1)}, bf16[16,128,128]{2,1,0:T(8,128)(2,1)}, u32[]{:S(2)}, u32[]{:S(2)}) collective-permute-start(bf16[16,128,128]{2,1,0:T(8,128)(2,1)} %gather_fusion.1), channel_id=1, source_target_pairs={{0,127},{1,0},{2,1},{3,2},{4,3},{5,4},{6,5},{7,6},{8,7},{9,8},{10,... | collective-permute-start | bytes 1572872 | tf_op jit(solution)/shard_map/ppermute | solution.py:11
  29.7 0.8 copy-start.3
  62.7 15.6 %copy-start = (bf16[64,128,128]{1,2,0:T(8,128)(2,1)}, bf16[64,128,128]{1,2,0:T(8,128)(2,1)S(1)}, u32[]{:S(2)}) copy-start(bf16[64,128,128]{1,2,0:T(8,128)(2,1)S(1)} %get-tuple-element.12) | copy-start | bytes 6291460
  64.0 14.3 %collective-permute-start.2 = (bf16[16,128,128]{1,2,0:T(8,128)(2,1)S(1)}, bf16[16,128,128]{1,2,0:T(8,128)(2,1)S(1)}, u32[]{:S(2)}, u32[]{:S(2)}) collective-permute-start(bf16[16,128,128]{1,2,0:T(8,128)(2,1)S(1)} %gather_fusion.3), channel_id=1, source_target_pairs={{0,1},{1,2},{2,3},{3,4},{4,5},{5,6},{6,7},{7,8},{8,9},{9,10},{10,1... | collective-permute-start | bytes 1572872 | tf_op jit(solution)/shard_map/ppermute | solution.py:11
  64.1 14.3 %collective-permute-start.3 = (bf16[16,128,128]{1,2,0:T(8,128)(2,1)S(1)}, bf16[16,128,128]{1,2,0:T(8,128)(2,1)S(1)}, u32[]{:S(2)}, u32[]{:S(2)}) collective-permute-start(bf16[16,128,128]{1,2,0:T(8,128)(2,1)S(1)} %gather_fusion.4), channel_id=1, source_target_pairs={{0,127},{1,0},{2,1},{3,2},{4,3},{5,4},{6,5},{7,6},{8,7},{9,8},{10,... | collective-permute-start | bytes 1572872 | tf_op jit(solution)/shard_map/ppermute | solution.py:11
  109.7 15.6 %copy-start.1 = (bf16[64,128,128]{1,2,0:T(8,128)(2,1)}, bf16[64,128,128]{1,2,0:T(8,128)(2,1)S(1)}, u32[]{:S(2)}) copy-start(bf16[64,128,128]{1,2,0:T(8,128)(2,1)S(1)} %get-tuple-element.14) | copy-start | bytes 6291460
  111.0 14.3 %collective-permute-start.4 = (bf16[16,128,128]{1,2,0:T(8,128)(2,1)S(1)}, bf16[16,128,128]{1,2,0:T(8,128)(2,1)S(1)}, u32[]{:S(2)}, u32[]{:S(2)}) collective-permute-start(bf16[16,128,128]{1,2,0:T(8,128)(2,1)S(1)} %gather_fusion.6), channel_id=1, source_target_pairs={{0,1},{1,2},{2,3},{3,4},{4,5},{5,6},{6,7},{7,8},{8,9},{9,10},{10,1... | collective-permute-start | bytes 1572872 | tf_op jit(solution)/shard_map/ppermute | solution.py:11
  111.1 14.2 %collective-permute-start.5 = (bf16[16,128,128]{1,2,0:T(8,128)(2,1)S(1)}, bf16[16,128,128]{1,2,0:T(8,128)(2,1)S(1)}, u32[]{:S(2)}, u32[]{:S(2)}) collective-permute-start(bf16[16,128,128]{1,2,0:T(8,128)(2,1)S(1)} %gather_fusion.7), channel_id=1, source_target_pairs={{0,127},{1,0},{2,1},{3,2},{4,3},{5,4},{6,5},{7,6},{8,7},{9,8},{10,... | collective-permute-start | bytes 1572872 | tf_op jit(solution)/shard_map/ppermute | solution.py:11
Sparse Core Ops, SparseCore 0:
  164.9 137.7 all-reduce.1
where the time goes:
time: 349 us; the launch traced here: 345 us
  waiting for transfers between devices  152 us (44%)
  matrix products  65.3 us (19%)
  local copies, waits for them, and re-layouts  54.7 us (16%)
  other arithmetic  34.9 us (10%)
  starting transfers between devices  23.5 us (7%)
  between operations  14.8 us (4%)
    psum x1, waiting for transfers between devices, local(): lax.psum(jnp.einsum('rk,rv->kv', flat, flat, precision=lax.Precision.HIGH...  138 us
    dot_general x3, matrix products, local(): jnp.einsum('bkij,bkjv->biv', blocks, gathered, preferred_element_type=jnp...  47.6 us
    gather x3, local copies, waits for them, and re-layouts, local(): gathered = extended[columns]  41.7 us
    ppermute x6, starting transfers between devices, passed_along(): lax.ppermute(shard, axis, [(i, (i + by) % length) for i in range(length)])  23.5 us
    ppermute x6, waiting for transfers between devices, passed_along(): lax.ppermute(shard, axis, [(i, (i + by) % length) for i in range(length)])  13.9 us
    another operation x3, other arithmetic, local(): jnp.linalg.cholesky(lax.psum(jnp.einsum('rk,rv->kv', flat, flat, precisio...  12.4 us
    another operation x1, matrix products, apply_inverse(): lax.linalg.triangular_solve(lower, matrix, left_side=False, lower=True, t...  10.1 us
    another operation x1, other arithmetic, apply_inverse(): lax.linalg.triangular_solve(lower, matrix, left_side=False, lower=True, t...  9.81 us
  transfers between devices with their start and end apart: 7, of which 5 were waited for; matrix products, arithmetic and copies ran while one was open for 2% of the time, Pallas kernels for 0%

commit v1 on v0

--- a/solution.py
+++ b/solution.py
@@ -9,6 +9,16 @@
 def passed_along(shard, axis, by):
     length = lax.axis_size(axis)
     return lax.ppermute(shard, axis, [(i, (i + by) % length) for i in range(length)])
+
+
+def tree_sum(value, axis):
+    length = lax.axis_size(axis)
+    distance = 1
+    while distance < length:
+        partner = [(i, i ^ distance) for i in range(length)]
+        value = value + lax.ppermute(value, axis, partner)
+        distance *= 2
+    return value
 
 
 def apply_inverse(matrix, lower):
@@ -31,7 +41,7 @@
         state = state + update * live
     flat = state.reshape(slots * width, vectors)
     first_low = jnp.linalg.cholesky(
-        lax.psum(jnp.einsum("rk,rv->kv", flat, flat, precision=lax.Precision.HIGHEST), "grains")
+        tree_sum(jnp.einsum("rk,rv->kv", flat, flat, precision=lax.Precision.HIGHEST), "grains")
     )
     basis = apply_inverse(flat, first_low)
     r_factor = first_low.T

time: 349 us -> 224 us (0.64); the launches traced: 345 us -> 224 us
  waiting for transfers between devices: 152 us -> 45.1 us
  between operations: 14.8 us -> 1.54 us
    psum x1 -> x0, waiting for transfers between devices: 138 us -> none  [local(): lax.psum(jnp.einsum('rk,rv->kv', flat, flat, precision=lax.Precision.HIGH...]
    ppermute x0 -> x7, waiting for transfers between devices: none -> 31.4 us  [tree_sum(): value = value + lax.ppermute(value, axis, partner)]
  transfers between devices with their start and end apart: 7 -> 13, of which waited for: 5 -> 12; matrix products, arithmetic and copies ran while one was open for 2% -> 3% of each run, Pallas kernels for 0% -> 0%
where the time goes in v1:
time: 224 us
  matrix products  64.4 us (29%)
  local copies, waits for them, and re-layouts  53.9 us (24%)
  waiting for transfers between devices  45.1 us (20%)
  other arithmetic  34.1 us (15%)
  starting transfers between devices  24.7 us (11%)
    dot_general x3, matrix products, local(): jnp.einsum('bkij,bkjv->biv', blocks, gathered, preferred_element_type=jnp...  47.6 us
    gather x3, local copies, waits for them, and re-layouts, local(): gathered = extended[columns]  41.8 us
    ppermute x7, waiting for transfers between devices, tree_sum(): value = value + lax.ppermute(value, axis, partner)  31.4 us
    ppermute x6, starting transfers between devices, passed_along(): lax.ppermute(shard, axis, [(i, (i + by) % length) for i in range(length)])  23.7 us
    ppermute x6, waiting for transfers between devices, passed_along(): lax.ppermute(shard, axis, [(i, (i + by) % length) for i in range(length)])  13.8 us
    another operation x3, other arithmetic, local(): jnp.linalg.cholesky(tree_sum(jnp.einsum('rk,rv->kv', flat, flat, precisio...  12.4 us
    another operation x1, other arithmetic, apply_inverse(): lax.linalg.triangular_solve(lower, matrix, left_side=False, lower=True, t...  9.81 us
    another operation x1, matrix products, apply_inverse(): lax.linalg.triangular_solve(lower, matrix, left_side=False, lower=True, t...  9.79 us
  transfers between devices with their start and end apart: 13, of which 12 were waited for; matrix products, arithmetic and copies ran while one was open for 3% of the time, Pallas kernels for 0%

profile of v1, /device:TPU:0, one launch (start us, length us, event | category | flops | bytes accessed | tf_op | source)
XLA Modules:
  0.0 223.8 jit_solution(4304443293915751713)
XLA Ops:
  1.3 0.8 fusion.4
  2.1 4.8 %fusion.6 = (bf16[64,128,128]{2,1,0:T(8,128)(2,1)S(1)}, f32[64,128,128]{2,1,0:T(8,128)}) fusion(f32[64,128,128]{2,1,0:T(8,128)} %param.5, f32[64]{0:T(128)S(1)} %compare_convert_fusion), kind=kLoop, calls=%fused_computation.40 | loop fusion | flops 2097152 | bytes 10486016 | tf_op jit(solution)/shard_map/convert_element_type | solution.py:33
  6.9 0.6 gather_fusion
  7.6 1.4 gather_fusion.1
  9.1 8.2 %collective-permute-start.1 = (bf16[16,128,128]{2,1,0:T(8,128)(2,1)}, bf16[16,128,128]{2,1,0:T(8,128)(2,1)}, u32[]{:S(2)}, u32[]{:S(2)}) collective-permute-start(bf16[16,128,128]{2,1,0:T(8,128)(2,1)} %gather_fusion.1), channel_id=1, source_target_pairs={{0,127},{1,0},{2,1},{3,2},{4,3},{5,4},{6,5},{7,6},{8,7},{9,8},{10,... | collective-permute-start | bytes 1572872 | tf_op jit(solution)/shard_map/ppermute | solution.py:11
  17.3 0.1 copy.16
  17.4 0.1 reshape.96
  17.5 5.6 %copy.18 = f32[64,128,128]{1,2,0:T(8,128)} copy(f32[64,128,128]{2,1,0:T(8,128)} %get-tuple-element.7) | data formatting | bytes 8388608 | tf_op jit(solution)/shard_map/mul | solution.py:31
  23.1 0.8 copy-done.3
  23.9 0.4 collective-permute-done.1
  24.3 2.1 pad_maximum_fusion
  26.4 13.9 %gather_fusion.2 = bf16[512,128,128]{2,1,0:T(8,128)(2,1)} fusion(bf16[96,128,128]{2,1,0:T(8,128)(2,1)S(1)} %pad_maximum_fusion, s32[1024]{0:T(1024)S(1)} %pad_clamp_fusion), kind=kCustom, calls=%fused_computation.2 | custom fusion | bytes 33556480 | tf_op jit(solution)/shard_map/gather | solution.py:39
  40.3 15.8 %fusion.7 = (bf16[64,128,128]{1,2,0:T(8,128)(2,1)S(1)}, f32[64,128,128]{1,2,0:T(8,128)}) fusion(f32[64,128,128]{1,2,0:T(8,128)} %copy.18, f32[64]{0:T(128)S(1)} %compare_convert_fusion, bf16[64,8,128,128]{3,2,1,0:T(8,128)(2,1)} %bitcast.61, bf16[64,8,128,128]{3,2,1,0:T(8,128)(2,1)} %param.6), kind=kOutput, calls=%fused_computation.41 | convolution fusion | flops 2150629376 | bytes 44040448 | tf_op jit(solution)/shard_map/bkij,bkjv->biv/dot_general | solution.py:40
  56.2 0.6 gather_fusion.4
  56.8 0.6 gather_fusion.3
  57.6 7.6 %collective-permute-start.3 = (bf16[16,128,128]{1,2,0:T(8,128)(2,1)S(1)}, bf16[16,128,128]{1,2,0:T(8,128)(2,1)S(1)}, u32[]{:S(2)}, u32[]{:S(2)}) collective-permute-start(bf16[16,128,128]{1,2,0:T(8,128)(2,1)S(1)} %gather_fusion.4), channel_id=1, source_target_pairs={{0,127},{1,0},{2,1},{3,2},{4,3},{5,4},{6,5},{7,6},{8,7},{9,8},{10,... | collective-permute-start | bytes 1572872 | tf_op jit(solution)/shard_map/ppermute | solution.py:11
  65.2 6.6 %collective-permute-done.2 = bf16[16,128,128]{1,2,0:T(8,128)(2,1)S(1)} collective-permute-done((bf16[16,128,128]{1,2,0:T(8,128)(2,1)S(1)}, bf16[16,128,128]{1,2,0:T(8,128)(2,1)S(1)}, u32[]{:S(2)}, u32[]{:S(2)}) %collective-permute-start.2) | collective-permute-done | bytes 524320 | tf_op jit(solution)/shard_map/ppermute | solution.py:11
  71.8 0.1 collective-permute-done.3
  71.9 1.8 pad_maximum_fusion.1
  73.6 13.9 %gather_fusion.5 = bf16[512,128,128]{1,2,0:T(8,128)(2,1)} fusion(bf16[96,128,128]{1,2,0:T(8,128)(2,1)S(1)} %pad_maximum_fusion.1, s32[1024]{0:T(1024)S(1)} %pad_clamp_fusion), kind=kCustom, calls=%fused_computation.5 | custom fusion | bytes 33556480 | tf_op jit(solution)/shard_map/gather | solution.py:39
  87.6 15.6 %fusion.8 = (bf16[64,128,128]{1,2,0:T(8,128)(2,1)S(1)}, f32[64,128,128]{1,2,0:T(8,128)}) fusion(f32[64,128,128]{1,2,0:T(8,128)} %get-tuple-element.13, f32[64]{0:T(128)S(1)} %compare_convert_fusion, bf16[64,8,128,128]{2,3,1,0:T(8,128)(2,1)} %bitcast.62, bf16[64,8,128,128]{3,2,1,0:T(8,128)(2,1)} %param.6), kind=kOutput, calls=%fused_computation.42 | convolution fusion | flops 2150629376 | bytes 44040448 | tf_op jit(solution)/shard_map/bkij,bkjv->biv/dot_general | solution.py:40
  103.2 0.6 gather_fusion.7
  103.8 0.6 gather_fusion.6
  104.6 7.6 %collective-permute-start.5 = (bf16[16,128,128]{1,2,0:T(8,128)(2,1)S(1)}, bf16[16,128,128]{1,2,0:T(8,128)(2,1)S(1)}, u32[]{:S(2)}, u32[]{:S(2)}) collective-permute-start(bf16[16,128,128]{1,2,0:T(8,128)(2,1)S(1)} %gather_fusion.7), channel_id=1, source_target_pairs={{0,127},{1,0},{2,1},{3,2},{4,3},{5,4},{6,5},{7,6},{8,7},{9,8},{10,... | collective-permute-start | bytes 1572872 | tf_op jit(solution)/shard_map/ppermute | solution.py:11
  112.2 6.6 %collective-permute-done.4 = bf16[16,128,128]{1,2,0:T(8,128)(2,1)S(1)} collective-permute-done((bf16[16,128,128]{1,2,0:T(8,128)(2,1)S(1)}, bf16[16,128,128]{1,2,0:T(8,128)(2,1)S(1)}, u32[]{:S(2)}, u32[]{:S(2)}) %collective-permute-start.4) | collective-permute-done | bytes 524320 | tf_op jit(solution)/shard_map/ppermute | solution.py:11
  118.8 0.1 collective-permute-done.5
  118.9 1.8 pad_maximum_fusion.2
  120.7 13.9 %gather_fusion.8 = bf16[512,128,128]{1,2,0:T(8,128)(2,1)} fusion(bf16[96,128,128]{1,2,0:T(8,128)(2,1)S(1)} %pad_maximum_fusion.2, s32[1024]{0:T(1024)S(1)} %pad_clamp_fusion), kind=kCustom, calls=%fused_computation.8 | custom fusion | bytes 33556480 | tf_op jit(solution)/shard_map/gather | solution.py:39
  134.6 16.2 %bitcast_add_fusion = f32[64,128,128]{1,2,0:T(8,128)} fusion(f32[64,128,128]{1,2,0:T(8,128)} %get-tuple-element.15, bf16[64,8,128,128]{2,3,1,0:T(8,128)(2,1)} %bitcast.60, bf16[64,8,128,128]{3,2,1,0:T(8,128)(2,1)} %param.6, f32[64]{0:T(128)S(1)} %compare_convert_fusion), kind=kOutput, calls=%fused_computation.9 | convolution fusion | flops 2149580800 | bytes 41943296 | tf_op jit(solution)/shard_map/bkij,bkjv->biv/dot_general | solution.py:40
  150.8 7.0 %convolution_bitcast_fusion = f32[128,128]{0,1:T(8,128)S(1)} fusion(f32[64,128,128]{1,2,0:T(8,128)} %bitcast_add_fusion), kind=kOutput, calls=%fused_computation.19 | convolution fusion | flops 1610612736 | bytes 4259840 | tf_op jit(solution)/shard_map/rk,rv->kv/dot_general | solution.py:44
  157.8 0.1 collective-permute-start.6
  157.8 1.2 collective-permute-done.6
  159.1 0.1 collective-permute-start.7
  159.2 4.3 %collective-permute-done.7 = f32[128,128]{0,1:T(8,128)S(1)} collective-permute-done((f32[128,128]{0,1:T(8,128)S(1)}, f32[128,128]{0,1:T(8,128)S(1)}, u32[]{:S(2)}, u32[]{:S(2)}) %collective-permute-start.7) | collective-permute-done | bytes 65568 | tf_op jit(solution)/shard_map/ppermute | solution.py:19
  163.5 5.8 %collective-permute-done.8 = f32[128,128]{0,1:T(8,128)S(1)} collective-permute-done((f32[128,128]{0,1:T(8,128)S(1)}, f32[128,128]{0,1:T(8,128)S(1)}, u32[]{:S(2)}, u32[]{:S(2)}) %collective-permute-start.8) | collective-permute-done | bytes 65568 | tf_op jit(solution)/shard_map/ppermute | solution.py:19
  169.4 4.3 %collective-permute-done.9 = f32[128,128]{0,1:T(8,128)S(1)} collective-permute-done((f32[128,128]{0,1:T(8,128)S(1)}, f32[128,128]{0,1:T(8,128)S(1)}, u32[]{:S(2)}, u32[]{:S(2)}) %collective-permute-start.9) | collective-permute-done | bytes 65568 | tf_op jit(solution)/shard_map/ppermute | solution.py:19
  173.8 5.8 %collective-permute-done.10 = f32[128,128]{0,1:T(8,128)S(1)} collective-permute-done((f32[128,128]{0,1:T(8,128)S(1)}, f32[128,128]{0,1:T(8,128)S(1)}, u32[]{:S(2)}, u32[]{:S(2)}) %collective-permute-start.10) | collective-permute-done | bytes 65568 | tf_op jit(solution)/shard_map/ppermute | solution.py:19
  179.5 0.1 collective-permute-start.11
  179.6 4.6 %collective-permute-done.11 = f32[128,128]{0,1:T(8,128)S(1)} collective-permute-done((f32[128,128]{0,1:T(8,128)S(1)}, f32[128,128]{0,1:T(8,128)S(1)}, u32[]{:S(2)}, u32[]{:S(2)}) %collective-permute-start.11) | collective-permute-done | bytes 65568 | tf_op jit(solution)/shard_map/ppermute | solution.py:19
  184.2 0.6 collective-permute-start.12
  184.8 5.6 %collective-permute-done.12 = f32[128,128]{0,1:T(8,128)S(1)} collective-permute-done((f32[128,128]{0,1:T(8,128)S(1)}, f32[128,128]{0,1:T(8,128)S(1)}, u32[]{:S(2)}, u32[]{:S(2)}) %collective-permute-start.12) | collective-permute-done | bytes 65568 | tf_op jit(solution)/shard_map/ppermute | solution.py:19
  190.3 0.1 copy.22
  190.4 11.7 %cholesky.16 = f32[128,128]{1,0:T(8,128)S(1)} custom-call(f32[128,128]{1,0:T(8,128)S(1)} %fusion.2), custom_call_target="Cholesky" | custom-call | tf_op jit(solution)/shard_map/jit(cholesky)/cholesky | solution.py:43
  202.2 0.6 compare_reduce_fusion
  202.8 0.7 fusion.3
  203.5 0.7 copy.25
  204.2 9.8 %custom-call.6 = f32[1,128,128]{1,2,0:T(8,128)S(1)} custom-call(f32[1,128,128]{2,1,0:T(8,128)S(1)} %get-tuple-element.9), custom_call_target="InvertDiagBlocksLowerTriangular" | custom-call | tf_op jit(solution)/shard_map/triangular_solve | solution.py:25
  214.0 9.8 %fusion = f32[64,128,128]{2,1,0:T(8,128)} fusion(f32[64,128,128]{1,2,0:T(8,128)} %bitcast_add_fusion, f32[1,128,128]{1,2,0:T(8,128)S(1)} %custom-call.6), kind=kOutput, calls=%fused_computation.20 | convolution fusion | flops 1610612736 | bytes 8454144 | tf_op jit(solution)/shard_map/triangular_solve | solution.py:25
  (30 shorter events, 0.6 us)
Async XLA Ops:
  2.1 15.2 %copy-start.4 = (s32[64,8]{0,1:T(8,128)S(1)}, s32[64,8]{0,1:T(8,128)}, u32[]{:S(2)}) copy-start(s32[64,8]{0,1:T(8,128)} %param.7) | copy-start | bytes 6148
  6.9 16.2 %copy-start.2 = (bf16[64,128,128]{2,1,0:T(8,128)(2,1)}, bf16[64,128,128]{2,1,0:T(8,128)(2,1)S(1)}, u32[]{:S(2)}) copy-start(bf16[64,128,128]{2,1,0:T(8,128)(2,1)S(1)} %get-tuple-element.6) | copy-start | bytes 6291460
  7.5 15.6 %collective-permute-start = (bf16[16,128,128]{2,1,0:T(8,128)(2,1)S(1)}, bf16[16,128,128]{2,1,0:T(8,128)(2,1)S(1)}, u32[]{:S(2)}, u32[]{:S(2)}) collective-permute-start(bf16[16,128,128]{2,1,0:T(8,128)(2,1)S(1)} %gather_fusion), channel_id=1, source_target_pairs={{0,1},{1,2},{2,3},{3,4},{4,5},{5,6},{6,7},{7,8},{8,9},{9,10},{10,1... | collective-permute-start | bytes 1572872 | tf_op jit(solution)/shard_map/ppermute | solution.py:11
  9.1 15.2 %collective-permute-start.1 = (bf16[16,128,128]{2,1,0:T(8,128)(2,1)}, bf16[16,128,128]{2,1,0:T(8,128)(2,1)}, u32[]{:S(2)}, u32[]{:S(2)}) collective-permute-start(bf16[16,128,128]{2,1,0:T(8,128)(2,1)} %gather_fusion.1), channel_id=1, source_target_pairs={{0,127},{1,0},{2,1},{3,2},{4,3},{5,4},{6,5},{7,6},{8,7},{9,8},{10,... | collective-permute-start | bytes 1572872 | tf_op jit(solution)/shard_map/ppermute | solution.py:11
  23.1 0.8 copy-start.3
  56.2 15.6 %copy-start = (bf16[64,128,128]{1,2,0:T(8,128)(2,1)}, bf16[64,128,128]{1,2,0:T(8,128)(2,1)S(1)}, u32[]{:S(2)}) copy-start(bf16[64,128,128]{1,2,0:T(8,128)(2,1)S(1)} %get-tuple-element.12) | copy-start | bytes 6291460
  57.5 14.3 %collective-permute-start.2 = (bf16[16,128,128]{1,2,0:T(8,128)(2,1)S(1)}, bf16[16,128,128]{1,2,0:T(8,128)(2,1)S(1)}, u32[]{:S(2)}, u32[]{:S(2)}) collective-permute-start(bf16[16,128,128]{1,2,0:T(8,128)(2,1)S(1)} %gather_fusion.3), channel_id=1, source_target_pairs={{0,1},{1,2},{2,3},{3,4},{4,5},{5,6},{6,7},{7,8},{8,9},{9,10},{10,1... | collective-permute-start | bytes 1572872 | tf_op jit(solution)/shard_map/ppermute | solution.py:11
  57.6 14.3 %collective-permute-start.3 = (bf16[16,128,128]{1,2,0:T(8,128)(2,1)S(1)}, bf16[16,128,128]{1,2,0:T(8,128)(2,1)S(1)}, u32[]{:S(2)}, u32[]{:S(2)}) collective-permute-start(bf16[16,128,128]{1,2,0:T(8,128)(2,1)S(1)} %gather_fusion.4), channel_id=1, source_target_pairs={{0,127},{1,0},{2,1},{3,2},{4,3},{5,4},{6,5},{7,6},{8,7},{9,8},{10,... | collective-permute-start | bytes 1572872 | tf_op jit(solution)/shard_map/ppermute | solution.py:11
  103.2 15.6 %copy-start.1 = (bf16[64,128,128]{1,2,0:T(8,128)(2,1)}, bf16[64,128,128]{1,2,0:T(8,128)(2,1)S(1)}, u32[]{:S(2)}) copy-start(bf16[64,128,128]{1,2,0:T(8,128)(2,1)S(1)} %get-tuple-element.14) | copy-start | bytes 6291460
  104.5 14.3 %collective-permute-start.4 = (bf16[16,128,128]{1,2,0:T(8,128)(2,1)S(1)}, bf16[16,128,128]{1,2,0:T(8,128)(2,1)S(1)}, u32[]{:S(2)}, u32[]{:S(2)}) collective-permute-start(bf16[16,128,128]{1,2,0:T(8,128)(2,1)S(1)} %gather_fusion.6), channel_id=1, source_target_pairs={{0,1},{1,2},{2,3},{3,4},{4,5},{5,6},{6,7},{7,8},{8,9},{9,10},{10,1... | collective-permute-start | bytes 1572872 | tf_op jit(solution)/shard_map/ppermute | solution.py:11
  104.6 14.3 %collective-permute-start.5 = (bf16[16,128,128]{1,2,0:T(8,128)(2,1)S(1)}, bf16[16,128,128]{1,2,0:T(8,128)(2,1)S(1)}, u32[]{:S(2)}, u32[]{:S(2)}) collective-permute-start(bf16[16,128,128]{1,2,0:T(8,128)(2,1)S(1)} %gather_fusion.7), channel_id=1, source_target_pairs={{0,127},{1,0},{2,1},{3,2},{4,3},{5,4},{6,5},{7,6},{8,7},{9,8},{10,... | collective-permute-start | bytes 1572872 | tf_op jit(solution)/shard_map/ppermute | solution.py:11
  157.8 1.3 collective-permute-start.6
  159.1 4.3 %collective-permute-start.7 = (f32[128,128]{0,1:T(8,128)S(1)}, f32[128,128]{0,1:T(8,128)S(1)}, u32[]{:S(2)}, u32[]{:S(2)}) collective-permute-start(f32[128,128]{0,1:T(8,128)S(1)} %add.76), channel_id=1, source_target_pairs={{0,2},{1,3},{2,0},{3,1},{4,6},{5,7},{6,4},{7,5},{8,10},{9,11},{10,... | collective-permute-start | bytes 196616 | tf_op jit(solution)/shard_map/ppermute | solution.py:19
  163.5 5.8 %collective-permute-start.8 = (f32[128,128]{0,1:T(8,128)S(1)}, f32[128,128]{0,1:T(8,128)S(1)}, u32[]{:S(2)}, u32[]{:S(2)}) collective-permute-start(f32[128,128]{0,1:T(8,128)S(1)} %add.77), channel_id=1, source_target_pairs={{0,4},{1,5},{2,6},{3,7},{4,0},{5,1},{6,2},{7,3},{8,12},{9,13},{10,... | collective-permute-start | bytes 196616 | tf_op jit(solution)/shard_map/ppermute | solution.py:19
  169.3 4.3 %collective-permute-start.9 = (f32[128,128]{0,1:T(8,128)S(1)}, f32[128,128]{0,1:T(8,128)S(1)}, u32[]{:S(2)}, u32[]{:S(2)}) collective-permute-start(f32[128,128]{0,1:T(8,128)S(1)} %add.78), channel_id=1, source_target_pairs={{0,8},{1,9},{2,10},{3,11},{4,12},{5,13},{6,14},{7,15},{8,0},{9,1},... | collective-permute-start | bytes 196616 | tf_op jit(solution)/shard_map/ppermute | solution.py:19
  173.7 5.8 %collective-permute-start.10 = (f32[128,128]{0,1:T(8,128)S(1)}, f32[128,128]{0,1:T(8,128)S(1)}, u32[]{:S(2)}, u32[]{:S(2)}) collective-permute-start(f32[128,128]{0,1:T(8,128)S(1)} %add.79), channel_id=1, source_target_pairs={{0,16},{1,17},{2,18},{3,19},{4,20},{5,21},{6,22},{7,23},{8,24},{9,... | collective-permute-start | bytes 196616 | tf_op jit(solution)/shard_map/ppermute | solution.py:19
  179.5 4.7 %collective-permute-start.11 = (f32[128,128]{0,1:T(8,128)S(1)}, f32[128,128]{0,1:T(8,128)S(1)}, u32[]{:S(2)}, u32[]{:S(2)}) collective-permute-start(f32[128,128]{0,1:T(8,128)S(1)} %add.80), channel_id=1, source_target_pairs={{0,32},{1,33},{2,34},{3,35},{4,36},{5,37},{6,38},{7,39},{8,40},{9,... | collective-permute-start | bytes 196616 | tf_op jit(solution)/shard_map/ppermute | solution.py:19
  184.2 6.1 %collective-permute-start.12 = (f32[128,128]{0,1:T(8,128)S(1)}, f32[128,128]{0,1:T(8,128)S(1)}, u32[]{:S(2)}, u32[]{:S(2)}) collective-permute-start(f32[128,128]{0,1:T(8,128)S(1)} %add.81), channel_id=1, source_target_pairs={{0,64},{1,65},{2,66},{3,67},{4,68},{5,69},{6,70},{7,71},{8,72},{9,... | collective-permute-start | bytes 196616 | tf_op jit(solution)/shard_map/ppermute | solution.py:19

commit v2 on v1

--- a/solution.py
+++ b/solution.py
@@ -1,9 +1,14 @@
+import functools
+
 import jax
 import jax.numpy as jnp
 from jax import lax
+from jax.experimental import pallas as pl
+from jax.experimental.pallas import tpu as pltpu
 from jax.sharding import PartitionSpec as P
 
 SUBSTEPS = 3
+ROWS_PER_STEP = 4
 
 
 def passed_along(shard, axis, by):
@@ -21,29 +26,89 @@
     return value
 
 
-def apply_inverse(matrix, lower):
-    return lax.linalg.triangular_solve(lower, matrix, left_side=False, lower=True, transpose_a=True)
+def substep_kernel(cols_ref, count_ref, own_hbm, low_hbm, high_hbm, blocks_ref, state_ref,
+                   new_state_ref, new_rounded_ref, extended, sems, *, nnz, per_step):
+    step = pl.program_id(0)
+    slots = own_hbm.shape[0]
+    halo = low_hbm.shape[0]
+
+    @pl.when(step == 0)
+    def _():
+        copies = [
+            pltpu.make_async_copy(own_hbm, extended.at[pl.ds(0, slots)], sems.at[0]),
+            pltpu.make_async_copy(low_hbm, extended.at[pl.ds(slots, halo)], sems.at[1]),
+            pltpu.make_async_copy(high_hbm, extended.at[pl.ds(slots + halo, halo)], sems.at[2]),
+        ]
+        for copy in copies:
+            copy.start()
+        for copy in copies:
+            copy.wait()
+
+    count = count_ref[0]
+    for r in range(per_step):
+        row = step * per_step + r
+        acc = jnp.zeros(state_ref.shape[1:], jnp.float32)
+        for k in range(nnz):
+            col = cols_ref[row * nnz + k]
+            acc = acc + jnp.dot(blocks_ref[r, k], extended[col], preferred_element_type=jnp.float32)
+        new = state_ref[r] + jnp.where(row < count, acc, 0.0)
+        new_state_ref[r] = new
+        new_rounded_ref[r] = new.astype(jnp.bfloat16)
+
+
+def substep(cols, count, rounded, from_lower, from_upper, blocks, state):
+    slots, width, vectors = state.shape
+    nnz = blocks.shape[1]
+    halo = from_lower.shape[0]
+    per_step = ROWS_PER_STEP
+    kernel = functools.partial(substep_kernel, nnz=nnz, per_step=per_step)
+    grid_spec = pltpu.PrefetchScalarGridSpec(
+        num_scalar_prefetch=2,
+        grid=(slots // per_step,),
+        in_specs=[
+            pl.BlockSpec(memory_space=pl.ANY),
+            pl.BlockSpec(memory_space=pl.ANY),
+            pl.BlockSpec(memory_space=pl.ANY),
+            pl.BlockSpec((per_step, nnz, width, width), lambda i, c, n: (i, 0, 0, 0)),
+            pl.BlockSpec((per_step, width, vectors), lambda i, c, n: (i, 0, 0)),
+        ],
+        out_specs=[
+            pl.BlockSpec((per_step, width, vectors), lambda i, c, n: (i, 0, 0)),
+            pl.BlockSpec((per_step, width, vectors), lambda i, c, n: (i, 0, 0)),
+        ],
+        scratch_shapes=[
+            pltpu.VMEM((slots + 2 * halo, width, vectors), jnp.bfloat16),
+            pltpu.SemaphoreType.DMA((3,)),
+        ],
+    )
+    return pl.pallas_call(
+        kernel,
+        grid_spec=grid_spec,
+        out_shape=[
+            jax.ShapeDtypeStruct(state.shape, jnp.float32),
+            jax.ShapeDtypeStruct(state.shape, jnp.bfloat16),
+        ],
+        compiler_params=pltpu.CompilerParams(dimension_semantics=("arbitrary",)),
+    )(cols, count, rounded, from_lower, from_upper, blocks, state)
 
 
 def local(tangent, blocks, columns, counts, send_lists):
     slots, width, vectors = tangent.shape
     live = (jnp.arange(slots, dtype=jnp.int32) < counts[0]).astype(jnp.float32)[:, None, None]
     state = tangent * live
+    rounded = state.astype(jnp.bfloat16)
+    cols = columns.reshape(-1)
     for step in range(SUBSTEPS):
-        rounded = state.astype(jnp.bfloat16)
         to_lower = rounded[send_lists[0, 0]]
         to_upper = rounded[send_lists[0, 1]]
         from_lower = passed_along(to_upper, "grains", 1)
         from_upper = passed_along(to_lower, "grains", -1)
-        extended = jnp.concatenate([rounded, from_lower, from_upper], axis=0)
-        gathered = extended[columns]
-        update = jnp.einsum("bkij,bkjv->biv", blocks, gathered, preferred_element_type=jnp.float32)
-        state = state + update * live
+        state, rounded = substep(cols, counts, rounded, from_lower, from_upper, blocks, state)
     flat = state.reshape(slots * width, vectors)
     first_low = jnp.linalg.cholesky(
         tree_sum(jnp.einsum("rk,rv->kv", flat, flat, precision=lax.Precision.HIGHEST), "grains")
     )
-    basis = apply_inverse(flat, first_low)
+    basis = lax.linalg.triangular_solve(first_low, flat, left_side=False, lower=True, transpose_a=True)
     r_factor = first_low.T
     return (basis.reshape(slots, width, vectors), r_factor)
 

time: 224 us -> 198 us (0.88)
  Pallas kernels: 0 us -> 58.4 us
  matrix products: 64.4 us -> 16.7 us
  local copies, waits for them, and re-layouts: 53.9 us -> 16.4 us
  waiting for transfers between devices: 45.1 us -> 51 us
  other arithmetic: 34.1 us -> 28.5 us
    pallas_call x0 -> x3, Pallas kernels: none -> 58.4 us  [substep(): pl.pallas_call(kernel, grid_spec=grid_spec, out_shape=[jax.ShapeDtypeStru...]
    dot_general x3 -> x0, matrix products: 47.6 us -> none  [local(): jnp.einsum('bkij,bkjv->biv', blocks, gathered, preferred_element_type=jnp...]
    gather x3 -> x0, local copies, waits for them, and re-layouts: 41.8 us -> none  [local(): gathered = extended[columns]]
    ppermute x6, waiting for transfers between devices: 13.8 us -> 19.8 us  [passed_along(): lax.ppermute(shard, axis, [(i, (i + by) % length) for i in range(length)])]
    mul x1 -> x0, local copies, waits for them, and re-layouts: 5.63 us -> none  [local(): state = tangent * live]
    concatenate x3 -> x0, other arithmetic: 5.61 us -> none  [local(): extended = jnp.concatenate([rounded, from_lower, from_upper], axis=0)]
    gather x3, local copies, waits for them, and re-layouts: 1.94 us -> 6.02 us  [local(): to_upper = rounded[send_lists[0, 1]]]
    another operation x1, matrix products: 9.79 us -> 6.52 us  [local(): lax.linalg.triangular_solve(first_low, flat, left_side=False, lower=True,...]
  transfers between devices with their start and end apart: 13 -> 13, of which waited for: 12 -> 11; matrix products, arithmetic and copies ran while one was open for 3% -> 1% of each run, Pallas kernels for 0% -> 0%
where the time goes in v2:
time: 198 us; the launch traced here: 196 us
  Pallas kernels  58.4 us (29%)
  waiting for transfers between devices  51 us (26%)
  other arithmetic  28.5 us (14%)
  starting transfers between devices  23.8 us (12%)
  matrix products  16.7 us (8%)
  local copies, waits for them, and re-layouts  16.4 us (8%)
    pallas_call x3, Pallas kernels, substep(): pl.pallas_call(kernel, grid_spec=grid_spec, out_shape=[jax.ShapeDtypeStru...  58.4 us
    ppermute x7, waiting for transfers between devices, tree_sum(): value = value + lax.ppermute(value, axis, partner)  31.2 us
    ppermute x6, starting transfers between devices, passed_along(): lax.ppermute(shard, axis, [(i, (i + by) % length) for i in range(length)])  22.9 us
    ppermute x6, waiting for transfers between devices, passed_along(): lax.ppermute(shard, axis, [(i, (i + by) % length) for i in range(length)])  19.8 us
    another operation x3, other arithmetic, local(): jnp.linalg.cholesky(tree_sum(jnp.einsum('rk,rv->kv', flat, flat, precisio...  12.4 us
    dot_general x1, matrix products, local(): jnp.einsum('rk,rv->kv', flat, flat, precision=lax.Precision.HIGHEST)  10.2 us
    another operation x1, other arithmetic, local(): lax.linalg.triangular_solve(first_low, flat, left_side=False, lower=True,...  9.81 us
    another operation x1, matrix products, local(): lax.linalg.triangular_solve(first_low, flat, left_side=False, lower=True,...  6.52 us
  transfers between devices with their start and end apart: 13, of which 11 were waited for; matrix products, arithmetic and copies ran while one was open for 1% of the time, Pallas kernels for 0%

profile of v2, /device:TPU:0, one launch (start us, length us, event | category | flops | bytes accessed | tf_op | source)
XLA Modules:
  0.0 196.4 jit_solution(15223506588194862737)
XLA Ops:
  1.3 0.8 fusion.5
  2.1 4.8 %fusion.6 = (bf16[64,128,128]{2,1,0:T(8,128)(2,1)S(1)}, f32[64,128,128]{2,1,0:T(8,128)}) fusion(f32[64,128,128]{2,1,0:T(8,128)} %param.5, f32[64]{0:T(128)S(1)} %compare_convert_fusion), kind=kLoop, calls=%fused_computation.26 | loop fusion | flops 2097152 | bytes 10486016 | tf_op jit(solution)/shard_map/convert_element_type | solution.py:99
  6.9 1.5 gather_fusion
  8.4 1.4 gather_fusion.1
  9.8 8.2 %collective-permute-start.1 = (bf16[16,128,128]{2,1,0:T(8,128)(2,1)}, bf16[16,128,128]{2,1,0:T(8,128)(2,1)S(1)}, u32[]{:S(2)}, u32[]{:S(2)}) collective-permute-start(bf16[16,128,128]{2,1,0:T(8,128)(2,1)} %gather_fusion.1), channel_id=1, source_target_pairs={{0,127},{1,0},{2,1},{3,2},{4,3},{5,4},{6,5},{7,6},{8,7},{9,8},{10,... | collective-permute-start | bytes 1572872 | tf_op jit(solution)/shard_map/ppermute | solution.py:16
  18.1 0.1 copy.13
  18.2 0.7 reshape.81.cols_ref
  18.8 4.9 %collective-permute-done.low_hbm = bf16[16,128,128]{2,1,0:T(8,128)(2,1)S(1)} collective-permute-done((bf16[16,128,128]{2,1,0:T(8,128)(2,1)}, bf16[16,128,128]{2,1,0:T(8,128)(2,1)S(1)}, u32[]{:S(2)}, u32[]{:S(2)}) %collective-permute-start) | collective-permute-done | bytes 524320 | tf_op jit(solution)/shard_map/ppermute | solution.py:16
  23.7 1.4 collective-permute-done.1.high_hbm
  25.1 0.8 copy-done.3
  25.9 19.5 %shard_map.68 = (f32[64,128,128]{2,1,0:T(8,128)}, bf16[64,128,128]{2,1,0:T(8,128)(2,1)}) custom-call(s32[512]{0:T(512)} %reshape.81.cols_ref, s32[1]{0:T(128)} %copy.26.count_ref, bf16[64,128,128]{2,1,0:T(8,128)(2,1)} %copy-done, bf16[16,128,128]{2,1,0:T(8,128)(2,1)} %copy-done.1, bf16[16,128,128]{2,1,0:T(8,128)(2,1)} %copy-done.3, ...), custom_call_target="tpu_custom_call" | custom-call | tf_op jit(solution)/shard_map/pallas_call | solution.py:84
  45.4 2.2 %gather_fusion.3 = bf16[16,128,128]{2,1,0:T(8,128)(2,1)S(1)} fusion(bf16[64,128,128]{2,1,0:T(8,128)(2,1)} %get-tuple-element.7.own_hbm, s32[1024]{0:T(1024)S(1)} %pad_clamp_fusion), kind=kCustom, calls=%fused_computation.3 | custom fusion | bytes 1048640 | tf_op jit(solution)/shard_map/gather | solution.py:102
  47.7 2.2 %gather_fusion.2 = bf16[16,128,128]{2,1,0:T(8,128)(2,1)S(1)} fusion(bf16[64,128,128]{2,1,0:T(8,128)(2,1)} %get-tuple-element.7.own_hbm, s32[1024]{0:T(1024)S(1)} %pad_clamp_fusion.1), kind=kCustom, calls=%fused_computation.2 | custom fusion | bytes 1048640 | tf_op jit(solution)/shard_map/gather | solution.py:103
  49.9 0.1 collective-permute-start.2
  50.0 7.3 %collective-permute-start.3 = (bf16[16,128,128]{2,1,0:T(8,128)(2,1)S(1)}, bf16[16,128,128]{2,1,0:T(8,128)(2,1)S(1)}, u32[]{:S(2)}, u32[]{:S(2)}) collective-permute-start(bf16[16,128,128]{2,1,0:T(8,128)(2,1)S(1)} %gather_fusion.3), channel_id=1, source_target_pairs={{0,127},{1,0},{2,1},{3,2},{4,3},{5,4},{6,5},{7,6},{8,7},{9,8},{10,... | collective-permute-start | bytes 1572872 | tf_op jit(solution)/shard_map/ppermute | solution.py:16
  57.3 6.8 %collective-permute-done.2.low_hbm = bf16[16,128,128]{2,1,0:T(8,128)(2,1)S(1)} collective-permute-done((bf16[16,128,128]{2,1,0:T(8,128)(2,1)S(1)}, bf16[16,128,128]{2,1,0:T(8,128)(2,1)S(1)}, u32[]{:S(2)}, u32[]{:S(2)}) %collective-permute-start.2) | collective-permute-done | bytes 524320 | tf_op jit(solution)/shard_map/ppermute | solution.py:16
  64.1 0.8 copy-done.4
  64.9 0.2 copy-done.6
  65.1 19.4 %shard_map.69 = (f32[64,128,128]{2,1,0:T(8,128)}, bf16[64,128,128]{2,1,0:T(8,128)(2,1)}) custom-call(s32[512]{0:T(512)} %reshape.81.cols_ref, s32[1]{0:T(128)} %copy.26.count_ref, bf16[64,128,128]{2,1,0:T(8,128)(2,1)} %get-tuple-element.7.own_hbm, bf16[16,128,128]{2,1,0:T(8,128)(2,1)} %copy-done.4, bf16[16,128,128]{2,1,0:T(8,128)(2,1)} %copy-done.6, ...), custom_call_target="tpu_custom_call" | custom-call | tf_op jit(solution)/shard_map/pallas_call | solution.py:84
  84.5 2.2 %gather_fusion.5 = bf16[16,128,128]{2,1,0:T(8,128)(2,1)S(1)} fusion(bf16[64,128,128]{2,1,0:T(8,128)(2,1)} %get-tuple-element.9.own_hbm, s32[1024]{0:T(1024)S(1)} %pad_clamp_fusion), kind=kCustom, calls=%fused_computation.5 | custom fusion | bytes 1048640 | tf_op jit(solution)/shard_map/gather | solution.py:102
  86.8 2.2 %gather_fusion.4 = bf16[16,128,128]{2,1,0:T(8,128)(2,1)S(1)} fusion(bf16[64,128,128]{2,1,0:T(8,128)(2,1)} %get-tuple-element.9.own_hbm, s32[1024]{0:T(1024)S(1)} %pad_clamp_fusion.1), kind=kCustom, calls=%fused_computation.4 | custom fusion | bytes 1048640 | tf_op jit(solution)/shard_map/gather | solution.py:103
  89.1 7.2 %collective-permute-start.5 = (bf16[16,128,128]{2,1,0:T(8,128)(2,1)S(1)}, bf16[16,128,128]{2,1,0:T(8,128)(2,1)S(1)}, u32[]{:S(2)}, u32[]{:S(2)}) collective-permute-start(bf16[16,128,128]{2,1,0:T(8,128)(2,1)S(1)} %gather_fusion.5), channel_id=1, source_target_pairs={{0,127},{1,0},{2,1},{3,2},{4,3},{5,4},{6,5},{7,6},{8,7},{9,8},{10,... | collective-permute-start | bytes 1572872 | tf_op jit(solution)/shard_map/ppermute | solution.py:16
  96.4 6.8 %collective-permute-done.4.low_hbm = bf16[16,128,128]{2,1,0:T(8,128)(2,1)S(1)} collective-permute-done((bf16[16,128,128]{2,1,0:T(8,128)(2,1)S(1)}, bf16[16,128,128]{2,1,0:T(8,128)(2,1)S(1)}, u32[]{:S(2)}, u32[]{:S(2)}) %collective-permute-start.4) | collective-permute-done | bytes 524320 | tf_op jit(solution)/shard_map/ppermute | solution.py:16
  103.1 0.8 copy-done.2
  104.0 0.2 copy-done.5
  104.2 19.5 %shard_map.70 = (f32[64,128,128]{2,1,0:T(8,128)}, bf16[64,128,128]{2,1,0:T(8,128)(2,1)}) custom-call(s32[512]{0:T(512)} %reshape.81.cols_ref, s32[1]{0:T(128)} %copy.26.count_ref, bf16[64,128,128]{2,1,0:T(8,128)(2,1)} %get-tuple-element.9.own_hbm, bf16[16,128,128]{2,1,0:T(8,128)(2,1)} %copy-done.2, bf16[16,128,128]{2,1,0:T(8,128)(2,1)} %copy-done.5, ...), custom_call_target="tpu_custom_call" | custom-call | tf_op jit(solution)/shard_map/pallas_call | solution.py:84
  123.7 10.2 %convolution_bitcast_fusion = f32[128,128]{0,1:T(8,128)S(1)} fusion(f32[64,128,128]{2,1,0:T(8,128)} %get-tuple-element.11), kind=kOutput, calls=%fused_computation.7 | convolution fusion | flops 1610612736 | bytes 4259840 | tf_op jit(solution)/shard_map/rk,rv->kv/dot_general | solution.py:109
  133.9 0.1 collective-permute-start.6
  134.0 1.2 collective-permute-done.6
  135.2 0.1 collective-permute-start.7
  135.3 4.3 %collective-permute-done.7 = f32[128,128]{0,1:T(8,128)S(1)} collective-permute-done((f32[128,128]{0,1:T(8,128)S(1)}, f32[128,128]{0,1:T(8,128)S(1)}, u32[]{:S(2)}, u32[]{:S(2)}) %collective-permute-start.7) | collective-permute-done | bytes 65568 | tf_op jit(solution)/shard_map/ppermute | solution.py:24
  139.6 0.1 collective-permute-start.8
  139.7 5.8 %collective-permute-done.8 = f32[128,128]{0,1:T(8,128)S(1)} collective-permute-done((f32[128,128]{0,1:T(8,128)S(1)}, f32[128,128]{0,1:T(8,128)S(1)}, u32[]{:S(2)}, u32[]{:S(2)}) %collective-permute-start.8) | collective-permute-done | bytes 65568 | tf_op jit(solution)/shard_map/ppermute | solution.py:24
  145.5 0.1 collective-permute-start.9
  145.6 4.3 %collective-permute-done.9 = f32[128,128]{0,1:T(8,128)S(1)} collective-permute-done((f32[128,128]{0,1:T(8,128)S(1)}, f32[128,128]{0,1:T(8,128)S(1)}, u32[]{:S(2)}, u32[]{:S(2)}) %collective-permute-start.9) | collective-permute-done | bytes 65568 | tf_op jit(solution)/shard_map/ppermute | solution.py:24
  149.8 0.1 collective-permute-start.10
  149.9 5.8 %collective-permute-done.10 = f32[128,128]{0,1:T(8,128)S(1)} collective-permute-done((f32[128,128]{0,1:T(8,128)S(1)}, f32[128,128]{0,1:T(8,128)S(1)}, u32[]{:S(2)}, u32[]{:S(2)}) %collective-permute-start.10) | collective-permute-done | bytes 65568 | tf_op jit(solution)/shard_map/ppermute | solution.py:24
  155.7 0.1 collective-permute-start.11
  155.8 4.3 %collective-permute-done.11 = f32[128,128]{0,1:T(8,128)S(1)} collective-permute-done((f32[128,128]{0,1:T(8,128)S(1)}, f32[128,128]{0,1:T(8,128)S(1)}, u32[]{:S(2)}, u32[]{:S(2)}) %collective-permute-start.11) | collective-permute-done | bytes 65568 | tf_op jit(solution)/shard_map/ppermute | solution.py:24
  160.0 0.4 collective-permute-start.12
  160.4 5.7 %collective-permute-done.12 = f32[128,128]{0,1:T(8,128)S(1)} collective-permute-done((f32[128,128]{0,1:T(8,128)S(1)}, f32[128,128]{0,1:T(8,128)S(1)}, u32[]{:S(2)}, u32[]{:S(2)}) %collective-permute-start.12) | collective-permute-done | bytes 65568 | tf_op jit(solution)/shard_map/ppermute | solution.py:24
  166.1 0.1 copy.17
  166.2 11.7 %cholesky.16 = f32[128,128]{1,0:T(8,128)S(1)} custom-call(f32[128,128]{1,0:T(8,128)S(1)} %fusion.2), custom_call_target="Cholesky" | custom-call | tf_op jit(solution)/shard_map/jit(cholesky)/cholesky | solution.py:108
  178.0 0.6 compare_reduce_fusion
  178.6 0.7 fusion.3
  179.3 0.7 copy.19
  180.0 9.8 %custom-call.6 = f32[1,128,128]{1,2,0:T(8,128)S(1)} custom-call(f32[1,128,128]{2,1,0:T(8,128)S(1)} %get-tuple-element.19), custom_call_target="InvertDiagBlocksLowerTriangular" | custom-call | tf_op jit(solution)/shard_map/triangular_solve | solution.py:111
  189.8 6.5 %fusion = f32[64,128,128]{2,1,0:T(8,128)} fusion(f32[64,128,128]{2,1,0:T(8,128)} %get-tuple-element.11, f32[1,128,128]{1,2,0:T(8,128)S(1)} %custom-call.6), kind=kOutput, calls=%fused_computation.8 | convolution fusion | flops 1610612736 | bytes 8454144 | tf_op jit(solution)/shard_map/triangular_solve | solution.py:111
  (27 shorter events, 0.2 us)
Async XLA Ops:
  2.1 16.0 %copy-start.7 = (s32[64,8]{0,1:T(8,128)S(1)}, s32[64,8]{0,1:T(8,128)}, u32[]{:S(2)}) copy-start(s32[64,8]{0,1:T(8,128)} %param.7) | copy-start | bytes 6148
  6.9 18.2 %copy-start = (bf16[64,128,128]{2,1,0:T(8,128)(2,1)}, bf16[64,128,128]{2,1,0:T(8,128)(2,1)S(1)}, u32[]{:S(2)}) copy-start(bf16[64,128,128]{2,1,0:T(8,128)(2,1)S(1)} %get-tuple-element.16.own_hbm) | copy-start | bytes 6291460
  8.4 15.3 %collective-permute-start = (bf16[16,128,128]{2,1,0:T(8,128)(2,1)}, bf16[16,128,128]{2,1,0:T(8,128)(2,1)S(1)}, u32[]{:S(2)}, u32[]{:S(2)}) collective-permute-start(bf16[16,128,128]{2,1,0:T(8,128)(2,1)} %gather_fusion), channel_id=1, source_target_pairs={{0,1},{1,2},{2,3},{3,4},{4,5},{5,6},{6,7},{7,8},{8,9},{9,10},{10,1... | collective-permute-start | bytes 1572872 | tf_op jit(solution)/shard_map/ppermute | solution.py:16
  9.8 15.2 %collective-permute-start.1 = (bf16[16,128,128]{2,1,0:T(8,128)(2,1)}, bf16[16,128,128]{2,1,0:T(8,128)(2,1)S(1)}, u32[]{:S(2)}, u32[]{:S(2)}) collective-permute-start(bf16[16,128,128]{2,1,0:T(8,128)(2,1)} %gather_fusion.1), channel_id=1, source_target_pairs={{0,127},{1,0},{2,1},{3,2},{4,3},{5,4},{6,5},{7,6},{8,7},{9,8},{10,... | collective-permute-start | bytes 1572872 | tf_op jit(solution)/shard_map/ppermute | solution.py:16
  23.7 1.4 copy-start.1
  25.1 0.8 copy-start.3
  49.9 14.2 %collective-permute-start.2 = (bf16[16,128,128]{2,1,0:T(8,128)(2,1)S(1)}, bf16[16,128,128]{2,1,0:T(8,128)(2,1)S(1)}, u32[]{:S(2)}, u32[]{:S(2)}) collective-permute-start(bf16[16,128,128]{2,1,0:T(8,128)(2,1)S(1)} %gather_fusion.2), channel_id=1, source_target_pairs={{0,1},{1,2},{2,3},{3,4},{4,5},{5,6},{6,7},{7,8},{8,9},{9,10},{10,1... | collective-permute-start | bytes 1572872 | tf_op jit(solution)/shard_map/ppermute | solution.py:16
  50.0 14.1 %collective-permute-start.3 = (bf16[16,128,128]{2,1,0:T(8,128)(2,1)S(1)}, bf16[16,128,128]{2,1,0:T(8,128)(2,1)S(1)}, u32[]{:S(2)}, u32[]{:S(2)}) collective-permute-start(bf16[16,128,128]{2,1,0:T(8,128)(2,1)S(1)} %gather_fusion.3), channel_id=1, source_target_pairs={{0,127},{1,0},{2,1},{3,2},{4,3},{5,4},{6,5},{7,6},{8,7},{9,8},{10,... | collective-permute-start | bytes 1572872 | tf_op jit(solution)/shard_map/ppermute | solution.py:16
  64.1 0.9 copy-start.4
  64.1 1.1 copy-start.6
  89.0 14.1 %collective-permute-start.4 = (bf16[16,128,128]{2,1,0:T(8,128)(2,1)S(1)}, bf16[16,128,128]{2,1,0:T(8,128)(2,1)S(1)}, u32[]{:S(2)}, u32[]{:S(2)}) collective-permute-start(bf16[16,128,128]{2,1,0:T(8,128)(2,1)S(1)} %gather_fusion.4), channel_id=1, source_target_pairs={{0,1},{1,2},{2,3},{3,4},{4,5},{5,6},{6,7},{7,8},{8,9},{9,10},{10,1... | collective-permute-start | bytes 1572872 | tf_op jit(solution)/shard_map/ppermute | solution.py:16
  89.1 14.0 %collective-permute-start.5 = (bf16[16,128,128]{2,1,0:T(8,128)(2,1)S(1)}, bf16[16,128,128]{2,1,0:T(8,128)(2,1)S(1)}, u32[]{:S(2)}, u32[]{:S(2)}) collective-permute-start(bf16[16,128,128]{2,1,0:T(8,128)(2,1)S(1)} %gather_fusion.5), channel_id=1, source_target_pairs={{0,127},{1,0},{2,1},{3,2},{4,3},{5,4},{6,5},{7,6},{8,7},{9,8},{10,... | collective-permute-start | bytes 1572872 | tf_op jit(solution)/shard_map/ppermute | solution.py:16
  103.1 0.9 copy-start.2
  103.1 1.1 copy-start.5
  133.9 1.3 collective-permute-start.6
  135.2 4.3 %collective-permute-start.7 = (f32[128,128]{0,1:T(8,128)S(1)}, f32[128,128]{0,1:T(8,128)S(1)}, u32[]{:S(2)}, u32[]{:S(2)}) collective-permute-start(f32[128,128]{0,1:T(8,128)S(1)} %add.58), channel_id=1, source_target_pairs={{0,2},{1,3},{2,0},{3,1},{4,6},{5,7},{6,4},{7,5},{8,10},{9,11},{10,... | collective-permute-start | bytes 196616 | tf_op jit(solution)/shard_map/ppermute | solution.py:24
  139.6 5.8 %collective-permute-start.8 = (f32[128,128]{0,1:T(8,128)S(1)}, f32[128,128]{0,1:T(8,128)S(1)}, u32[]{:S(2)}, u32[]{:S(2)}) collective-permute-start(f32[128,128]{0,1:T(8,128)S(1)} %add.59), channel_id=1, source_target_pairs={{0,4},{1,5},{2,6},{3,7},{4,0},{5,1},{6,2},{7,3},{8,12},{9,13},{10,... | collective-permute-start | bytes 196616 | tf_op jit(solution)/shard_map/ppermute | solution.py:24
  145.5 4.3 %collective-permute-start.9 = (f32[128,128]{0,1:T(8,128)S(1)}, f32[128,128]{0,1:T(8,128)S(1)}, u32[]{:S(2)}, u32[]{:S(2)}) collective-permute-start(f32[128,128]{0,1:T(8,128)S(1)} %add.60), channel_id=1, source_target_pairs={{0,8},{1,9},{2,10},{3,11},{4,12},{5,13},{6,14},{7,15},{8,0},{9,1},... | collective-permute-start | bytes 196616 | tf_op jit(solution)/shard_map/ppermute | solution.py:24
  149.8 5.8 %collective-permute-start.10 = (f32[128,128]{0,1:T(8,128)S(1)}, f32[128,128]{0,1:T(8,128)S(1)}, u32[]{:S(2)}, u32[]{:S(2)}) collective-permute-start(f32[128,128]{0,1:T(8,128)S(1)} %add.61), channel_id=1, source_target_pairs={{0,16},{1,17},{2,18},{3,19},{4,20},{5,21},{6,22},{7,23},{8,24},{9,... | collective-permute-start | bytes 196616 | tf_op jit(solution)/shard_map/ppermute | solution.py:24
  155.7 4.3 %collective-permute-start.11 = (f32[128,128]{0,1:T(8,128)S(1)}, f32[128,128]{0,1:T(8,128)S(1)}, u32[]{:S(2)}, u32[]{:S(2)}) collective-permute-start(f32[128,128]{0,1:T(8,128)S(1)} %add.62), channel_id=1, source_target_pairs={{0,32},{1,33},{2,34},{3,35},{4,36},{5,37},{6,38},{7,39},{8,40},{9,... | collective-permute-start | bytes 196616 | tf_op jit(solution)/shard_map/ppermute | solution.py:24
  160.0 6.1 %collective-permute-start.12 = (f32[128,128]{0,1:T(8,128)S(1)}, f32[128,128]{0,1:T(8,128)S(1)}, u32[]{:S(2)}, u32[]{:S(2)}) collective-permute-start(f32[128,128]{0,1:T(8,128)S(1)} %add.63), channel_id=1, source_target_pairs={{0,64},{1,65},{2,66},{3,67},{4,68},{5,69},{6,70},{7,71},{8,72},{9,... | collective-permute-start | bytes 196616 | tf_op jit(solution)/shard_map/ppermute | solution.py:24

commit v3 on v2

--- a/solution.py
+++ b/solution.py
@@ -8,7 +8,7 @@
 from jax.sharding import PartitionSpec as P
 
 SUBSTEPS = 3
-ROWS_PER_STEP = 4
+ROWS_PER_STEP = 16
 
 
 def passed_along(shard, axis, by):
@@ -27,7 +27,7 @@
 
 
 def substep_kernel(cols_ref, count_ref, own_hbm, low_hbm, high_hbm, blocks_ref, state_ref,
-                   new_state_ref, new_rounded_ref, extended, sems, *, nnz, per_step):
+                   new_state_ref, out_ref, extended, sems, *, nnz, per_step, last):
     step = pl.program_id(0)
     slots = own_hbm.shape[0]
     halo = low_hbm.shape[0]
@@ -53,15 +53,24 @@
             acc = acc + jnp.dot(blocks_ref[r, k], extended[col], preferred_element_type=jnp.float32)
         new = state_ref[r] + jnp.where(row < count, acc, 0.0)
         new_state_ref[r] = new
-        new_rounded_ref[r] = new.astype(jnp.bfloat16)
+        if not last:
+            out_ref[r] = new.astype(jnp.bfloat16)
+            continue
+        part = lax.dot_general(new, new, (((0,), (0,)), ((), ())), precision=lax.Precision.HIGHEST,
+                               preferred_element_type=jnp.float32)
+        if r == 0:
+            @pl.when(step == 0)
+            def _():
+                out_ref[...] = jnp.zeros_like(out_ref)
+        out_ref[...] += part
 
 
-def substep(cols, count, rounded, from_lower, from_upper, blocks, state):
+def substep(cols, count, rounded, from_lower, from_upper, blocks, state, last):
     slots, width, vectors = state.shape
     nnz = blocks.shape[1]
     halo = from_lower.shape[0]
     per_step = ROWS_PER_STEP
-    kernel = functools.partial(substep_kernel, nnz=nnz, per_step=per_step)
+    kernel = functools.partial(substep_kernel, nnz=nnz, per_step=per_step, last=last)
     grid_spec = pltpu.PrefetchScalarGridSpec(
         num_scalar_prefetch=2,
         grid=(slots // per_step,),
@@ -74,7 +83,8 @@
         ],
         out_specs=[
             pl.BlockSpec((per_step, width, vectors), lambda i, c, n: (i, 0, 0)),
-            pl.BlockSpec((per_step, width, vectors), lambda i, c, n: (i, 0, 0)),
+            pl.BlockSpec((vectors, vectors), lambda i, c, n: (0, 0)) if last
+            else pl.BlockSpec((per_step, width, vectors), lambda i, c, n: (i, 0, 0)),
         ],
         scratch_shapes=[
             pltpu.VMEM((slots + 2 * halo, width, vectors), jnp.bfloat16),
@@ -86,7 +96,8 @@
         grid_spec=grid_spec,
         out_shape=[
             jax.ShapeDtypeStruct(state.shape, jnp.float32),
-            jax.ShapeDtypeStruct(state.shape, jnp.bfloat16),
+            jax.ShapeDtypeStruct((vectors, vectors), jnp.float32) if last
+            else jax.ShapeDtypeStruct(state.shape, jnp.bfloat16),
         ],
         compiler_params=pltpu.CompilerParams(dimension_semantics=("arbitrary",)),
     )(cols, count, rounded, from_lower, from_upper, blocks, state)
@@ -103,12 +114,15 @@
         to_upper = rounded[send_lists[0, 1]]
         from_lower = passed_along(to_upper, "grains", 1)
         from_upper = passed_along(to_lower, "grains", -1)
-        state, rounded = substep(cols, counts, rounded, from_lower, from_upper, blocks, state)
+        state, rounded = substep(cols, counts, rounded, from_lower, from_upper, blocks, state,
+                                 step == SUBSTEPS - 1)
+    gram = rounded
     flat = state.reshape(slots * width, vectors)
-    first_low = jnp.linalg.cholesky(
-        tree_sum(jnp.einsum("rk,rv->kv", flat, flat, precision=lax.Precision.HIGHEST), "grains")
+    first_low = jnp.linalg.cholesky(tree_sum(gram, "grains"))
+    inverse = lax.linalg.triangular_solve(
+        first_low, jnp.eye(vectors, dtype=jnp.float32), left_side=True, lower=True
     )
-    basis = lax.linalg.triangular_solve(first_low, flat, left_side=False, lower=True, transpose_a=True)
+    basis = jnp.dot(flat, inverse.T, precision=lax.Precision.HIGHEST)
     r_factor = first_low.T
     return (basis.reshape(slots, width, vectors), r_factor)
 

time: 198 us -> 177 us (0.89)
  Pallas kernels: 58.4 us -> 47.4 us
  matrix products: 16.7 us -> 6.8 us
    pallas_call x3, Pallas kernels: 58.4 us -> 47.4 us  [substep(): pl.pallas_call(kernel, grid_spec=grid_spec, out_shape=[jax.ShapeDtypeStru...]
    another operation x1, matrix products: 6.52 us -> 0.25 us  [local(): lax.linalg.triangular_solve(first_low, jnp.eye(vectors, dtype=jnp.float32...]
    dot_general x1, matrix products: 10.2 us -> 6.55 us  [local(): basis = jnp.dot(flat, inverse.T, precision=lax.Precision.HIGHEST)]
where the time goes in v3:
time: 177 us; the launch traced here: 176 us
  waiting for transfers between devices  51.2 us (29%)
  Pallas kernels  47.4 us (27%)
  other arithmetic  28.5 us (16%)
  starting transfers between devices  23.7 us (13%)
  local copies, waits for them, and re-layouts  17.2 us (10%)
  matrix products  6.8 us (4%)
    pallas_call x3, Pallas kernels, substep(): pl.pallas_call(kernel, grid_spec=grid_spec, out_shape=[jax.ShapeDtypeStru...  47.4 us
    ppermute x7, waiting for transfers between devices, tree_sum(): value = value + lax.ppermute(value, axis, partner)  31.2 us
    ppermute x6, starting transfers between devices, passed_along(): lax.ppermute(shard, axis, [(i, (i + by) % length) for i in range(length)])  22.8 us
    ppermute x6, waiting for transfers between devices, passed_along(): lax.ppermute(shard, axis, [(i, (i + by) % length) for i in range(length)])  19.9 us
    another operation x3, other arithmetic, local(): first_low = jnp.linalg.cholesky(tree_sum(gram, 'grains'))  12.4 us
    another operation x1, other arithmetic, local(): lax.linalg.triangular_solve(first_low, jnp.eye(vectors, dtype=jnp.float32...  9.81 us
    dot_general x1, matrix products, local(): basis = jnp.dot(flat, inverse.T, precision=lax.Precision.HIGHEST)  6.55 us
    gather x3, local copies, waits for them, and re-layouts, local(): to_upper = rounded[send_lists[0, 1]]  6.02 us
  transfers between devices with their start and end apart: 13, of which 11 were waited for; matrix products, arithmetic and copies ran while one was open for 1% of the time, Pallas kernels for 0%

profile of v3, /device:TPU:0, one launch (start us, length us, event | category | flops | bytes accessed | tf_op | source)
XLA Modules:
  0.0 176.3 jit_solution(14621196979354821308)
XLA Ops:
  1.3 0.8 fusion.4
  2.1 4.8 %fusion.5 = (bf16[64,128,128]{2,1,0:T(8,128)(2,1)S(1)}, f32[64,128,128]{2,1,0:T(8,128)}) fusion(f32[64,128,128]{2,1,0:T(8,128)} %param.5, f32[64]{0:T(128)S(1)} %compare_convert_fusion), kind=kLoop, calls=%fused_computation.25 | loop fusion | flops 2097152 | bytes 10486016 | tf_op jit(solution)/shard_map/convert_element_type | solution.py:110
  6.9 1.5 gather_fusion
  8.4 1.4 gather_fusion.1
  9.8 8.2 %collective-permute-start.1 = (bf16[16,128,128]{2,1,0:T(8,128)(2,1)}, bf16[16,128,128]{2,1,0:T(8,128)(2,1)S(1)}, u32[]{:S(2)}, u32[]{:S(2)}) collective-permute-start(bf16[16,128,128]{2,1,0:T(8,128)(2,1)} %gather_fusion.1), channel_id=1, source_target_pairs={{0,127},{1,0},{2,1},{3,2},{4,3},{5,4},{6,5},{7,6},{8,7},{9,8},{10,... | collective-permute-start | bytes 1572872 | tf_op jit(solution)/shard_map/ppermute | solution.py:16
  18.1 0.1 copy.11
  18.2 0.6 reshape.81.cols_ref
  18.8 4.9 %collective-permute-done.low_hbm = bf16[16,128,128]{2,1,0:T(8,128)(2,1)S(1)} collective-permute-done((bf16[16,128,128]{2,1,0:T(8,128)(2,1)}, bf16[16,128,128]{2,1,0:T(8,128)(2,1)S(1)}, u32[]{:S(2)}, u32[]{:S(2)}) %collective-permute-start) | collective-permute-done | bytes 524320 | tf_op jit(solution)/shard_map/ppermute | solution.py:16
  23.7 1.4 collective-permute-done.1.high_hbm
  25.1 0.8 copy-done.3
  25.9 14.7 %shard_map.68 = (f32[64,128,128]{2,1,0:T(8,128)}, bf16[64,128,128]{2,1,0:T(8,128)(2,1)}) custom-call(s32[512]{0:T(512)} %reshape.81.cols_ref, s32[1]{0:T(128)} %copy.16.count_ref, bf16[64,128,128]{2,1,0:T(8,128)(2,1)} %copy-done, bf16[16,128,128]{2,1,0:T(8,128)(2,1)} %copy-done.1, bf16[16,128,128]{2,1,0:T(8,128)(2,1)} %copy-done.3, ...), custom_call_target="tpu_custom_call" | custom-call | tf_op jit(solution)/shard_map/pallas_call | solution.py:94
  40.6 2.2 %gather_fusion.3 = bf16[16,128,128]{2,1,0:T(8,128)(2,1)S(1)} fusion(bf16[64,128,128]{2,1,0:T(8,128)(2,1)} %get-tuple-element.8.own_hbm, s32[1024]{0:T(1024)S(1)} %pad_clamp_fusion), kind=kCustom, calls=%fused_computation.3 | custom fusion | bytes 1048640 | tf_op jit(solution)/shard_map/gather | solution.py:113
  42.8 2.2 %gather_fusion.2 = bf16[16,128,128]{2,1,0:T(8,128)(2,1)S(1)} fusion(bf16[64,128,128]{2,1,0:T(8,128)(2,1)} %get-tuple-element.8.own_hbm, s32[1024]{0:T(1024)S(1)} %pad_clamp_fusion.1), kind=kCustom, calls=%fused_computation.2 | custom fusion | bytes 1048640 | tf_op jit(solution)/shard_map/gather | solution.py:114
  45.2 7.3 %collective-permute-start.3 = (bf16[16,128,128]{2,1,0:T(8,128)(2,1)S(1)}, bf16[16,128,128]{2,1,0:T(8,128)(2,1)S(1)}, u32[]{:S(2)}, u32[]{:S(2)}) collective-permute-start(bf16[16,128,128]{2,1,0:T(8,128)(2,1)S(1)} %gather_fusion.3), channel_id=1, source_target_pairs={{0,127},{1,0},{2,1},{3,2},{4,3},{5,4},{6,5},{7,6},{8,7},{9,8},{10,... | collective-permute-start | bytes 1572872 | tf_op jit(solution)/shard_map/ppermute | solution.py:16
  52.5 6.8 %collective-permute-done.2.low_hbm = bf16[16,128,128]{2,1,0:T(8,128)(2,1)S(1)} collective-permute-done((bf16[16,128,128]{2,1,0:T(8,128)(2,1)S(1)}, bf16[16,128,128]{2,1,0:T(8,128)(2,1)S(1)}, u32[]{:S(2)}, u32[]{:S(2)}) %collective-permute-start.2) | collective-permute-done | bytes 524320 | tf_op jit(solution)/shard_map/ppermute | solution.py:16
  59.3 0.8 copy-done.4
  60.1 0.2 copy-done.6
  60.3 14.6 %shard_map.69 = (f32[64,128,128]{2,1,0:T(8,128)}, bf16[64,128,128]{2,1,0:T(8,128)(2,1)}) custom-call(s32[512]{0:T(512)} %reshape.81.cols_ref, s32[1]{0:T(128)} %copy.16.count_ref, bf16[64,128,128]{2,1,0:T(8,128)(2,1)} %get-tuple-element.8.own_hbm, bf16[16,128,128]{2,1,0:T(8,128)(2,1)} %copy-done.4, bf16[16,128,128]{2,1,0:T(8,128)(2,1)} %copy-done.6, ...), custom_call_target="tpu_custom_call" | custom-call | tf_op jit(solution)/shard_map/pallas_call | solution.py:94
  75.0 2.2 %gather_fusion.5 = bf16[16,128,128]{2,1,0:T(8,128)(2,1)S(1)} fusion(bf16[64,128,128]{2,1,0:T(8,128)(2,1)} %get-tuple-element.10.own_hbm, s32[1024]{0:T(1024)S(1)} %pad_clamp_fusion), kind=kCustom, calls=%fused_computation.5 | custom fusion | bytes 1048640 | tf_op jit(solution)/shard_map/gather | solution.py:113
  77.2 2.2 %gather_fusion.4 = bf16[16,128,128]{2,1,0:T(8,128)(2,1)S(1)} fusion(bf16[64,128,128]{2,1,0:T(8,128)(2,1)} %get-tuple-element.10.own_hbm, s32[1024]{0:T(1024)S(1)} %pad_clamp_fusion.1), kind=kCustom, calls=%fused_computation.4 | custom fusion | bytes 1048640 | tf_op jit(solution)/shard_map/gather | solution.py:114
  79.5 7.2 %collective-permute-start.5 = (bf16[16,128,128]{2,1,0:T(8,128)(2,1)S(1)}, bf16[16,128,128]{2,1,0:T(8,128)(2,1)S(1)}, u32[]{:S(2)}, u32[]{:S(2)}) collective-permute-start(bf16[16,128,128]{2,1,0:T(8,128)(2,1)S(1)} %gather_fusion.5), channel_id=1, source_target_pairs={{0,127},{1,0},{2,1},{3,2},{4,3},{5,4},{6,5},{7,6},{8,7},{9,8},{10,... | collective-permute-start | bytes 1572872 | tf_op jit(solution)/shard_map/ppermute | solution.py:16
  86.7 6.9 %collective-permute-done.4.low_hbm = bf16[16,128,128]{2,1,0:T(8,128)(2,1)S(1)} collective-permute-done((bf16[16,128,128]{2,1,0:T(8,128)(2,1)S(1)}, bf16[16,128,128]{2,1,0:T(8,128)(2,1)S(1)}, u32[]{:S(2)}, u32[]{:S(2)}) %collective-permute-start.4) | collective-permute-done | bytes 524320 | tf_op jit(solution)/shard_map/ppermute | solution.py:16
  93.6 0.8 copy-done.2
  94.3 0.2 copy-done.5
  94.5 18.1 %shard_map.70 = (f32[64,128,128]{2,1,0:T(8,128)}, f32[128,128]{1,0:T(8,128)}) custom-call(s32[512]{0:T(512)} %reshape.81.cols_ref, s32[1]{0:T(128)} %copy.16.count_ref, bf16[64,128,128]{2,1,0:T(8,128)(2,1)} %get-tuple-element.10.own_hbm, bf16[16,128,128]{2,1,0:T(8,128)(2,1)} %copy-done.2, bf16[16,128,128]{2,1,0:T(8,128)(2,1)} %copy-done.5, ...), custom_call_target="tpu_custom_call" | custom-call | tf_op jit(solution)/shard_map/pallas_call | solution.py:94
  112.7 0.9 copy.13
  113.6 0.1 collective-permute-start.6
  113.7 1.2 collective-permute-done.6
  115.0 0.1 collective-permute-start.7
  115.1 4.3 %collective-permute-done.7 = f32[128,128]{0,1:T(8,128)S(1)} collective-permute-done((f32[128,128]{0,1:T(8,128)S(1)}, f32[128,128]{0,1:T(8,128)S(1)}, u32[]{:S(2)}, u32[]{:S(2)}) %collective-permute-start.7) | collective-permute-done | bytes 65568 | tf_op jit(solution)/shard_map/ppermute | solution.py:24
  119.3 0.1 collective-permute-start.8
  119.4 5.8 %collective-permute-done.8 = f32[128,128]{0,1:T(8,128)S(1)} collective-permute-done((f32[128,128]{0,1:T(8,128)S(1)}, f32[128,128]{0,1:T(8,128)S(1)}, u32[]{:S(2)}, u32[]{:S(2)}) %collective-permute-start.8) | collective-permute-done | bytes 65568 | tf_op jit(solution)/shard_map/ppermute | solution.py:24
  125.2 0.1 collective-permute-start.9
  125.3 4.3 %collective-permute-done.9 = f32[128,128]{0,1:T(8,128)S(1)} collective-permute-done((f32[128,128]{0,1:T(8,128)S(1)}, f32[128,128]{0,1:T(8,128)S(1)}, u32[]{:S(2)}, u32[]{:S(2)}) %collective-permute-start.9) | collective-permute-done | bytes 65568 | tf_op jit(solution)/shard_map/ppermute | solution.py:24
  129.5 0.1 collective-permute-start.10
  129.6 5.8 %collective-permute-done.10 = f32[128,128]{0,1:T(8,128)S(1)} collective-permute-done((f32[128,128]{0,1:T(8,128)S(1)}, f32[128,128]{0,1:T(8,128)S(1)}, u32[]{:S(2)}, u32[]{:S(2)}) %collective-permute-start.10) | collective-permute-done | bytes 65568 | tf_op jit(solution)/shard_map/ppermute | solution.py:24
  135.4 0.1 collective-permute-start.11
  135.5 4.3 %collective-permute-done.11 = f32[128,128]{0,1:T(8,128)S(1)} collective-permute-done((f32[128,128]{0,1:T(8,128)S(1)}, f32[128,128]{0,1:T(8,128)S(1)}, u32[]{:S(2)}, u32[]{:S(2)}) %collective-permute-start.11) | collective-permute-done | bytes 65568 | tf_op jit(solution)/shard_map/ppermute | solution.py:24
  139.8 0.3 collective-permute-start.12
  140.1 5.7 %collective-permute-done.12 = f32[128,128]{0,1:T(8,128)S(1)} collective-permute-done((f32[128,128]{0,1:T(8,128)S(1)}, f32[128,128]{0,1:T(8,128)S(1)}, u32[]{:S(2)}, u32[]{:S(2)}) %collective-permute-start.12) | collective-permute-done | bytes 65568 | tf_op jit(solution)/shard_map/ppermute | solution.py:24
  145.8 0.1 copy.14
  145.9 11.7 %cholesky.17 = f32[128,128]{1,0:T(8,128)S(1)} custom-call(f32[128,128]{1,0:T(8,128)S(1)} %fusion.1), custom_call_target="Cholesky" | custom-call | tf_op jit(solution)/shard_map/jit(cholesky)/cholesky | solution.py:121
  157.7 0.6 compare_reduce_fusion
  158.3 0.7 fusion.2
  159.0 0.7 copy.15
  159.7 9.8 %custom-call.6 = f32[1,128,128]{1,2,0:T(8,128)S(1)} custom-call(f32[1,128,128]{2,1,0:T(8,128)S(1)} %get-tuple-element.21), custom_call_target="InvertDiagBlocksLowerTriangular" | custom-call | tf_op jit(solution)/shard_map/triangular_solve | solution.py:122
  169.5 0.2 convolution_bitcast_fusion
  169.8 6.6 %fusion.6 = f32[64,128,128]{2,1,0:T(8,128)} fusion(f32[64,128,128]{2,1,0:T(8,128)} %get-tuple-element.12, f32[128,128,1]{1,0,2:T(8,128)S(1)} %convolution_bitcast_fusion), kind=kOutput, calls=%fused_computation.26 | convolution fusion | flops 1610612736 | bytes 8454144 | tf_op jit(solution)/shard_map/dot_general | solution.py:125
  (28 shorter events, 0.3 us)
Async XLA Ops:
  2.1 16.0 %copy-start.7 = (s32[64,8]{0,1:T(8,128)S(1)}, s32[64,8]{0,1:T(8,128)}, u32[]{:S(2)}) copy-start(s32[64,8]{0,1:T(8,128)} %param.7) | copy-start | bytes 6148
  6.9 18.2 %copy-start = (bf16[64,128,128]{2,1,0:T(8,128)(2,1)}, bf16[64,128,128]{2,1,0:T(8,128)(2,1)S(1)}, u32[]{:S(2)}) copy-start(bf16[64,128,128]{2,1,0:T(8,128)(2,1)S(1)} %get-tuple-element.18.own_hbm) | copy-start | bytes 6291460
  8.4 15.3 %collective-permute-start = (bf16[16,128,128]{2,1,0:T(8,128)(2,1)}, bf16[16,128,128]{2,1,0:T(8,128)(2,1)S(1)}, u32[]{:S(2)}, u32[]{:S(2)}) collective-permute-start(bf16[16,128,128]{2,1,0:T(8,128)(2,1)} %gather_fusion), channel_id=1, source_target_pairs={{0,1},{1,2},{2,3},{3,4},{4,5},{5,6},{6,7},{7,8},{8,9},{9,10},{10,1... | collective-permute-start | bytes 1572872 | tf_op jit(solution)/shard_map/ppermute | solution.py:16
  9.8 15.2 %collective-permute-start.1 = (bf16[16,128,128]{2,1,0:T(8,128)(2,1)}, bf16[16,128,128]{2,1,0:T(8,128)(2,1)S(1)}, u32[]{:S(2)}, u32[]{:S(2)}) collective-permute-start(bf16[16,128,128]{2,1,0:T(8,128)(2,1)} %gather_fusion.1), channel_id=1, source_target_pairs={{0,127},{1,0},{2,1},{3,2},{4,3},{5,4},{6,5},{7,6},{8,7},{9,8},{10,... | collective-permute-start | bytes 1572872 | tf_op jit(solution)/shard_map/ppermute | solution.py:16
  23.7 1.4 copy-start.1
  25.1 0.8 copy-start.3
  45.1 14.2 %collective-permute-start.2 = (bf16[16,128,128]{2,1,0:T(8,128)(2,1)S(1)}, bf16[16,128,128]{2,1,0:T(8,128)(2,1)S(1)}, u32[]{:S(2)}, u32[]{:S(2)}) collective-permute-start(bf16[16,128,128]{2,1,0:T(8,128)(2,1)S(1)} %gather_fusion.2), channel_id=1, source_target_pairs={{0,1},{1,2},{2,3},{3,4},{4,5},{5,6},{6,7},{7,8},{8,9},{9,10},{10,1... | collective-permute-start | bytes 1572872 | tf_op jit(solution)/shard_map/ppermute | solution.py:16
  45.2 14.1 %collective-permute-start.3 = (bf16[16,128,128]{2,1,0:T(8,128)(2,1)S(1)}, bf16[16,128,128]{2,1,0:T(8,128)(2,1)S(1)}, u32[]{:S(2)}, u32[]{:S(2)}) collective-permute-start(bf16[16,128,128]{2,1,0:T(8,128)(2,1)S(1)} %gather_fusion.3), channel_id=1, source_target_pairs={{0,127},{1,0},{2,1},{3,2},{4,3},{5,4},{6,5},{7,6},{8,7},{9,8},{10,... | collective-permute-start | bytes 1572872 | tf_op jit(solution)/shard_map/ppermute | solution.py:16
  59.3 0.9 copy-start.4
  59.3 1.1 copy-start.6
  79.4 14.1 %collective-permute-start.4 = (bf16[16,128,128]{2,1,0:T(8,128)(2,1)S(1)}, bf16[16,128,128]{2,1,0:T(8,128)(2,1)S(1)}, u32[]{:S(2)}, u32[]{:S(2)}) collective-permute-start(bf16[16,128,128]{2,1,0:T(8,128)(2,1)S(1)} %gather_fusion.4), channel_id=1, source_target_pairs={{0,1},{1,2},{2,3},{3,4},{4,5},{5,6},{6,7},{7,8},{8,9},{9,10},{10,1... | collective-permute-start | bytes 1572872 | tf_op jit(solution)/shard_map/ppermute | solution.py:16
  79.5 14.0 %collective-permute-start.5 = (bf16[16,128,128]{2,1,0:T(8,128)(2,1)S(1)}, bf16[16,128,128]{2,1,0:T(8,128)(2,1)S(1)}, u32[]{:S(2)}, u32[]{:S(2)}) collective-permute-start(bf16[16,128,128]{2,1,0:T(8,128)(2,1)S(1)} %gather_fusion.5), channel_id=1, source_target_pairs={{0,127},{1,0},{2,1},{3,2},{4,3},{5,4},{6,5},{7,6},{8,7},{9,8},{10,... | collective-permute-start | bytes 1572872 | tf_op jit(solution)/shard_map/ppermute | solution.py:16
  93.5 0.8 copy-start.2
  93.6 1.0 copy-start.5
  113.6 1.3 collective-permute-start.6
  115.0 4.3 %collective-permute-start.7 = (f32[128,128]{0,1:T(8,128)S(1)}, f32[128,128]{0,1:T(8,128)S(1)}, u32[]{:S(2)}, u32[]{:S(2)}) collective-permute-start(f32[128,128]{0,1:T(8,128)S(1)} %add.58), channel_id=1, source_target_pairs={{0,2},{1,3},{2,0},{3,1},{4,6},{5,7},{6,4},{7,5},{8,10},{9,11},{10,... | collective-permute-start | bytes 196616 | tf_op jit(solution)/shard_map/ppermute | solution.py:24
  119.3 5.8 %collective-permute-start.8 = (f32[128,128]{0,1:T(8,128)S(1)}, f32[128,128]{0,1:T(8,128)S(1)}, u32[]{:S(2)}, u32[]{:S(2)}) collective-permute-start(f32[128,128]{0,1:T(8,128)S(1)} %add.59), channel_id=1, source_target_pairs={{0,4},{1,5},{2,6},{3,7},{4,0},{5,1},{6,2},{7,3},{8,12},{9,13},{10,... | collective-permute-start | bytes 196616 | tf_op jit(solution)/shard_map/ppermute | solution.py:24
  125.2 4.3 %collective-permute-start.9 = (f32[128,128]{0,1:T(8,128)S(1)}, f32[128,128]{0,1:T(8,128)S(1)}, u32[]{:S(2)}, u32[]{:S(2)}) collective-permute-start(f32[128,128]{0,1:T(8,128)S(1)} %add.60), channel_id=1, source_target_pairs={{0,8},{1,9},{2,10},{3,11},{4,12},{5,13},{6,14},{7,15},{8,0},{9,1},... | collective-permute-start | bytes 196616 | tf_op jit(solution)/shard_map/ppermute | solution.py:24
  129.5 5.8 %collective-permute-start.10 = (f32[128,128]{0,1:T(8,128)S(1)}, f32[128,128]{0,1:T(8,128)S(1)}, u32[]{:S(2)}, u32[]{:S(2)}) collective-permute-start(f32[128,128]{0,1:T(8,128)S(1)} %add.61), channel_id=1, source_target_pairs={{0,16},{1,17},{2,18},{3,19},{4,20},{5,21},{6,22},{7,23},{8,24},{9,... | collective-permute-start | bytes 196616 | tf_op jit(solution)/shard_map/ppermute | solution.py:24
  135.4 4.3 %collective-permute-start.11 = (f32[128,128]{0,1:T(8,128)S(1)}, f32[128,128]{0,1:T(8,128)S(1)}, u32[]{:S(2)}, u32[]{:S(2)}) collective-permute-start(f32[128,128]{0,1:T(8,128)S(1)} %add.62), channel_id=1, source_target_pairs={{0,32},{1,33},{2,34},{3,35},{4,36},{5,37},{6,38},{7,39},{8,40},{9,... | collective-permute-start | bytes 196616 | tf_op jit(solution)/shard_map/ppermute | solution.py:24
  139.8 6.0 %collective-permute-start.12 = (f32[128,128]{0,1:T(8,128)S(1)}, f32[128,128]{0,1:T(8,128)S(1)}, u32[]{:S(2)}, u32[]{:S(2)}) collective-permute-start(f32[128,128]{0,1:T(8,128)S(1)} %add.63), channel_id=1, source_target_pairs={{0,64},{1,65},{2,66},{3,67},{4,68},{5,69},{6,70},{7,71},{8,72},{9,... | collective-permute-start | bytes 196616 | tf_op jit(solution)/shard_map/ppermute | solution.py:24

commit v4 on v3

--- a/solution.py
+++ b/solution.py
@@ -26,32 +26,95 @@
     return value
 
 
+def row_update(cols_ref, blocks, extended, state, row, live, nnz):
+    acc = jnp.zeros(state.shape, jnp.float32)
+    for k in range(nnz):
+        col = cols_ref[row * nnz + k]
+        acc = acc + jnp.dot(blocks[k], extended[col], preferred_element_type=jnp.float32)
+    return state + jnp.where(live, acc, 0.0)
+
+
+def load_extended(own_hbm, low_hbm, high_hbm, extended, sems):
+    slots = own_hbm.shape[0]
+    halo = low_hbm.shape[0]
+    copies = [
+        pltpu.make_async_copy(own_hbm, extended.at[pl.ds(0, slots)], sems.at[0]),
+        pltpu.make_async_copy(low_hbm, extended.at[pl.ds(slots, halo)], sems.at[1]),
+        pltpu.make_async_copy(high_hbm, extended.at[pl.ds(slots + halo, halo)], sems.at[2]),
+    ]
+    for copy in copies:
+        copy.start()
+    return copies
+
+
+def send_kernel(cols_ref, count_ref, sends_ref, own_hbm, low_hbm, high_hbm, blocks_hbm, state_hbm,
+                to_lower_ref, to_upper_ref, extended, block_buf, state_buf, sems, row_sems, *, nnz):
+    rows = block_buf.shape[0]
+    copies = load_extended(own_hbm, low_hbm, high_hbm, extended, sems)
+    row_copies = []
+    for j in range(rows):
+        row = sends_ref[j]
+        pair = (
+            pltpu.make_async_copy(blocks_hbm.at[row], block_buf.at[j], row_sems.at[0, j]),
+            pltpu.make_async_copy(state_hbm.at[row], state_buf.at[j], row_sems.at[1, j]),
+        )
+        for copy in pair:
+            copy.start()
+        row_copies.append(pair)
+    for copy in copies:
+        copy.wait()
+    count = count_ref[0]
+    half = rows // 2
+    for j in range(rows):
+        for copy in row_copies[j]:
+            copy.wait()
+        row = sends_ref[j]
+        new = row_update(cols_ref, block_buf.at[j], extended, state_buf[j], row, row < count, nnz)
+        if j < half:
+            to_lower_ref[j] = new.astype(jnp.bfloat16)
+        else:
+            to_upper_ref[j - half] = new.astype(jnp.bfloat16)
+
+
+def send_rows(cols, count, sends, rounded, from_lower, from_upper, blocks, state):
+    slots, width, vectors = state.shape
+    nnz = blocks.shape[1]
+    halo = from_lower.shape[0]
+    rows = sends.shape[0]
+    kernel = functools.partial(send_kernel, nnz=nnz)
+    grid_spec = pltpu.PrefetchScalarGridSpec(
+        num_scalar_prefetch=3,
+        grid=(),
+        in_specs=[pl.BlockSpec(memory_space=pl.ANY)] * 5,
+        out_specs=[pl.BlockSpec(memory_space=pltpu.VMEM)] * 2,
+        scratch_shapes=[
+            pltpu.VMEM((slots + 2 * halo, width, vectors), jnp.bfloat16),
+            pltpu.VMEM((rows, nnz, width, width), jnp.bfloat16),
+            pltpu.VMEM((rows, width, vectors), jnp.float32),
+            pltpu.SemaphoreType.DMA((3,)),
+            pltpu.SemaphoreType.DMA((2, rows)),
+        ],
+    )
+    return pl.pallas_call(
+        kernel,
+        grid_spec=grid_spec,
+        out_shape=[jax.ShapeDtypeStruct((rows // 2, width, vectors), jnp.bfloat16)] * 2,
+    )(cols, count, sends, rounded, from_lower, from_upper, blocks, state)
+
+
 def substep_kernel(cols_ref, count_ref, own_hbm, low_hbm, high_hbm, blocks_ref, state_ref,
                    new_state_ref, out_ref, extended, sems, *, nnz, per_step, last):
     step = pl.program_id(0)
-    slots = own_hbm.shape[0]
-    halo = low_hbm.shape[0]
 
     @pl.when(step == 0)
     def _():
-        copies = [
-            pltpu.make_async_copy(own_hbm, extended.at[pl.ds(0, slots)], sems.at[0]),
-            pltpu.make_async_copy(low_hbm, extended.at[pl.ds(slots, halo)], sems.at[1]),
-            pltpu.make_async_copy(high_hbm, extended.at[pl.ds(slots + halo, halo)], sems.at[2]),
-        ]
-        for copy in copies:
-            copy.start()
-        for copy in copies:
+        for copy in load_extended(own_hbm, low_hbm, high_hbm, extended, sems):
             copy.wait()
 
     count = count_ref[0]
     for r in range(per_step):
         row = step * per_step + r
-        acc = jnp.zeros(state_ref.shape[1:], jnp.float32)
-        for k in range(nnz):
-            col = cols_ref[row * nnz + k]
-            acc = acc + jnp.dot(blocks_ref[r, k], extended[col], preferred_element_type=jnp.float32)
-        new = state_ref[r] + jnp.where(row < count, acc, 0.0)
+        new = row_update(cols_ref, blocks_ref.at[r], extended, state_ref[r], row, row < count, nnz)
         new_state_ref[r] = new
         if not last:
             out_ref[r] = new.astype(jnp.bfloat16)
@@ -109,11 +172,14 @@
     state = tangent * live
     rounded = state.astype(jnp.bfloat16)
     cols = columns.reshape(-1)
+    sends = send_lists.reshape(-1)
+    to_lower = rounded[send_lists[0, 0]]
+    to_upper = rounded[send_lists[0, 1]]
     for step in range(SUBSTEPS):
-        to_lower = rounded[send_lists[0, 0]]
-        to_upper = rounded[send_lists[0, 1]]
         from_lower = passed_along(to_upper, "grains", 1)
         from_upper = passed_along(to_lower, "grains", -1)
+        if step < SUBSTEPS - 1:
+            to_lower, to_upper = send_rows(cols, counts, sends, rounded, from_lower, from_upper, blocks, state)
         state, rounded = substep(cols, counts, rounded, from_lower, from_upper, blocks, state,
                                  step == SUBSTEPS - 1)
     gram = rounded

time: 177 us -> 186 us (1.051)
  Pallas kernels: 47.4 us -> 79.6 us
  waiting for transfers between devices: 51.2 us -> 36.9 us
  local copies, waits for them, and re-layouts: 17.2 us -> 8.8 us
    pallas_call x0 -> x2, Pallas kernels: none -> 32.2 us  [send_rows(): pl.pallas_call(kernel, grid_spec=grid_spec, out_shape=[jax.ShapeDtypeStru...]
    ppermute x6, waiting for transfers between devices: 19.9 us -> 5.66 us  [passed_along(): lax.ppermute(shard, axis, [(i, (i + by) % length) for i in range(length)])]
    gather x3 -> x1, local copies, waits for them, and re-layouts: 6.02 us -> 1.53 us  [local(): to_upper = rounded[send_lists[0, 1]]]
    gather x3 -> x1, local copies, waits for them, and re-layouts: 5.88 us -> 1.42 us  [local(): to_lower = rounded[send_lists[0, 0]]]
  transfers between devices with their start and end apart: 13 -> 13, of which waited for: 11 -> 9; matrix products, arithmetic and copies ran while one was open for 1% -> 1% of each run, Pallas kernels for 0% -> 16%
where the time goes in v4:
time: 186 us
  Pallas kernels  79.6 us (43%)
  waiting for transfers between devices  36.9 us (20%)
  other arithmetic  28.5 us (15%)
  starting transfers between devices  23.5 us (13%)
  local copies, waits for them, and re-layouts  8.8 us (5%)
  matrix products  6.79 us (4%)
    pallas_call x3, Pallas kernels, substep(): pl.pallas_call(kernel, grid_spec=grid_spec, out_shape=[jax.ShapeDtypeStru...  47.4 us
    pallas_call x2, Pallas kernels, send_rows(): pl.pallas_call(kernel, grid_spec=grid_spec, out_shape=[jax.ShapeDtypeStru...  32.2 us
    ppermute x7, waiting for transfers between devices, tree_sum(): value = value + lax.ppermute(value, axis, partner)  31.3 us
    ppermute x6, starting transfers between devices, passed_along(): lax.ppermute(shard, axis, [(i, (i + by) % length) for i in range(length)])  22.7 us
    another operation x3, other arithmetic, local(): first_low = jnp.linalg.cholesky(tree_sum(gram, 'grains'))  12.4 us
    another operation x1, other arithmetic, local(): lax.linalg.triangular_solve(first_low, jnp.eye(vectors, dtype=jnp.float32...  9.81 us
    dot_general x1, matrix products, local(): basis = jnp.dot(flat, inverse.T, precision=lax.Precision.HIGHEST)  6.54 us
    ppermute x6, waiting for transfers between devices, passed_along(): lax.ppermute(shard, axis, [(i, (i + by) % length) for i in range(length)])  5.66 us
  transfers between devices with their start and end apart: 13, of which 9 were waited for; matrix products, arithmetic and copies ran while one was open for 1% of the time, Pallas kernels for 16%

profile of v4, /device:TPU:0, one launch (start us, length us, event | category | flops | bytes accessed | tf_op | source)
XLA Modules:
  0.0 185.7 jit_solution(2245612918157846131)
XLA Ops:
  1.3 0.8 fusion.4
  2.1 0.0 copy-start.8
  2.1 4.8 %fusion.5 = (bf16[64,128,128]{2,1,0:T(8,128)(2,1)S(1)}, f32[64,128,128]{2,1,0:T(8,128)}) fusion(f32[64,128,128]{2,1,0:T(8,128)} %param.5, f32[64]{0:T(128)S(1)} %compare_convert_fusion), kind=kLoop, calls=%fused_computation.21 | loop fusion | flops 2097152 | bytes 10486016 | tf_op jit(solution)/shard_map/convert_element_type | solution.py:173
  6.9 1.5 gather_fusion
  8.4 1.4 gather_fusion.1
  9.9 8.2 %collective-permute-start.1 = (bf16[16,128,128]{2,1,0:T(8,128)(2,1)}, bf16[16,128,128]{2,1,0:T(8,128)(2,1)S(1)}, u32[]{:S(2)}, u32[]{:S(2)}) collective-permute-start(bf16[16,128,128]{2,1,0:T(8,128)(2,1)} %gather_fusion.1), channel_id=1, source_target_pairs={{0,127},{1,0},{2,1},{3,2},{4,3},{5,4},{6,5},{7,6},{8,7},{9,8},{10,... | collective-permute-start | bytes 1572872 | tf_op jit(solution)/shard_map/ppermute | solution.py:16
  18.1 0.6 reshape.85.sends_ref
  18.7 0.1 copy.11
  18.8 0.7 reshape.84.cols_ref
  19.5 4.3 %collective-permute-done.low_hbm = bf16[16,128,128]{2,1,0:T(8,128)(2,1)S(1)} collective-permute-done((bf16[16,128,128]{2,1,0:T(8,128)(2,1)}, bf16[16,128,128]{2,1,0:T(8,128)(2,1)S(1)}, u32[]{:S(2)}, u32[]{:S(2)}) %collective-permute-start) | collective-permute-done | bytes 524320 | tf_op jit(solution)/shard_map/ppermute | solution.py:16
  23.7 1.4 collective-permute-done.1.high_hbm
  25.1 0.8 copy-done.4
  25.9 16.1 %shard_map.69 = (bf16[16,128,128]{2,1,0:T(8,128)(2,1)}, bf16[16,128,128]{2,1,0:T(8,128)(2,1)}) custom-call(s32[512]{0:T(512)} %reshape.84.cols_ref, s32[1]{0:T(128)} %copy.16.count_ref, s32[32]{0:T(128)} %reshape.85.sends_ref, bf16[64,128,128]{2,1,0:T(8,128)(2,1)} %copy-done, bf16[16,128,128]{2,1,0:T(8,128)(2,1)} %copy-done.1, ...), custom_call_target="tpu_custom_call" | custom-call | tf_op jit(solution)/shard_map/pallas_call | solution.py:98
  42.1 0.1 collective-permute-start.2
  42.1 7.2 %collective-permute-start.3 = (bf16[16,128,128]{2,1,0:T(8,128)(2,1)}, bf16[16,128,128]{2,1,0:T(8,128)(2,1)S(1)}, u32[]{:S(2)}, u32[]{:S(2)}) collective-permute-start(bf16[16,128,128]{2,1,0:T(8,128)(2,1)} %get-tuple-element.14), channel_id=1, source_target_pairs={{0,127},{1,0},{2,1},{3,2},{4,3},{5,4},{6,5},{7,6},{8,7},{9,8},{10,... | collective-permute-start | bytes 1572872 | tf_op jit(solution)/shard_map/ppermute | solution.py:16
  49.3 14.7 %shard_map.68 = (f32[64,128,128]{2,1,0:T(8,128)}, bf16[64,128,128]{2,1,0:T(8,128)(2,1)}) custom-call(s32[512]{0:T(512)} %reshape.84.cols_ref, s32[1]{0:T(128)} %copy.16.count_ref, bf16[64,128,128]{2,1,0:T(8,128)(2,1)} %copy-done, bf16[16,128,128]{2,1,0:T(8,128)(2,1)} %copy-done.1, bf16[16,128,128]{2,1,0:T(8,128)(2,1)} %copy-done.4, ...), custom_call_target="tpu_custom_call" | custom-call | tf_op jit(solution)/shard_map/pallas_call | solution.py:157
  64.0 0.8 copy-done.2
  64.9 0.1 copy-done.3
  65.0 16.0 %shard_map.71 = (bf16[16,128,128]{2,1,0:T(8,128)(2,1)}, bf16[16,128,128]{2,1,0:T(8,128)(2,1)}) custom-call(s32[512]{0:T(512)} %reshape.84.cols_ref, s32[1]{0:T(128)} %copy.16.count_ref, s32[32]{0:T(128)} %reshape.85.sends_ref, bf16[64,128,128]{2,1,0:T(8,128)(2,1)} %get-tuple-element.12.own_hbm, bf16[16,128,128]{2,1,0:T(8,128)(2,1)} %copy-done.2, ...), custom_call_target="tpu_custom_call" | custom-call | tf_op jit(solution)/shard_map/pallas_call | solution.py:98
  81.0 0.1 collective-permute-start.4
  81.1 7.2 %collective-permute-start.5 = (bf16[16,128,128]{2,1,0:T(8,128)(2,1)}, bf16[16,128,128]{2,1,0:T(8,128)(2,1)S(1)}, u32[]{:S(2)}, u32[]{:S(2)}) collective-permute-start(bf16[16,128,128]{2,1,0:T(8,128)(2,1)} %get-tuple-element.18), channel_id=1, source_target_pairs={{0,127},{1,0},{2,1},{3,2},{4,3},{5,4},{6,5},{7,6},{8,7},{9,8},{10,... | collective-permute-start | bytes 1572872 | tf_op jit(solution)/shard_map/ppermute | solution.py:16
  88.3 14.6 %shard_map.70 = (f32[64,128,128]{2,1,0:T(8,128)}, bf16[64,128,128]{2,1,0:T(8,128)(2,1)}) custom-call(s32[512]{0:T(512)} %reshape.84.cols_ref, s32[1]{0:T(128)} %copy.16.count_ref, bf16[64,128,128]{2,1,0:T(8,128)(2,1)} %get-tuple-element.12.own_hbm, bf16[16,128,128]{2,1,0:T(8,128)(2,1)} %copy-done.2, bf16[16,128,128]{2,1,0:T(8,128)(2,1)} %copy-done.3, ...), custom_call_target="tpu_custom_call" | custom-call | tf_op jit(solution)/shard_map/pallas_call | solution.py:157
  103.0 0.8 copy-done.5
  103.7 0.2 copy-done.6
  103.9 18.1 %shard_map.72 = (f32[64,128,128]{2,1,0:T(8,128)}, f32[128,128]{1,0:T(8,128)}) custom-call(s32[512]{0:T(512)} %reshape.84.cols_ref, s32[1]{0:T(128)} %copy.16.count_ref, bf16[64,128,128]{2,1,0:T(8,128)(2,1)} %get-tuple-element.16.own_hbm, bf16[16,128,128]{2,1,0:T(8,128)(2,1)} %copy-done.5, bf16[16,128,128]{2,1,0:T(8,128)(2,1)} %copy-done.6, ...), custom_call_target="tpu_custom_call" | custom-call | tf_op jit(solution)/shard_map/pallas_call | solution.py:157
  122.0 0.9 copy.13
  123.0 0.1 collective-permute-start.6
  123.1 1.2 collective-permute-done.6
  124.3 0.1 collective-permute-start.7
  124.4 4.3 %collective-permute-done.7 = f32[128,128]{0,1:T(8,128)S(1)} collective-permute-done((f32[128,128]{0,1:T(8,128)S(1)}, f32[128,128]{0,1:T(8,128)S(1)}, u32[]{:S(2)}, u32[]{:S(2)}) %collective-permute-start.7) | collective-permute-done | bytes 65568 | tf_op jit(solution)/shard_map/ppermute | solution.py:24
  128.7 0.1 collective-permute-start.8
  128.8 5.8 %collective-permute-done.8 = f32[128,128]{0,1:T(8,128)S(1)} collective-permute-done((f32[128,128]{0,1:T(8,128)S(1)}, f32[128,128]{0,1:T(8,128)S(1)}, u32[]{:S(2)}, u32[]{:S(2)}) %collective-permute-start.8) | collective-permute-done | bytes 65568 | tf_op jit(solution)/shard_map/ppermute | solution.py:24
  134.6 0.1 collective-permute-start.9
  134.6 4.3 %collective-permute-done.9 = f32[128,128]{0,1:T(8,128)S(1)} collective-permute-done((f32[128,128]{0,1:T(8,128)S(1)}, f32[128,128]{0,1:T(8,128)S(1)}, u32[]{:S(2)}, u32[]{:S(2)}) %collective-permute-start.9) | collective-permute-done | bytes 65568 | tf_op jit(solution)/shard_map/ppermute | solution.py:24
  138.9 0.1 collective-permute-start.10
  139.0 5.8 %collective-permute-done.10 = f32[128,128]{0,1:T(8,128)S(1)} collective-permute-done((f32[128,128]{0,1:T(8,128)S(1)}, f32[128,128]{0,1:T(8,128)S(1)}, u32[]{:S(2)}, u32[]{:S(2)}) %collective-permute-start.10) | collective-permute-done | bytes 65568 | tf_op jit(solution)/shard_map/ppermute | solution.py:24
  144.8 0.1 collective-permute-start.11
  144.9 4.3 %collective-permute-done.11 = f32[128,128]{0,1:T(8,128)S(1)} collective-permute-done((f32[128,128]{0,1:T(8,128)S(1)}, f32[128,128]{0,1:T(8,128)S(1)}, u32[]{:S(2)}, u32[]{:S(2)}) %collective-permute-start.11) | collective-permute-done | bytes 65568 | tf_op jit(solution)/shard_map/ppermute | solution.py:24
  149.1 0.3 collective-permute-start.12
  149.4 5.8 %collective-permute-done.12 = f32[128,128]{0,1:T(8,128)S(1)} collective-permute-done((f32[128,128]{0,1:T(8,128)S(1)}, f32[128,128]{0,1:T(8,128)S(1)}, u32[]{:S(2)}, u32[]{:S(2)}) %collective-permute-start.12) | collective-permute-done | bytes 65568 | tf_op jit(solution)/shard_map/ppermute | solution.py:24
  155.2 0.1 copy.14
  155.3 11.7 %cholesky.17 = f32[128,128]{1,0:T(8,128)S(1)} custom-call(f32[128,128]{1,0:T(8,128)S(1)} %fusion.1), custom_call_target="Cholesky" | custom-call | tf_op jit(solution)/shard_map/jit(cholesky)/cholesky | solution.py:187
  167.1 0.6 compare_reduce_fusion
  167.7 0.7 fusion.2
  168.4 9.8 %custom-call.6 = f32[1,128,128]{1,2,0:T(8,128)S(1)} custom-call(f32[1,128,128]{2,1,0:T(8,128)S(1)} %get-tuple-element.29), custom_call_target="InvertDiagBlocksLowerTriangular" | custom-call | tf_op jit(solution)/shard_map/triangular_solve | solution.py:188
  178.2 0.2 convolution_bitcast_fusion
  178.4 0.7 copy.15
  179.2 6.5 %fusion.6 = f32[64,128,128]{2,1,0:T(8,128)} fusion(f32[64,128,128]{2,1,0:T(8,128)} %get-tuple-element.20, f32[128,128,1]{1,0,2:T(8,128)S(1)} %convolution_bitcast_fusion), kind=kOutput, calls=%fused_computation.22 | convolution fusion | flops 1610612736 | bytes 8454144 | tf_op jit(solution)/shard_map/dot_general | solution.py:191
  (29 shorter events, 0.2 us)
Async XLA Ops:
  2.1 16.0 %copy-start.8 = (s32[1,2,16]{2,1,0:T(2,128)S(1)}, s32[1,2,16]{2,1,0:T(2,128)}, u32[]{:S(2)}) copy-start(s32[1,2,16]{2,1,0:T(2,128)} %param.9) | copy-start | bytes 388
  2.1 16.6 %copy-start.7 = (s32[64,8]{0,1:T(8,128)S(1)}, s32[64,8]{0,1:T(8,128)}, u32[]{:S(2)}) copy-start(s32[64,8]{0,1:T(8,128)} %param.7) | copy-start | bytes 6148
  6.9 18.2 %copy-start = (bf16[64,128,128]{2,1,0:T(8,128)(2,1)}, bf16[64,128,128]{2,1,0:T(8,128)(2,1)S(1)}, u32[]{:S(2)}) copy-start(bf16[64,128,128]{2,1,0:T(8,128)(2,1)S(1)} %get-tuple-element.26.own_hbm) | copy-start | bytes 6291460
  8.4 15.3 %collective-permute-start = (bf16[16,128,128]{2,1,0:T(8,128)(2,1)}, bf16[16,128,128]{2,1,0:T(8,128)(2,1)S(1)}, u32[]{:S(2)}, u32[]{:S(2)}) collective-permute-start(bf16[16,128,128]{2,1,0:T(8,128)(2,1)} %gather_fusion), channel_id=1, source_target_pairs={{0,1},{1,2},{2,3},{3,4},{4,5},{5,6},{6,7},{7,8},{8,9},{9,10},{10,1... | collective-permute-start | bytes 1572872 | tf_op jit(solution)/shard_map/ppermute | solution.py:16
  9.9 15.2 %collective-permute-start.1 = (bf16[16,128,128]{2,1,0:T(8,128)(2,1)}, bf16[16,128,128]{2,1,0:T(8,128)(2,1)S(1)}, u32[]{:S(2)}, u32[]{:S(2)}) collective-permute-start(bf16[16,128,128]{2,1,0:T(8,128)(2,1)} %gather_fusion.1), channel_id=1, source_target_pairs={{0,127},{1,0},{2,1},{3,2},{4,3},{5,4},{6,5},{7,6},{8,7},{9,8},{10,... | collective-permute-start | bytes 1572872 | tf_op jit(solution)/shard_map/ppermute | solution.py:16
  23.7 1.4 copy-start.1
  25.1 0.8 copy-start.4
  42.1 21.9 %collective-permute-start.2 = (bf16[16,128,128]{2,1,0:T(8,128)(2,1)}, bf16[16,128,128]{2,1,0:T(8,128)(2,1)S(1)}, u32[]{:S(2)}, u32[]{:S(2)}) collective-permute-start(bf16[16,128,128]{2,1,0:T(8,128)(2,1)} %get-tuple-element.13), channel_id=1, source_target_pairs={{0,1},{1,2},{2,3},{3,4},{4,5},{5,6},{6,7},{7,8},{8,9},{9,10},{10,1... | collective-permute-start | bytes 1572872 | tf_op jit(solution)/shard_map/ppermute | solution.py:16
  42.1 21.9 %collective-permute-start.3 = (bf16[16,128,128]{2,1,0:T(8,128)(2,1)}, bf16[16,128,128]{2,1,0:T(8,128)(2,1)S(1)}, u32[]{:S(2)}, u32[]{:S(2)}) collective-permute-start(bf16[16,128,128]{2,1,0:T(8,128)(2,1)} %get-tuple-element.14), channel_id=1, source_target_pairs={{0,127},{1,0},{2,1},{3,2},{4,3},{5,4},{6,5},{7,6},{8,7},{9,8},{10,... | collective-permute-start | bytes 1572872 | tf_op jit(solution)/shard_map/ppermute | solution.py:16
  64.0 0.9 copy-start.2
  64.0 1.0 copy-start.3
  81.0 21.9 %collective-permute-start.4 = (bf16[16,128,128]{2,1,0:T(8,128)(2,1)}, bf16[16,128,128]{2,1,0:T(8,128)(2,1)S(1)}, u32[]{:S(2)}, u32[]{:S(2)}) collective-permute-start(bf16[16,128,128]{2,1,0:T(8,128)(2,1)} %get-tuple-element.17), channel_id=1, source_target_pairs={{0,1},{1,2},{2,3},{3,4},{4,5},{5,6},{6,7},{7,8},{8,9},{9,10},{10,1... | collective-permute-start | bytes 1572872 | tf_op jit(solution)/shard_map/ppermute | solution.py:16
  81.1 21.8 %collective-permute-start.5 = (bf16[16,128,128]{2,1,0:T(8,128)(2,1)}, bf16[16,128,128]{2,1,0:T(8,128)(2,1)S(1)}, u32[]{:S(2)}, u32[]{:S(2)}) collective-permute-start(bf16[16,128,128]{2,1,0:T(8,128)(2,1)} %get-tuple-element.18), channel_id=1, source_target_pairs={{0,127},{1,0},{2,1},{3,2},{4,3},{5,4},{6,5},{7,6},{8,7},{9,8},{10,... | collective-permute-start | bytes 1572872 | tf_op jit(solution)/shard_map/ppermute | solution.py:16
  102.9 0.8 copy-start.5
  102.9 1.0 copy-start.6
  123.0 1.3 collective-permute-start.6
  124.3 4.3 %collective-permute-start.7 = (f32[128,128]{0,1:T(8,128)S(1)}, f32[128,128]{0,1:T(8,128)S(1)}, u32[]{:S(2)}, u32[]{:S(2)}) collective-permute-start(f32[128,128]{0,1:T(8,128)S(1)} %add.54), channel_id=1, source_target_pairs={{0,2},{1,3},{2,0},{3,1},{4,6},{5,7},{6,4},{7,5},{8,10},{9,11},{10,... | collective-permute-start | bytes 196616 | tf_op jit(solution)/shard_map/ppermute | solution.py:24
  128.7 5.8 %collective-permute-start.8 = (f32[128,128]{0,1:T(8,128)S(1)}, f32[128,128]{0,1:T(8,128)S(1)}, u32[]{:S(2)}, u32[]{:S(2)}) collective-permute-start(f32[128,128]{0,1:T(8,128)S(1)} %add.55), channel_id=1, source_target_pairs={{0,4},{1,5},{2,6},{3,7},{4,0},{5,1},{6,2},{7,3},{8,12},{9,13},{10,... | collective-permute-start | bytes 196616 | tf_op jit(solution)/shard_map/ppermute | solution.py:24
  134.6 4.3 %collective-permute-start.9 = (f32[128,128]{0,1:T(8,128)S(1)}, f32[128,128]{0,1:T(8,128)S(1)}, u32[]{:S(2)}, u32[]{:S(2)}) collective-permute-start(f32[128,128]{0,1:T(8,128)S(1)} %add.56), channel_id=1, source_target_pairs={{0,8},{1,9},{2,10},{3,11},{4,12},{5,13},{6,14},{7,15},{8,0},{9,1},... | collective-permute-start | bytes 196616 | tf_op jit(solution)/shard_map/ppermute | solution.py:24
  138.9 5.8 %collective-permute-start.10 = (f32[128,128]{0,1:T(8,128)S(1)}, f32[128,128]{0,1:T(8,128)S(1)}, u32[]{:S(2)}, u32[]{:S(2)}) collective-permute-start(f32[128,128]{0,1:T(8,128)S(1)} %add.57), channel_id=1, source_target_pairs={{0,16},{1,17},{2,18},{3,19},{4,20},{5,21},{6,22},{7,23},{8,24},{9,... | collective-permute-start | bytes 196616 | tf_op jit(solution)/shard_map/ppermute | solution.py:24
  144.8 4.3 %collective-permute-start.11 = (f32[128,128]{0,1:T(8,128)S(1)}, f32[128,128]{0,1:T(8,128)S(1)}, u32[]{:S(2)}, u32[]{:S(2)}) collective-permute-start(f32[128,128]{0,1:T(8,128)S(1)} %add.58), channel_id=1, source_target_pairs={{0,32},{1,33},{2,34},{3,35},{4,36},{5,37},{6,38},{7,39},{8,40},{9,... | collective-permute-start | bytes 196616 | tf_op jit(solution)/shard_map/ppermute | solution.py:24
  149.1 6.1 %collective-permute-start.12 = (f32[128,128]{0,1:T(8,128)S(1)}, f32[128,128]{0,1:T(8,128)S(1)}, u32[]{:S(2)}, u32[]{:S(2)}) collective-permute-start(f32[128,128]{0,1:T(8,128)S(1)} %add.59), channel_id=1, source_target_pairs={{0,64},{1,65},{2,66},{3,67},{4,68},{5,69},{6,70},{7,71},{8,72},{9,... | collective-permute-start | bytes 196616 | tf_op jit(solution)/shard_map/ppermute | solution.py:24

commit v5 on v4

--- a/solution.py
+++ b/solution.py
@@ -9,6 +9,7 @@
 
 SUBSTEPS = 3
 ROWS_PER_STEP = 16
+SEND_WINDOW = 4
 
 
 def passed_along(shard, axis, by):
@@ -48,32 +49,38 @@
 
 
 def send_kernel(cols_ref, count_ref, sends_ref, own_hbm, low_hbm, high_hbm, blocks_hbm, state_hbm,
-                to_lower_ref, to_upper_ref, extended, block_buf, state_buf, sems, row_sems, *, nnz):
-    rows = block_buf.shape[0]
+                to_lower_ref, to_upper_ref, extended, block_buf, state_buf, sems, row_sems, *, nnz, rows):
+    window = block_buf.shape[0]
     copies = load_extended(own_hbm, low_hbm, high_hbm, extended, sems)
-    row_copies = []
-    for j in range(rows):
+
+    def row_copies(j):
         row = sends_ref[j]
-        pair = (
-            pltpu.make_async_copy(blocks_hbm.at[row], block_buf.at[j], row_sems.at[0, j]),
-            pltpu.make_async_copy(state_hbm.at[row], state_buf.at[j], row_sems.at[1, j]),
+        slot = j % window
+        return (
+            pltpu.make_async_copy(blocks_hbm.at[row], block_buf.at[slot], row_sems.at[0, slot]),
+            pltpu.make_async_copy(state_hbm.at[row], state_buf.at[slot], row_sems.at[1, slot]),
         )
-        for copy in pair:
+
+    for j in range(min(window, rows)):
+        for copy in row_copies(j):
             copy.start()
-        row_copies.append(pair)
     for copy in copies:
         copy.wait()
     count = count_ref[0]
     half = rows // 2
     for j in range(rows):
-        for copy in row_copies[j]:
+        for copy in row_copies(j):
             copy.wait()
         row = sends_ref[j]
-        new = row_update(cols_ref, block_buf.at[j], extended, state_buf[j], row, row < count, nnz)
+        slot = j % window
+        new = row_update(cols_ref, block_buf.at[slot], extended, state_buf[slot], row, row < count, nnz)
         if j < half:
             to_lower_ref[j] = new.astype(jnp.bfloat16)
         else:
             to_upper_ref[j - half] = new.astype(jnp.bfloat16)
+        if j + window < rows:
+            for copy in row_copies(j + window):
+                copy.start()
 
 
 def send_rows(cols, count, sends, rounded, from_lower, from_upper, blocks, state):
@@ -81,7 +88,8 @@
     nnz = blocks.shape[1]
     halo = from_lower.shape[0]
     rows = sends.shape[0]
-    kernel = functools.partial(send_kernel, nnz=nnz)
+    window = SEND_WINDOW
+    kernel = functools.partial(send_kernel, nnz=nnz, rows=rows)
     grid_spec = pltpu.PrefetchScalarGridSpec(
         num_scalar_prefetch=3,
         grid=(),
@@ -89,10 +97,10 @@
         out_specs=[pl.BlockSpec(memory_space=pltpu.VMEM)] * 2,
         scratch_shapes=[
             pltpu.VMEM((slots + 2 * halo, width, vectors), jnp.bfloat16),
-            pltpu.VMEM((rows, nnz, width, width), jnp.bfloat16),
-            pltpu.VMEM((rows, width, vectors), jnp.float32),
+            pltpu.VMEM((window, nnz, width, width), jnp.bfloat16),
+            pltpu.VMEM((window, width, vectors), jnp.float32),
             pltpu.SemaphoreType.DMA((3,)),
-            pltpu.SemaphoreType.DMA((2, rows)),
+            pltpu.SemaphoreType.DMA((2, window)),
         ],
     )
     return pl.pallas_call(
@@ -103,7 +111,8 @@
 
 
 def substep_kernel(cols_ref, count_ref, own_hbm, low_hbm, high_hbm, blocks_ref, state_ref,
-                   new_state_ref, out_ref, extended, sems, *, nnz, per_step, last):
+                   *rest, nnz, per_step, last, base):
+    new_state_ref, out_ref, extended, sems = rest[-4:]
     step = pl.program_id(0)
 
     @pl.when(step == 0)
@@ -113,7 +122,7 @@
 
     count = count_ref[0]
     for r in range(per_step):
-        row = step * per_step + r
+        row = (step + base) * per_step + r
         new = row_update(cols_ref, blocks_ref.at[r], extended, state_ref[r], row, row < count, nnz)
         new_state_ref[r] = new
         if not last:
@@ -128,26 +137,28 @@
         out_ref[...] += part
 
 
-def substep(cols, count, rounded, from_lower, from_upper, blocks, state, last):
+def substep(cols, count, rounded, from_lower, from_upper, blocks, state, last, part=0, parts=1, prev=()):
     slots, width, vectors = state.shape
     nnz = blocks.shape[1]
     halo = from_lower.shape[0]
     per_step = ROWS_PER_STEP
-    kernel = functools.partial(substep_kernel, nnz=nnz, per_step=per_step, last=last)
+    steps = slots // per_step // parts
+    base = part * steps
+    kernel = functools.partial(substep_kernel, nnz=nnz, per_step=per_step, last=last, base=base)
     grid_spec = pltpu.PrefetchScalarGridSpec(
         num_scalar_prefetch=2,
-        grid=(slots // per_step,),
+        grid=(steps,),
         in_specs=[
             pl.BlockSpec(memory_space=pl.ANY),
             pl.BlockSpec(memory_space=pl.ANY),
             pl.BlockSpec(memory_space=pl.ANY),
-            pl.BlockSpec((per_step, nnz, width, width), lambda i, c, n: (i, 0, 0, 0)),
-            pl.BlockSpec((per_step, width, vectors), lambda i, c, n: (i, 0, 0)),
-        ],
+            pl.BlockSpec((per_step, nnz, width, width), lambda i, c, n: (i + base, 0, 0, 0)),
+            pl.BlockSpec((per_step, width, vectors), lambda i, c, n: (i + base, 0, 0)),
+        ] + [pl.BlockSpec(memory_space=pl.ANY)] * len(prev),
         out_specs=[
-            pl.BlockSpec((per_step, width, vectors), lambda i, c, n: (i, 0, 0)),
+            pl.BlockSpec((per_step, width, vectors), lambda i, c, n: (i + base, 0, 0)),
             pl.BlockSpec((vectors, vectors), lambda i, c, n: (0, 0)) if last
-            else pl.BlockSpec((per_step, width, vectors), lambda i, c, n: (i, 0, 0)),
+            else pl.BlockSpec((per_step, width, vectors), lambda i, c, n: (i + base, 0, 0)),
         ],
         scratch_shapes=[
             pltpu.VMEM((slots + 2 * halo, width, vectors), jnp.bfloat16),
@@ -162,8 +173,9 @@
             jax.ShapeDtypeStruct((vectors, vectors), jnp.float32) if last
             else jax.ShapeDtypeStruct(state.shape, jnp.bfloat16),
         ],
+        input_output_aliases={7 + i: i for i in range(len(prev))},
         compiler_params=pltpu.CompilerParams(dimension_semantics=("arbitrary",)),
-    )(cols, count, rounded, from_lower, from_upper, blocks, state)
+    )(cols, count, rounded, from_lower, from_upper, blocks, state, *prev)
 
 
 def local(tangent, blocks, columns, counts, send_lists):
@@ -175,13 +187,17 @@
     sends = send_lists.reshape(-1)
     to_lower = rounded[send_lists[0, 0]]
     to_upper = rounded[send_lists[0, 1]]
-    for step in range(SUBSTEPS):
-        from_lower = passed_along(to_upper, "grains", 1)
-        from_upper = passed_along(to_lower, "grains", -1)
-        if step < SUBSTEPS - 1:
-            to_lower, to_upper = send_rows(cols, counts, sends, rounded, from_lower, from_upper, blocks, state)
-        state, rounded = substep(cols, counts, rounded, from_lower, from_upper, blocks, state,
-                                 step == SUBSTEPS - 1)
+    from_lower = passed_along(to_upper, "grains", 1)
+    from_upper = passed_along(to_lower, "grains", -1)
+    for step in range(SUBSTEPS - 1):
+        to_lower, to_upper = send_rows(cols, counts, sends, rounded, from_lower, from_upper, blocks, state)
+        next_upper = passed_along(to_lower, "grains", -1)
+        first = substep(cols, counts, rounded, from_lower, from_upper, blocks, state, False, 0, 2)
+        to_upper, first = lax.optimization_barrier((to_upper, first))
+        next_lower = passed_along(to_upper, "grains", 1)
+        state, rounded = substep(cols, counts, rounded, from_lower, from_upper, blocks, state, False, 1, 2, first)
+        from_lower, from_upper = next_lower, next_upper
+    state, rounded = substep(cols, counts, rounded, from_lower, from_upper, blocks, state, True)
     gram = rounded
     flat = state.reshape(slots * width, vectors)
     first_low = jnp.linalg.cholesky(tree_sum(gram, "grains"))

time: 186 us -> 193 us (1.038)
  waiting for transfers between devices: 36.9 us -> 46 us
  starting transfers between devices: 23.5 us -> 19.6 us
    ppermute x6, waiting for transfers between devices: 5.66 us -> 14.7 us  [passed_along(): lax.ppermute(shard, axis, [(i, (i + by) % length) for i in range(length)])]
    pallas_call x3 -> x5, Pallas kernels: 47.4 us -> 56.1 us  [substep(): pl.pallas_call(kernel, grid_spec=grid_spec, out_shape=[jax.ShapeDtypeStru...]
    pallas_call x2, Pallas kernels: 32.2 us -> 25.3 us  [send_rows(): pl.pallas_call(kernel, grid_spec=grid_spec, out_shape=[jax.ShapeDtypeStru...]
    ppermute x6, starting transfers between devices: 22.7 us -> 18.8 us  [passed_along(): lax.ppermute(shard, axis, [(i, (i + by) % length) for i in range(length)])]
  transfers between devices with their start and end apart: 13 -> 13, of which waited for: 9 -> 11; matrix products, arithmetic and copies ran while one was open for 1% -> 1% of each run, Pallas kernels for 16% -> 20%
where the time goes in v5:
time: 193 us; the launch traced here: 192 us
  Pallas kernels  81.4 us (42%)
  waiting for transfers between devices  46 us (24%)
  other arithmetic  28.5 us (15%)
  starting transfers between devices  19.6 us (10%)
  local copies, waits for them, and re-layouts  8.51 us (4%)
  matrix products  6.8 us (4%)
    pallas_call x5, Pallas kernels, substep(): pl.pallas_call(kernel, grid_spec=grid_spec, out_shape=[jax.ShapeDtypeStru...  56.1 us
    ppermute x7, waiting for transfers between devices, tree_sum(): value = value + lax.ppermute(value, axis, partner)  31.3 us
    pallas_call x2, Pallas kernels, send_rows(): pl.pallas_call(kernel, grid_spec=grid_spec, out_shape=[jax.ShapeDtypeStru...  25.3 us
    ppermute x6, starting transfers between devices, passed_along(): lax.ppermute(shard, axis, [(i, (i + by) % length) for i in range(length)])  18.8 us
    ppermute x6, waiting for transfers between devices, passed_along(): lax.ppermute(shard, axis, [(i, (i + by) % length) for i in range(length)])  14.7 us
    another operation x3, other arithmetic, local(): first_low = jnp.linalg.cholesky(tree_sum(gram, 'grains'))  12.4 us
    another operation x1, other arithmetic, local(): lax.linalg.triangular_solve(first_low, jnp.eye(vectors, dtype=jnp.float32...  9.81 us
    dot_general x1, matrix products, local(): basis = jnp.dot(flat, inverse.T, precision=lax.Precision.HIGHEST)  6.55 us
  transfers between devices with their start and end apart: 13, of which 11 were waited for; matrix products, arithmetic and copies ran while one was open for 1% of the time, Pallas kernels for 20%

profile of v5, /device:TPU:0, one launch (start us, length us, event | category | flops | bytes accessed | tf_op | source)
XLA Modules:
  0.0 192.4 jit_solution(7586523343534579708)
XLA Ops:
  1.3 0.8 fusion.4
  2.1 4.8 %fusion.5 = (bf16[64,128,128]{2,1,0:T(8,128)(2,1)S(1)}, f32[64,128,128]{2,1,0:T(8,128)}) fusion(f32[64,128,128]{2,1,0:T(8,128)} %param.5, f32[64]{0:T(128)S(1)} %compare_convert_fusion), kind=kLoop, calls=%fused_computation.21 | loop fusion | flops 2097152 | bytes 10486016 | tf_op jit(solution)/shard_map/convert_element_type | solution.py:185
  6.9 1.5 gather_fusion
  8.5 1.4 gather_fusion.1
  9.9 8.2 %collective-permute-start.1 = (bf16[16,128,128]{2,1,0:T(8,128)(2,1)}, bf16[16,128,128]{2,1,0:T(8,128)(2,1)S(1)}, u32[]{:S(2)}, u32[]{:S(2)}) collective-permute-start(bf16[16,128,128]{2,1,0:T(8,128)(2,1)} %gather_fusion.1), channel_id=1, source_target_pairs={{0,127},{1,0},{2,1},{3,2},{4,3},{5,4},{6,5},{7,6},{8,7},{9,8},{10,... | collective-permute-start | bytes 1572872 | tf_op jit(solution)/shard_map/ppermute | solution.py:17
  18.1 0.6 reshape.85.sends_ref
  18.7 0.1 copy.15
  18.8 0.6 reshape.84.cols_ref
  19.4 4.3 %collective-permute-done.low_hbm = bf16[16,128,128]{2,1,0:T(8,128)(2,1)S(1)} collective-permute-done((bf16[16,128,128]{2,1,0:T(8,128)(2,1)}, bf16[16,128,128]{2,1,0:T(8,128)(2,1)S(1)}, u32[]{:S(2)}, u32[]{:S(2)}) %collective-permute-start) | collective-permute-done | bytes 524320 | tf_op jit(solution)/shard_map/ppermute | solution.py:17
  23.8 1.4 collective-permute-done.1.high_hbm
  25.2 0.8 copy-done.4
  25.9 12.6 %shard_map.68 = (bf16[16,128,128]{2,1,0:T(8,128)(2,1)}, bf16[16,128,128]{2,1,0:T(8,128)(2,1)}) custom-call(s32[512]{0:T(512)} %reshape.84.cols_ref, s32[1]{0:T(128)} %copy.24.count_ref, s32[32]{0:T(128)} %reshape.85.sends_ref, bf16[64,128,128]{2,1,0:T(8,128)(2,1)} %copy-done, bf16[16,128,128]{2,1,0:T(8,128)(2,1)} %copy-done.2, ...), custom_call_target="tpu_custom_call" | custom-call | tf_op jit(solution)/shard_map/pallas_call | solution.py:106
  38.6 7.3 %collective-permute-start.3 = (bf16[16,128,128]{2,1,0:T(8,128)(2,1)}, bf16[16,128,128]{2,1,0:T(8,128)(2,1)S(1)}, u32[]{:S(2)}, u32[]{:S(2)}) collective-permute-start(bf16[16,128,128]{2,1,0:T(8,128)(2,1)} %get-tuple-element.29), channel_id=1, source_target_pairs={{0,127},{1,0},{2,1},{3,2},{4,3},{5,4},{6,5},{7,6},{8,7},{9,8},{10,... | collective-permute-start | bytes 1572872 | tf_op jit(solution)/shard_map/ppermute | solution.py:17
  45.9 9.5 %shard_map.69 = (f32[64,128,128]{2,1,0:T(8,128)}, bf16[64,128,128]{2,1,0:T(8,128)(2,1)}) custom-call(s32[512]{0:T(512)} %reshape.84.cols_ref, s32[1]{0:T(128)} %copy.24.count_ref, bf16[64,128,128]{2,1,0:T(8,128)(2,1)} %copy-done, bf16[16,128,128]{2,1,0:T(8,128)(2,1)} %copy-done.2, bf16[16,128,128]{2,1,0:T(8,128)(2,1)} %copy-done.4, ...), custom_call_target="tpu_custom_call" | custom-call | tf_op jit(solution)/shard_map/pallas_call | solution.py:168
  55.4 0.3 collective-permute-start.2
  55.6 9.5 %shard_map.70 = (f32[64,128,128]{2,1,0:T(8,128)}, bf16[64,128,128]{2,1,0:T(8,128)(2,1)}) custom-call(s32[512]{0:T(512)} %reshape.84.cols_ref, s32[1]{0:T(128)} %copy.24.count_ref, bf16[64,128,128]{2,1,0:T(8,128)(2,1)} %copy-done, bf16[16,128,128]{2,1,0:T(8,128)(2,1)} %copy-done.2, ...), custom_call_target="tpu_custom_call", output_to_operand_aliasing={{0}: (7, {}), {1}: (8, {})} | custom-call | tf_op jit(solution)/shard_map/pallas_call | solution.py:168
  65.2 4.5 %collective-permute-done.2.low_hbm = bf16[16,128,128]{2,1,0:T(8,128)(2,1)S(1)} collective-permute-done((bf16[16,128,128]{2,1,0:T(8,128)(2,1)S(1)}, bf16[16,128,128]{2,1,0:T(8,128)(2,1)S(1)}, u32[]{:S(2)}, u32[]{:S(2)}) %collective-permute-start.2) | collective-permute-done | bytes 524320 | tf_op jit(solution)/shard_map/ppermute | solution.py:17
  69.7 0.9 copy-done.3
  70.5 12.6 %shard_map.71 = (bf16[16,128,128]{2,1,0:T(8,128)(2,1)}, bf16[16,128,128]{2,1,0:T(8,128)(2,1)}) custom-call(s32[512]{0:T(512)} %reshape.84.cols_ref, s32[1]{0:T(128)} %copy.24.count_ref, s32[32]{0:T(128)} %reshape.85.sends_ref, bf16[64,128,128]{2,1,0:T(8,128)(2,1)} %get-tuple-element.27.own_hbm, bf16[16,128,128]{2,1,0:T(8,128)(2,1)} %copy-done.3, ...), custom_call_target="tpu_custom_call" | custom-call | tf_op jit(solution)/shard_map/pallas_call | solution.py:106
  83.2 3.0 %collective-permute-start.5 = (bf16[16,128,128]{2,1,0:T(8,128)(2,1)}, bf16[16,128,128]{2,1,0:T(8,128)(2,1)S(1)}, u32[]{:S(2)}, u32[]{:S(2)}) collective-permute-start(bf16[16,128,128]{2,1,0:T(8,128)(2,1)} %get-tuple-element.38), channel_id=1, source_target_pairs={{0,127},{1,0},{2,1},{3,2},{4,3},{5,4},{6,5},{7,6},{8,7},{9,8},{10,... | collective-permute-start | bytes 1572872 | tf_op jit(solution)/shard_map/ppermute | solution.py:17
  86.2 9.5 %shard_map.72 = (f32[64,128,128]{2,1,0:T(8,128)}, bf16[64,128,128]{2,1,0:T(8,128)(2,1)}) custom-call(s32[512]{0:T(512)} %reshape.84.cols_ref, s32[1]{0:T(128)} %copy.24.count_ref, bf16[64,128,128]{2,1,0:T(8,128)(2,1)} %get-tuple-element.27.own_hbm, bf16[16,128,128]{2,1,0:T(8,128)(2,1)} %copy-done.3, bf16[16,128,128]{2,1,0:T(8,128)(2,1)} %copy-done.1, ...), custom_call_target="tpu_custom_call" | custom-call | tf_op jit(solution)/shard_map/pallas_call | solution.py:168
  95.7 9.5 %shard_map.73 = (f32[64,128,128]{2,1,0:T(8,128)}, bf16[64,128,128]{2,1,0:T(8,128)(2,1)}) custom-call(s32[512]{0:T(512)} %reshape.84.cols_ref, s32[1]{0:T(128)} %copy.24.count_ref, bf16[64,128,128]{2,1,0:T(8,128)(2,1)} %get-tuple-element.27.own_hbm, bf16[16,128,128]{2,1,0:T(8,128)(2,1)} %copy-done.3, ...), custom_call_target="tpu_custom_call", output_to_operand_aliasing={{0}: (7, {}), {1}: (8, {})} | custom-call | tf_op jit(solution)/shard_map/pallas_call | solution.py:168
  105.2 4.5 %collective-permute-done.4.low_hbm = bf16[16,128,128]{2,1,0:T(8,128)(2,1)S(1)} collective-permute-done((bf16[16,128,128]{2,1,0:T(8,128)(2,1)S(1)}, bf16[16,128,128]{2,1,0:T(8,128)(2,1)S(1)}, u32[]{:S(2)}, u32[]{:S(2)}) %collective-permute-start.4) | collective-permute-done | bytes 524320 | tf_op jit(solution)/shard_map/ppermute | solution.py:17
  109.8 0.8 copy-done.6
  110.6 18.1 %shard_map.74 = (f32[64,128,128]{2,1,0:T(8,128)}, f32[128,128]{1,0:T(8,128)}) custom-call(s32[512]{0:T(512)} %reshape.84.cols_ref, s32[1]{0:T(128)} %copy.24.count_ref, bf16[64,128,128]{2,1,0:T(8,128)(2,1)} %get-tuple-element.36.own_hbm, bf16[16,128,128]{2,1,0:T(8,128)(2,1)} %copy-done.6, bf16[16,128,128]{2,1,0:T(8,128)(2,1)} %copy-done.5, ...), custom_call_target="tpu_custom_call" | custom-call | tf_op jit(solution)/shard_map/pallas_call | solution.py:168
  128.7 0.9 copy.17
  129.6 0.1 collective-permute-start.6
  129.7 1.2 collective-permute-done.6
  131.0 0.1 collective-permute-start.7
  131.1 4.3 %collective-permute-done.7 = f32[128,128]{0,1:T(8,128)S(1)} collective-permute-done((f32[128,128]{0,1:T(8,128)S(1)}, f32[128,128]{0,1:T(8,128)S(1)}, u32[]{:S(2)}, u32[]{:S(2)}) %collective-permute-start.7) | collective-permute-done | bytes 65568 | tf_op jit(solution)/shard_map/ppermute | solution.py:25
  135.3 0.1 collective-permute-start.8
  135.4 5.8 %collective-permute-done.8 = f32[128,128]{0,1:T(8,128)S(1)} collective-permute-done((f32[128,128]{0,1:T(8,128)S(1)}, f32[128,128]{0,1:T(8,128)S(1)}, u32[]{:S(2)}, u32[]{:S(2)}) %collective-permute-start.8) | collective-permute-done | bytes 65568 | tf_op jit(solution)/shard_map/ppermute | solution.py:25
  141.2 0.3 collective-permute-start.9
  141.5 4.3 %collective-permute-done.9 = f32[128,128]{0,1:T(8,128)S(1)} collective-permute-done((f32[128,128]{0,1:T(8,128)S(1)}, f32[128,128]{0,1:T(8,128)S(1)}, u32[]{:S(2)}, u32[]{:S(2)}) %collective-permute-start.9) | collective-permute-done | bytes 65568 | tf_op jit(solution)/shard_map/ppermute | solution.py:25
  145.8 0.1 collective-permute-start.10
  145.9 5.8 %collective-permute-done.10 = f32[128,128]{0,1:T(8,128)S(1)} collective-permute-done((f32[128,128]{0,1:T(8,128)S(1)}, f32[128,128]{0,1:T(8,128)S(1)}, u32[]{:S(2)}, u32[]{:S(2)}) %collective-permute-start.10) | collective-permute-done | bytes 65568 | tf_op jit(solution)/shard_map/ppermute | solution.py:25
  151.7 0.1 collective-permute-start.11
  151.7 4.3 %collective-permute-done.11 = f32[128,128]{0,1:T(8,128)S(1)} collective-permute-done((f32[128,128]{0,1:T(8,128)S(1)}, f32[128,128]{0,1:T(8,128)S(1)}, u32[]{:S(2)}, u32[]{:S(2)}) %collective-permute-start.11) | collective-permute-done | bytes 65568 | tf_op jit(solution)/shard_map/ppermute | solution.py:25
  156.0 0.1 collective-permute-start.12
  156.1 5.8 %collective-permute-done.12 = f32[128,128]{0,1:T(8,128)S(1)} collective-permute-done((f32[128,128]{0,1:T(8,128)S(1)}, f32[128,128]{0,1:T(8,128)S(1)}, u32[]{:S(2)}, u32[]{:S(2)}) %collective-permute-start.12) | collective-permute-done | bytes 65568 | tf_op jit(solution)/shard_map/ppermute | solution.py:25
  161.9 0.1 copy.18
  162.0 11.7 %cholesky.17 = f32[128,128]{1,0:T(8,128)S(1)} custom-call(f32[128,128]{1,0:T(8,128)S(1)} %fusion.1), custom_call_target="Cholesky" | custom-call | tf_op jit(solution)/shard_map/jit(cholesky)/cholesky | solution.py:203
  173.7 0.6 compare_reduce_fusion
  174.4 0.7 fusion.2
  175.0 0.7 copy.19
  175.8 9.8 %custom-call.6 = f32[1,128,128]{1,2,0:T(8,128)S(1)} custom-call(f32[1,128,128]{2,1,0:T(8,128)S(1)} %get-tuple-element.49), custom_call_target="InvertDiagBlocksLowerTriangular" | custom-call | tf_op jit(solution)/shard_map/triangular_solve | solution.py:204
  185.6 0.2 convolution_bitcast_fusion
  185.8 6.5 %fusion.6 = f32[64,128,128]{2,1,0:T(8,128)} fusion(f32[64,128,128]{2,1,0:T(8,128)} %get-tuple-element.40, f32[128,128,1]{1,0,2:T(8,128)S(1)} %convolution_bitcast_fusion), kind=kOutput, calls=%fused_computation.22 | convolution fusion | flops 1610612736 | bytes 8454144 | tf_op jit(solution)/shard_map/dot_general | solution.py:207
  (35 shorter events, 0.3 us)
Async XLA Ops:
  2.1 16.1 %copy-start.8 = (s32[1,2,16]{2,1,0:T(2,128)S(1)}, s32[1,2,16]{2,1,0:T(2,128)}, u32[]{:S(2)}) copy-start(s32[1,2,16]{2,1,0:T(2,128)} %param.9) | copy-start | bytes 388
  2.1 16.7 %copy-start.7 = (s32[64,8]{0,1:T(8,128)S(1)}, s32[64,8]{0,1:T(8,128)}, u32[]{:S(2)}) copy-start(s32[64,8]{0,1:T(8,128)} %param.7) | copy-start | bytes 6148
  6.9 18.2 %copy-start = (bf16[64,128,128]{2,1,0:T(8,128)(2,1)}, bf16[64,128,128]{2,1,0:T(8,128)(2,1)S(1)}, u32[]{:S(2)}) copy-start(bf16[64,128,128]{2,1,0:T(8,128)(2,1)S(1)} %get-tuple-element.46.own_hbm) | copy-start | bytes 6291460
  8.5 15.3 %collective-permute-start = (bf16[16,128,128]{2,1,0:T(8,128)(2,1)}, bf16[16,128,128]{2,1,0:T(8,128)(2,1)S(1)}, u32[]{:S(2)}, u32[]{:S(2)}) collective-permute-start(bf16[16,128,128]{2,1,0:T(8,128)(2,1)} %gather_fusion), channel_id=1, source_target_pairs={{0,1},{1,2},{2,3},{3,4},{4,5},{5,6},{6,7},{7,8},{8,9},{9,10},{10,1... | collective-permute-start | bytes 1572872 | tf_op jit(solution)/shard_map/ppermute | solution.py:17
  9.9 15.2 %collective-permute-start.1 = (bf16[16,128,128]{2,1,0:T(8,128)(2,1)}, bf16[16,128,128]{2,1,0:T(8,128)(2,1)S(1)}, u32[]{:S(2)}, u32[]{:S(2)}) collective-permute-start(bf16[16,128,128]{2,1,0:T(8,128)(2,1)} %gather_fusion.1), channel_id=1, source_target_pairs={{0,127},{1,0},{2,1},{3,2},{4,3},{5,4},{6,5},{7,6},{8,7},{9,8},{10,... | collective-permute-start | bytes 1572872 | tf_op jit(solution)/shard_map/ppermute | solution.py:17
  23.8 1.4 copy-start.2
  25.1 0.8 copy-start.4
  38.6 16.8 %copy-start.10 = (bf16[16,128,128]{2,1,0:T(8,128)(2,1)S(1)}, bf16[16,128,128]{2,1,0:T(8,128)(2,1)}, u32[]{:S(2)}) copy-start(bf16[16,128,128]{2,1,0:T(8,128)(2,1)} %get-tuple-element.28) | copy-start | bytes 1572868
  38.6 26.6 %collective-permute-start.3 = (bf16[16,128,128]{2,1,0:T(8,128)(2,1)}, bf16[16,128,128]{2,1,0:T(8,128)(2,1)S(1)}, u32[]{:S(2)}, u32[]{:S(2)}) collective-permute-start(bf16[16,128,128]{2,1,0:T(8,128)(2,1)} %get-tuple-element.29), channel_id=1, source_target_pairs={{0,127},{1,0},{2,1},{3,2},{4,3},{5,4},{6,5},{7,6},{8,7},{9,8},{10,... | collective-permute-start | bytes 1572872 | tf_op jit(solution)/shard_map/ppermute | solution.py:17
  55.4 14.3 %collective-permute-start.2 = (bf16[16,128,128]{2,1,0:T(8,128)(2,1)S(1)}, bf16[16,128,128]{2,1,0:T(8,128)(2,1)S(1)}, u32[]{:S(2)}, u32[]{:S(2)}) collective-permute-start(bf16[16,128,128]{2,1,0:T(8,128)(2,1)S(1)} %copy-done.10), channel_id=1, source_target_pairs={{0,1},{1,2},{2,3},{3,4},{4,5},{5,6},{6,7},{7,8},{8,9},{9,10},{10,1... | collective-permute-start | bytes 1572872 | tf_op jit(solution)/shard_map/ppermute | solution.py:17
  65.2 4.5 %copy-start.1 = (bf16[16,128,128]{2,1,0:T(8,128)(2,1)}, bf16[16,128,128]{2,1,0:T(8,128)(2,1)S(1)}, u32[]{:S(2)}) copy-start(bf16[16,128,128]{2,1,0:T(8,128)(2,1)S(1)} %collective-permute-done.3.high_hbm) | copy-start | bytes 1572868
  69.7 0.9 copy-start.3
  83.2 12.4 %copy-start.9 = (bf16[16,128,128]{2,1,0:T(8,128)(2,1)S(1)}, bf16[16,128,128]{2,1,0:T(8,128)(2,1)}, u32[]{:S(2)}) copy-start(bf16[16,128,128]{2,1,0:T(8,128)(2,1)} %get-tuple-element.37) | copy-start | bytes 1572868
  83.2 22.0 %collective-permute-start.5 = (bf16[16,128,128]{2,1,0:T(8,128)(2,1)}, bf16[16,128,128]{2,1,0:T(8,128)(2,1)S(1)}, u32[]{:S(2)}, u32[]{:S(2)}) collective-permute-start(bf16[16,128,128]{2,1,0:T(8,128)(2,1)} %get-tuple-element.38), channel_id=1, source_target_pairs={{0,127},{1,0},{2,1},{3,2},{4,3},{5,4},{6,5},{7,6},{8,7},{9,8},{10,... | collective-permute-start | bytes 1572872 | tf_op jit(solution)/shard_map/ppermute | solution.py:17
  95.6 14.1 %collective-permute-start.4 = (bf16[16,128,128]{2,1,0:T(8,128)(2,1)S(1)}, bf16[16,128,128]{2,1,0:T(8,128)(2,1)S(1)}, u32[]{:S(2)}, u32[]{:S(2)}) collective-permute-start(bf16[16,128,128]{2,1,0:T(8,128)(2,1)S(1)} %copy-done.9), channel_id=1, source_target_pairs={{0,1},{1,2},{2,3},{3,4},{4,5},{5,6},{6,7},{7,8},{8,9},{9,10},{10,1... | collective-permute-start | bytes 1572872 | tf_op jit(solution)/shard_map/ppermute | solution.py:17
  105.2 4.5 %copy-start.5 = (bf16[16,128,128]{2,1,0:T(8,128)(2,1)}, bf16[16,128,128]{2,1,0:T(8,128)(2,1)S(1)}, u32[]{:S(2)}) copy-start(bf16[16,128,128]{2,1,0:T(8,128)(2,1)S(1)} %collective-permute-done.5.high_hbm) | copy-start | bytes 1572868
  109.7 0.8 copy-start.6
  129.6 1.3 collective-permute-start.6
  131.0 4.3 %collective-permute-start.7 = (f32[128,128]{0,1:T(8,128)S(1)}, f32[128,128]{0,1:T(8,128)S(1)}, u32[]{:S(2)}, u32[]{:S(2)}) collective-permute-start(f32[128,128]{0,1:T(8,128)S(1)} %add.54), channel_id=1, source_target_pairs={{0,2},{1,3},{2,0},{3,1},{4,6},{5,7},{6,4},{7,5},{8,10},{9,11},{10,... | collective-permute-start | bytes 196616 | tf_op jit(solution)/shard_map/ppermute | solution.py:25
  135.3 5.8 %collective-permute-start.8 = (f32[128,128]{0,1:T(8,128)S(1)}, f32[128,128]{0,1:T(8,128)S(1)}, u32[]{:S(2)}, u32[]{:S(2)}) collective-permute-start(f32[128,128]{0,1:T(8,128)S(1)} %add.55), channel_id=1, source_target_pairs={{0,4},{1,5},{2,6},{3,7},{4,0},{5,1},{6,2},{7,3},{8,12},{9,13},{10,... | collective-permute-start | bytes 196616 | tf_op jit(solution)/shard_map/ppermute | solution.py:25
  141.2 4.6 %collective-permute-start.9 = (f32[128,128]{0,1:T(8,128)S(1)}, f32[128,128]{0,1:T(8,128)S(1)}, u32[]{:S(2)}, u32[]{:S(2)}) collective-permute-start(f32[128,128]{0,1:T(8,128)S(1)} %add.56), channel_id=1, source_target_pairs={{0,8},{1,9},{2,10},{3,11},{4,12},{5,13},{6,14},{7,15},{8,0},{9,1},... | collective-permute-start | bytes 196616 | tf_op jit(solution)/shard_map/ppermute | solution.py:25
  145.8 5.8 %collective-permute-start.10 = (f32[128,128]{0,1:T(8,128)S(1)}, f32[128,128]{0,1:T(8,128)S(1)}, u32[]{:S(2)}, u32[]{:S(2)}) collective-permute-start(f32[128,128]{0,1:T(8,128)S(1)} %add.57), channel_id=1, source_target_pairs={{0,16},{1,17},{2,18},{3,19},{4,20},{5,21},{6,22},{7,23},{8,24},{9,... | collective-permute-start | bytes 196616 | tf_op jit(solution)/shard_map/ppermute | solution.py:25
  151.7 4.3 %collective-permute-start.11 = (f32[128,128]{0,1:T(8,128)S(1)}, f32[128,128]{0,1:T(8,128)S(1)}, u32[]{:S(2)}, u32[]{:S(2)}) collective-permute-start(f32[128,128]{0,1:T(8,128)S(1)} %add.58), channel_id=1, source_target_pairs={{0,32},{1,33},{2,34},{3,35},{4,36},{5,37},{6,38},{7,39},{8,40},{9,... | collective-permute-start | bytes 196616 | tf_op jit(solution)/shard_map/ppermute | solution.py:25
  156.0 5.8 %collective-permute-start.12 = (f32[128,128]{0,1:T(8,128)S(1)}, f32[128,128]{0,1:T(8,128)S(1)}, u32[]{:S(2)}, u32[]{:S(2)}) collective-permute-start(f32[128,128]{0,1:T(8,128)S(1)} %add.59), channel_id=1, source_target_pairs={{0,64},{1,65},{2,66},{3,67},{4,68},{5,69},{6,70},{7,71},{8,72},{9,... | collective-permute-start | bytes 196616 | tf_op jit(solution)/shard_map/ppermute | solution.py:25

commit v6 on v3

--- a/solution.py
+++ b/solution.py
@@ -18,16 +18,23 @@
 
 def tree_sum(value, axis):
     length = lax.axis_size(axis)
-    distance = 1
-    while distance < length:
-        partner = [(i, i ^ distance) for i in range(length)]
+    masks = [1]
+    bit = 2
+    while bit < length:
+        masks += [bit, 3 * bit] if 4 * bit <= length else [bit]
+        bit *= 4
+    for mask in masks:
+        partner = [(i, i ^ mask) for i in range(length)]
         value = value + lax.ppermute(value, axis, partner)
-        distance *= 2
     return value
 
 
-def substep_kernel(cols_ref, count_ref, own_hbm, low_hbm, high_hbm, blocks_ref, state_ref,
-                   new_state_ref, out_ref, extended, sems, *, nnz, per_step, last):
+def substep_kernel(cols_ref, count_ref, sends_ref, own_hbm, low_hbm, high_hbm, blocks_ref, state_ref,
+                   new_state_ref, out_ref, *rest, nnz, per_step, last):
+    if last:
+        extended, sems = rest
+    else:
+        to_lower_ref, to_upper_ref, extended, sems = rest
     step = pl.program_id(0)
     slots = own_hbm.shape[0]
     halo = low_hbm.shape[0]
@@ -63,29 +70,41 @@
             def _():
                 out_ref[...] = jnp.zeros_like(out_ref)
         out_ref[...] += part
+    if last:
+        return
+    half = to_lower_ref.shape[0]
+    for j in range(2 * half):
+        local = sends_ref[j] - step * per_step
+
+        @pl.when((local >= 0) & (local < per_step))
+        def _():
+            if j < half:
+                to_lower_ref[j] = out_ref[local]
+            else:
+                to_upper_ref[j - half] = out_ref[local]
 
 
-def substep(cols, count, rounded, from_lower, from_upper, blocks, state, last):
+def substep(cols, count, sends, rounded, from_lower, from_upper, blocks, state, last):
     slots, width, vectors = state.shape
     nnz = blocks.shape[1]
     halo = from_lower.shape[0]
     per_step = ROWS_PER_STEP
     kernel = functools.partial(substep_kernel, nnz=nnz, per_step=per_step, last=last)
     grid_spec = pltpu.PrefetchScalarGridSpec(
-        num_scalar_prefetch=2,
+        num_scalar_prefetch=3,
         grid=(slots // per_step,),
         in_specs=[
             pl.BlockSpec(memory_space=pl.ANY),
             pl.BlockSpec(memory_space=pl.ANY),
             pl.BlockSpec(memory_space=pl.ANY),
-            pl.BlockSpec((per_step, nnz, width, width), lambda i, c, n: (i, 0, 0, 0)),
-            pl.BlockSpec((per_step, width, vectors), lambda i, c, n: (i, 0, 0)),
+            pl.BlockSpec((per_step, nnz, width, width), lambda i, c, n, q: (i, 0, 0, 0)),
+            pl.BlockSpec((per_step, width, vectors), lambda i, c, n, q: (i, 0, 0)),
         ],
         out_specs=[
-            pl.BlockSpec((per_step, width, vectors), lambda i, c, n: (i, 0, 0)),
-            pl.BlockSpec((vectors, vectors), lambda i, c, n: (0, 0)) if last
-            else pl.BlockSpec((per_step, width, vectors), lambda i, c, n: (i, 0, 0)),
-        ],
+            pl.BlockSpec((per_step, width, vectors), lambda i, c, n, q: (i, 0, 0)),
+            pl.BlockSpec((vectors, vectors), lambda i, c, n, q: (0, 0)) if last
+            else pl.BlockSpec((per_step, width, vectors), lambda i, c, n, q: (i, 0, 0)),
+        ] + ([] if last else [pl.BlockSpec((halo, width, vectors), lambda i, c, n, q: (0, 0, 0))] * 2),
         scratch_shapes=[
             pltpu.VMEM((slots + 2 * halo, width, vectors), jnp.bfloat16),
             pltpu.SemaphoreType.DMA((3,)),
@@ -98,9 +117,9 @@
             jax.ShapeDtypeStruct(state.shape, jnp.float32),
             jax.ShapeDtypeStruct((vectors, vectors), jnp.float32) if last
             else jax.ShapeDtypeStruct(state.shape, jnp.bfloat16),
-        ],
+        ] + ([] if last else [jax.ShapeDtypeStruct((halo, width, vectors), jnp.bfloat16)] * 2),
         compiler_params=pltpu.CompilerParams(dimension_semantics=("arbitrary",)),
-    )(cols, count, rounded, from_lower, from_upper, blocks, state)
+    )(cols, count, sends, rounded, from_lower, from_upper, blocks, state)
 
 
 def local(tangent, blocks, columns, counts, send_lists):
@@ -109,14 +128,17 @@
     state = tangent * live
     rounded = state.astype(jnp.bfloat16)
     cols = columns.reshape(-1)
+    sends = send_lists.reshape(-1)
+    to_lower = tangent[send_lists[0, 0]].astype(jnp.bfloat16)
+    to_upper = tangent[send_lists[0, 1]].astype(jnp.bfloat16)
     for step in range(SUBSTEPS):
-        to_lower = rounded[send_lists[0, 0]]
-        to_upper = rounded[send_lists[0, 1]]
         from_lower = passed_along(to_upper, "grains", 1)
         from_upper = passed_along(to_lower, "grains", -1)
-        state, rounded = substep(cols, counts, rounded, from_lower, from_upper, blocks, state,
-                                 step == SUBSTEPS - 1)
-    gram = rounded
+        if step < SUBSTEPS - 1:
+            state, rounded, to_lower, to_upper = substep(
+                cols, counts, sends, rounded, from_lower, from_upper, blocks, state, False)
+        else:
+            state, gram = substep(cols, counts, sends, rounded, from_lower, from_upper, blocks, state, True)
     flat = state.reshape(slots * width, vectors)
     first_low = jnp.linalg.cholesky(tree_sum(gram, "grains"))
     inverse = lax.linalg.triangular_solve(

time: 177 us -> 174 us (0.983)
  local copies, waits for them, and re-layouts: 17.2 us -> 12.9 us
  waiting for transfers between devices: 51.2 us -> 47.8 us
  Pallas kernels: 47.4 us -> 49.5 us
    gather x6 -> x2, local copies, waits for them, and re-layouts: 11.9 us -> 5.64 us  [the longest x1 2.82 us: local(): to_lower = tangent[send_lists[0, 0]].astype(jnp.bfloat16)]
    ppermute x7, waiting for transfers between devices: 31.2 us -> 28.6 us  [tree_sum(): value = value + lax.ppermute(value, axis, partner)]
    pallas_call x3, Pallas kernels: 47.4 us -> 49.5 us  [substep(): pl.pallas_call(kernel, grid_spec=grid_spec, out_shape=[jax.ShapeDtypeStru...]
    unnamed x18 -> x14, local copies, waits for them, and re-layouts: 3.68 us -> 4.25 us
  transfers between devices with their start and end apart: 13 -> 13, of which waited for: 11 -> 10; matrix products, arithmetic and copies ran while one was open for 1% -> 6% of each run, Pallas kernels for 0% -> 0%
where the time goes in v6:
time: 174 us; the launch traced here: 173 us
  Pallas kernels  49.5 us (28%)
  waiting for transfers between devices  47.8 us (27%)
  other arithmetic  29.2 us (17%)
  starting transfers between devices  25.4 us (15%)
  local copies, waits for them, and re-layouts  12.9 us (7%)
  matrix products  6.8 us (4%)
    pallas_call x3, Pallas kernels, substep(): pl.pallas_call(kernel, grid_spec=grid_spec, out_shape=[jax.ShapeDtypeStru...  49.5 us
    ppermute x7, waiting for transfers between devices, tree_sum(): value = value + lax.ppermute(value, axis, partner)  28.6 us
    ppermute x6, starting transfers between devices, passed_along(): lax.ppermute(shard, axis, [(i, (i + by) % length) for i in range(length)])  22.9 us
    ppermute x6, waiting for transfers between devices, passed_along(): lax.ppermute(shard, axis, [(i, (i + by) % length) for i in range(length)])  19.2 us
    another operation x3, other arithmetic, local(): first_low = jnp.linalg.cholesky(tree_sum(gram, 'grains'))  12.4 us
    another operation x1, other arithmetic, local(): lax.linalg.triangular_solve(first_low, jnp.eye(vectors, dtype=jnp.float32...  9.81 us
    dot_general x1, matrix products, local(): basis = jnp.dot(flat, inverse.T, precision=lax.Precision.HIGHEST)  6.55 us
    convert_element_type x1, other arithmetic, local(): rounded = state.astype(jnp.bfloat16)  5.53 us
  transfers between devices with their start and end apart: 13, of which 10 were waited for; matrix products, arithmetic and copies ran while one was open for 6% of the time, Pallas kernels for 0%

profile of v6, /device:TPU:0, one launch (start us, length us, event | category | flops | bytes accessed | tf_op | source)
XLA Modules:
  0.0 173.1 jit_solution(8958797785119401020)
XLA Ops:
  0.6 0.8 fusion.4
  1.4 2.8 %gather_fusion.1 = bf16[16,128,128]{2,1,0:T(8,128)(2,1)S(1)} fusion(f32[64,128,128]{2,1,0:T(8,128)} %param.5, s32[1024]{0:T(1024)S(1)} %pad_clamp_fusion), kind=kCustom, calls=%fused_computation.1 | custom fusion | bytes 1048640 | tf_op jit(solution)/shard_map/gather | solution.py:132
  4.2 8.3 %collective-permute-start.1 = (bf16[16,128,128]{2,1,0:T(8,128)(2,1)S(1)}, bf16[16,128,128]{2,1,0:T(8,128)(2,1)S(1)}, u32[]{:S(2)}, u32[]{:S(2)}) collective-permute-start(bf16[16,128,128]{2,1,0:T(8,128)(2,1)S(1)} %gather_fusion.1), channel_id=1, source_target_pairs={{0,127},{1,0},{2,1},{3,2},{4,3},{5,4},{6,5},{7,6},{8,7},{9,8},{10,... | collective-permute-start | bytes 1572872 | tf_op jit(solution)/shard_map/ppermute | solution.py:16
  12.5 2.8 %gather_fusion = bf16[16,128,128]{2,1,0:T(8,128)(2,1)S(1)} fusion(f32[64,128,128]{2,1,0:T(8,128)} %param.5, s32[1024]{0:T(1024)S(1)} %pad_clamp_fusion.1), kind=kCustom, calls=%fused_computation | custom fusion | bytes 1048640 | tf_op jit(solution)/shard_map/gather | solution.py:133
  15.4 0.1 collective-permute-start
  16.1 1.3 reshape.85.sends_ref
  17.4 0.8 copy.11
  18.2 0.7 reshape.84.cols_ref
  18.9 5.5 %fusion.5 = (bf16[64,128,128]{2,1,0:T(8,128)(2,1)}, f32[64,128,128]{2,1,0:T(8,128)}) fusion(f32[64,128,128]{2,1,0:T(8,128)} %param.5, f32[64]{0:T(128)S(1)} %compare_convert_fusion), kind=kLoop, calls=%fused_computation.21 | loop fusion | flops 2097152 | bytes 10486016 | tf_op jit(solution)/shard_map/convert_element_type | solution.py:129
  24.4 5.0 %collective-permute-done.low_hbm = bf16[16,128,128]{2,1,0:T(8,128)(2,1)S(1)} collective-permute-done((bf16[16,128,128]{2,1,0:T(8,128)(2,1)S(1)}, bf16[16,128,128]{2,1,0:T(8,128)(2,1)S(1)}, u32[]{:S(2)}, u32[]{:S(2)}) %collective-permute-start) | collective-permute-done | bytes 524320 | tf_op jit(solution)/shard_map/ppermute | solution.py:16
  29.5 0.8 copy-done.1
  30.3 15.7 %shard_map.68 = (f32[64,128,128]{2,1,0:T(8,128)}, bf16[64,128,128]{2,1,0:T(8,128)(2,1)}, bf16[16,128,128]{2,1,0:T(8,128)(2,1)}, bf16[16,128,128]{2,1,0:T(8,128)(2,1)}) custom-call(s32[512]{0:T(512)} %reshape.84.cols_ref, s32[1]{0:T(128)} %copy.16.count_ref, s32[32]{0:T(128)} %reshape.85.sends_ref, bf16[64,128,128]{2,1,0:T(8,128)(2,1)} %get-tuple-element.26.own_hbm, ...), custom_call_target="tpu_custom_call" | custom-call | tf_op jit(solution)/shard_map/pallas_call | solution.py:113
  46.0 0.1 collective-permute-start.2
  46.1 7.2 %collective-permute-start.3 = (bf16[16,128,128]{2,1,0:T(8,128)(2,1)}, bf16[16,128,128]{2,1,0:T(8,128)(2,1)S(1)}, u32[]{:S(2)}, u32[]{:S(2)}) collective-permute-start(bf16[16,128,128]{2,1,0:T(8,128)(2,1)} %get-tuple-element.14), channel_id=1, source_target_pairs={{0,127},{1,0},{2,1},{3,2},{4,3},{5,4},{6,5},{7,6},{8,7},{9,8},{10,... | collective-permute-start | bytes 1572872 | tf_op jit(solution)/shard_map/ppermute | solution.py:16
  53.2 7.1 %collective-permute-done.2.low_hbm = bf16[16,128,128]{2,1,0:T(8,128)(2,1)S(1)} collective-permute-done((bf16[16,128,128]{2,1,0:T(8,128)(2,1)}, bf16[16,128,128]{2,1,0:T(8,128)(2,1)S(1)}, u32[]{:S(2)}, u32[]{:S(2)}) %collective-permute-start.2) | collective-permute-done | bytes 524320 | tf_op jit(solution)/shard_map/ppermute | solution.py:16
  60.3 0.0 collective-permute-done.3.high_hbm
  60.3 0.8 copy-done.3
  61.1 0.1 copy-done.5
  61.3 15.6 %shard_map.69 = (f32[64,128,128]{2,1,0:T(8,128)}, bf16[64,128,128]{2,1,0:T(8,128)(2,1)}, bf16[16,128,128]{2,1,0:T(8,128)(2,1)}, bf16[16,128,128]{2,1,0:T(8,128)(2,1)}) custom-call(s32[512]{0:T(512)} %reshape.84.cols_ref, s32[1]{0:T(128)} %copy.16.count_ref, s32[32]{0:T(128)} %reshape.85.sends_ref, bf16[64,128,128]{2,1,0:T(8,128)(2,1)} %get-tuple-element.12.own_hbm, ...), custom_call_target="tpu_custom_call" | custom-call | tf_op jit(solution)/shard_map/pallas_call | solution.py:113
  76.9 0.1 collective-permute-start.4
  77.0 7.2 %collective-permute-start.5 = (bf16[16,128,128]{2,1,0:T(8,128)(2,1)}, bf16[16,128,128]{2,1,0:T(8,128)(2,1)S(1)}, u32[]{:S(2)}, u32[]{:S(2)}) collective-permute-start(bf16[16,128,128]{2,1,0:T(8,128)(2,1)} %get-tuple-element.18), channel_id=1, source_target_pairs={{0,127},{1,0},{2,1},{3,2},{4,3},{5,4},{6,5},{7,6},{8,7},{9,8},{10,... | collective-permute-start | bytes 1572872 | tf_op jit(solution)/shard_map/ppermute | solution.py:16
  84.2 7.1 %collective-permute-done.4.low_hbm = bf16[16,128,128]{2,1,0:T(8,128)(2,1)S(1)} collective-permute-done((bf16[16,128,128]{2,1,0:T(8,128)(2,1)}, bf16[16,128,128]{2,1,0:T(8,128)(2,1)S(1)}, u32[]{:S(2)}, u32[]{:S(2)}) %collective-permute-start.4) | collective-permute-done | bytes 524320 | tf_op jit(solution)/shard_map/ppermute | solution.py:16
  91.2 0.8 copy-done.2
  92.0 0.2 copy-done.4
  92.2 18.1 %shard_map.70 = (f32[64,128,128]{2,1,0:T(8,128)}, f32[128,128]{1,0:T(8,128)}) custom-call(s32[512]{0:T(512)} %reshape.84.cols_ref, s32[1]{0:T(128)} %copy.16.count_ref, s32[32]{0:T(128)} %reshape.85.sends_ref, bf16[64,128,128]{2,1,0:T(8,128)(2,1)} %get-tuple-element.16.own_hbm, bf16[16,128,128]{2,1,0:T(8,128)(2,1)} %copy-done.2, ...), custom_call_target="tpu_custom_call" | custom-call | tf_op jit(solution)/shard_map/pallas_call | solution.py:113
  110.4 0.9 copy.13
  111.3 0.1 collective-permute-start.6
  111.4 1.2 collective-permute-done.6
  112.7 0.1 collective-permute-start.7
  112.7 4.3 %collective-permute-done.7 = f32[128,128]{0,1:T(8,128)S(1)} collective-permute-done((f32[128,128]{0,1:T(8,128)S(1)}, f32[128,128]{0,1:T(8,128)S(1)}, u32[]{:S(2)}, u32[]{:S(2)}) %collective-permute-start.7) | collective-permute-done | bytes 65568 | tf_op jit(solution)/shard_map/ppermute | solution.py:28
  117.0 0.1 collective-permute-start.8
  117.1 5.5 %collective-permute-done.8 = f32[128,128]{0,1:T(8,128)S(1)} collective-permute-done((f32[128,128]{0,1:T(8,128)S(1)}, f32[128,128]{0,1:T(8,128)S(1)}, u32[]{:S(2)}, u32[]{:S(2)}) %collective-permute-start.8) | collective-permute-done | bytes 65568 | tf_op jit(solution)/shard_map/ppermute | solution.py:28
  122.6 0.1 collective-permute-start.9
  122.7 4.3 %collective-permute-done.9 = f32[128,128]{0,1:T(8,128)S(1)} collective-permute-done((f32[128,128]{0,1:T(8,128)S(1)}, f32[128,128]{0,1:T(8,128)S(1)}, u32[]{:S(2)}, u32[]{:S(2)}) %collective-permute-start.9) | collective-permute-done | bytes 65568 | tf_op jit(solution)/shard_map/ppermute | solution.py:28
  126.9 0.1 collective-permute-start.10
  127.0 5.5 %collective-permute-done.10 = f32[128,128]{0,1:T(8,128)S(1)} collective-permute-done((f32[128,128]{0,1:T(8,128)S(1)}, f32[128,128]{0,1:T(8,128)S(1)}, u32[]{:S(2)}, u32[]{:S(2)}) %collective-permute-start.10) | collective-permute-done | bytes 65568 | tf_op jit(solution)/shard_map/ppermute | solution.py:28
  132.5 0.1 collective-permute-start.11
  132.6 4.3 %collective-permute-done.11 = f32[128,128]{0,1:T(8,128)S(1)} collective-permute-done((f32[128,128]{0,1:T(8,128)S(1)}, f32[128,128]{0,1:T(8,128)S(1)}, u32[]{:S(2)}, u32[]{:S(2)}) %collective-permute-start.11) | collective-permute-done | bytes 65568 | tf_op jit(solution)/shard_map/ppermute | solution.py:28
  136.9 2.0 %collective-permute-start.12 = (f32[128,128]{0,1:T(8,128)S(1)}, f32[128,128]{0,1:T(8,128)S(1)}, u32[]{:S(2)}, u32[]{:S(2)}) collective-permute-start(f32[128,128]{0,1:T(8,128)S(1)} %add.59), channel_id=1, source_target_pairs={{0,96},{1,97},{2,98},{3,99},{4,100},{5,101},{6,102},{7,103},{8,104... | collective-permute-start | bytes 196616 | tf_op jit(solution)/shard_map/ppermute | solution.py:28
  138.9 3.7 %collective-permute-done.12 = f32[128,128]{0,1:T(8,128)S(1)} collective-permute-done((f32[128,128]{0,1:T(8,128)S(1)}, f32[128,128]{0,1:T(8,128)S(1)}, u32[]{:S(2)}, u32[]{:S(2)}) %collective-permute-start.12) | collective-permute-done | bytes 65568 | tf_op jit(solution)/shard_map/ppermute | solution.py:28
  142.6 0.1 copy.14
  142.7 11.7 %cholesky.17 = f32[128,128]{1,0:T(8,128)S(1)} custom-call(f32[128,128]{1,0:T(8,128)S(1)} %fusion.1), custom_call_target="Cholesky" | custom-call | tf_op jit(solution)/shard_map/jit(cholesky)/cholesky | solution.py:143
  154.5 0.6 compare_reduce_fusion
  155.1 0.7 fusion.2
  155.8 0.7 copy.15
  156.5 9.8 %custom-call.6 = f32[1,128,128]{1,2,0:T(8,128)S(1)} custom-call(f32[1,128,128]{2,1,0:T(8,128)S(1)} %get-tuple-element.29), custom_call_target="InvertDiagBlocksLowerTriangular" | custom-call | tf_op jit(solution)/shard_map/triangular_solve | solution.py:144
  166.3 0.2 convolution_bitcast_fusion
  166.6 6.5 %fusion.6 = f32[64,128,128]{2,1,0:T(8,128)} fusion(f32[64,128,128]{2,1,0:T(8,128)} %get-tuple-element.20, f32[128,128,1]{1,0,2:T(8,128)S(1)} %convolution_bitcast_fusion), kind=kOutput, calls=%fused_computation.22 | convolution fusion | flops 1610612736 | bytes 8454144 | tf_op jit(solution)/shard_map/dot_general | solution.py:147
  (21 shorter events, 0.1 us)
Async XLA Ops:
  4.2 20.2 %collective-permute-start.1 = (bf16[16,128,128]{2,1,0:T(8,128)(2,1)S(1)}, bf16[16,128,128]{2,1,0:T(8,128)(2,1)S(1)}, u32[]{:S(2)}, u32[]{:S(2)}) collective-permute-start(bf16[16,128,128]{2,1,0:T(8,128)(2,1)S(1)} %gather_fusion.1), channel_id=1, source_target_pairs={{0,127},{1,0},{2,1},{3,2},{4,3},{5,4},{6,5},{7,6},{8,7},{9,8},{10,... | collective-permute-start | bytes 1572872 | tf_op jit(solution)/shard_map/ppermute | solution.py:16
  15.4 14.1 %collective-permute-start = (bf16[16,128,128]{2,1,0:T(8,128)(2,1)S(1)}, bf16[16,128,128]{2,1,0:T(8,128)(2,1)S(1)}, u32[]{:S(2)}, u32[]{:S(2)}) collective-permute-start(bf16[16,128,128]{2,1,0:T(8,128)(2,1)S(1)} %gather_fusion), channel_id=1, source_target_pairs={{0,1},{1,2},{2,3},{3,4},{4,5},{5,6},{6,7},{7,8},{8,9},{9,10},{10,1... | collective-permute-start | bytes 1572872 | tf_op jit(solution)/shard_map/ppermute | solution.py:16
  24.4 5.0 %copy-start = (bf16[16,128,128]{2,1,0:T(8,128)(2,1)}, bf16[16,128,128]{2,1,0:T(8,128)(2,1)S(1)}, u32[]{:S(2)}) copy-start(bf16[16,128,128]{2,1,0:T(8,128)(2,1)S(1)} %collective-permute-done.1.high_hbm) | copy-start | bytes 1572868
  29.5 0.8 copy-start.1
  46.0 14.3 %collective-permute-start.2 = (bf16[16,128,128]{2,1,0:T(8,128)(2,1)}, bf16[16,128,128]{2,1,0:T(8,128)(2,1)S(1)}, u32[]{:S(2)}, u32[]{:S(2)}) collective-permute-start(bf16[16,128,128]{2,1,0:T(8,128)(2,1)} %get-tuple-element.13), channel_id=1, source_target_pairs={{0,1},{1,2},{2,3},{3,4},{4,5},{5,6},{6,7},{7,8},{8,9},{9,10},{10,1... | collective-permute-start | bytes 1572872 | tf_op jit(solution)/shard_map/ppermute | solution.py:16
  46.1 14.2 %collective-permute-start.3 = (bf16[16,128,128]{2,1,0:T(8,128)(2,1)}, bf16[16,128,128]{2,1,0:T(8,128)(2,1)S(1)}, u32[]{:S(2)}, u32[]{:S(2)}) collective-permute-start(bf16[16,128,128]{2,1,0:T(8,128)(2,1)} %get-tuple-element.14), channel_id=1, source_target_pairs={{0,127},{1,0},{2,1},{3,2},{4,3},{5,4},{6,5},{7,6},{8,7},{9,8},{10,... | collective-permute-start | bytes 1572872 | tf_op jit(solution)/shard_map/ppermute | solution.py:16
  60.3 0.8 copy-start.3
  60.3 1.0 copy-start.5
  76.9 14.3 %collective-permute-start.4 = (bf16[16,128,128]{2,1,0:T(8,128)(2,1)}, bf16[16,128,128]{2,1,0:T(8,128)(2,1)S(1)}, u32[]{:S(2)}, u32[]{:S(2)}) collective-permute-start(bf16[16,128,128]{2,1,0:T(8,128)(2,1)} %get-tuple-element.17), channel_id=1, source_target_pairs={{0,1},{1,2},{2,3},{3,4},{4,5},{5,6},{6,7},{7,8},{8,9},{9,10},{10,1... | collective-permute-start | bytes 1572872 | tf_op jit(solution)/shard_map/ppermute | solution.py:16
  77.0 14.2 %collective-permute-start.5 = (bf16[16,128,128]{2,1,0:T(8,128)(2,1)}, bf16[16,128,128]{2,1,0:T(8,128)(2,1)S(1)}, u32[]{:S(2)}, u32[]{:S(2)}) collective-permute-start(bf16[16,128,128]{2,1,0:T(8,128)(2,1)} %get-tuple-element.18), channel_id=1, source_target_pairs={{0,127},{1,0},{2,1},{3,2},{4,3},{5,4},{6,5},{7,6},{8,7},{9,8},{10,... | collective-permute-start | bytes 1572872 | tf_op jit(solution)/shard_map/ppermute | solution.py:16
  91.2 0.8 copy-start.2
  91.2 1.0 copy-start.4
  111.3 1.3 collective-permute-start.6
  112.7 4.3 %collective-permute-start.7 = (f32[128,128]{0,1:T(8,128)S(1)}, f32[128,128]{0,1:T(8,128)S(1)}, u32[]{:S(2)}, u32[]{:S(2)}) collective-permute-start(f32[128,128]{0,1:T(8,128)S(1)} %add.54), channel_id=1, source_target_pairs={{0,2},{1,3},{2,0},{3,1},{4,6},{5,7},{6,4},{7,5},{8,10},{9,11},{10,... | collective-permute-start | bytes 196616 | tf_op jit(solution)/shard_map/ppermute | solution.py:28
  117.0 5.6 %collective-permute-start.8 = (f32[128,128]{0,1:T(8,128)S(1)}, f32[128,128]{0,1:T(8,128)S(1)}, u32[]{:S(2)}, u32[]{:S(2)}) collective-permute-start(f32[128,128]{0,1:T(8,128)S(1)} %add.55), channel_id=1, source_target_pairs={{0,6},{1,7},{2,4},{3,5},{4,2},{5,3},{6,0},{7,1},{8,14},{9,15},{10,... | collective-permute-start | bytes 196616 | tf_op jit(solution)/shard_map/ppermute | solution.py:28
  122.6 4.3 %collective-permute-start.9 = (f32[128,128]{0,1:T(8,128)S(1)}, f32[128,128]{0,1:T(8,128)S(1)}, u32[]{:S(2)}, u32[]{:S(2)}) collective-permute-start(f32[128,128]{0,1:T(8,128)S(1)} %add.56), channel_id=1, source_target_pairs={{0,8},{1,9},{2,10},{3,11},{4,12},{5,13},{6,14},{7,15},{8,0},{9,1},... | collective-permute-start | bytes 196616 | tf_op jit(solution)/shard_map/ppermute | solution.py:28
  126.9 5.6 %collective-permute-start.10 = (f32[128,128]{0,1:T(8,128)S(1)}, f32[128,128]{0,1:T(8,128)S(1)}, u32[]{:S(2)}, u32[]{:S(2)}) collective-permute-start(f32[128,128]{0,1:T(8,128)S(1)} %add.57), channel_id=1, source_target_pairs={{0,24},{1,25},{2,26},{3,27},{4,28},{5,29},{6,30},{7,31},{8,16},{9,... | collective-permute-start | bytes 196616 | tf_op jit(solution)/shard_map/ppermute | solution.py:28
  132.5 4.3 %collective-permute-start.11 = (f32[128,128]{0,1:T(8,128)S(1)}, f32[128,128]{0,1:T(8,128)S(1)}, u32[]{:S(2)}, u32[]{:S(2)}) collective-permute-start(f32[128,128]{0,1:T(8,128)S(1)} %add.58), channel_id=1, source_target_pairs={{0,32},{1,33},{2,34},{3,35},{4,36},{5,37},{6,38},{7,39},{8,40},{9,... | collective-permute-start | bytes 196616 | tf_op jit(solution)/shard_map/ppermute | solution.py:28
  136.9 5.7 %collective-permute-start.12 = (f32[128,128]{0,1:T(8,128)S(1)}, f32[128,128]{0,1:T(8,128)S(1)}, u32[]{:S(2)}, u32[]{:S(2)}) collective-permute-start(f32[128,128]{0,1:T(8,128)S(1)} %add.59), channel_id=1, source_target_pairs={{0,96},{1,97},{2,98},{3,99},{4,100},{5,101},{6,102},{7,103},{8,104... | collective-permute-start | bytes 196616 | tf_op jit(solution)/shard_map/ppermute | solution.py:28

commit v7 on v6

--- a/solution.py
+++ b/solution.py
@@ -27,6 +27,37 @@
         partner = [(i, i ^ mask) for i in range(length)]
         value = value + lax.ppermute(value, axis, partner)
     return value
+
+
+def pick_kernel(sends_ref, tangent_hbm, to_lower_ref, to_upper_ref, buf, sems):
+    rows = buf.shape[0]
+    half = rows // 2
+    copies = [pltpu.make_async_copy(tangent_hbm.at[sends_ref[j]], buf.at[j], sems.at[j]) for j in range(rows)]
+    for copy in copies:
+        copy.start()
+    for j in range(rows):
+        copies[j].wait()
+        if j < half:
+            to_lower_ref[j] = buf[j].astype(jnp.bfloat16)
+        else:
+            to_upper_ref[j - half] = buf[j].astype(jnp.bfloat16)
+
+
+def pick_rows(sends, tangent):
+    rows = sends.shape[0]
+    slots, width, vectors = tangent.shape
+    grid_spec = pltpu.PrefetchScalarGridSpec(
+        num_scalar_prefetch=1,
+        grid=(),
+        in_specs=[pl.BlockSpec(memory_space=pl.ANY)],
+        out_specs=[pl.BlockSpec(memory_space=pltpu.VMEM)] * 2,
+        scratch_shapes=[pltpu.VMEM((rows, width, vectors), jnp.float32), pltpu.SemaphoreType.DMA((rows,))],
+    )
+    return pl.pallas_call(
+        pick_kernel,
+        grid_spec=grid_spec,
+        out_shape=[jax.ShapeDtypeStruct((rows // 2, width, vectors), jnp.bfloat16)] * 2,
+    )(sends, tangent)
 
 
 def substep_kernel(cols_ref, count_ref, sends_ref, own_hbm, low_hbm, high_hbm, blocks_ref, state_ref,
@@ -129,8 +160,7 @@
     rounded = state.astype(jnp.bfloat16)
     cols = columns.reshape(-1)
     sends = send_lists.reshape(-1)
-    to_lower = tangent[send_lists[0, 0]].astype(jnp.bfloat16)
-    to_upper = tangent[send_lists[0, 1]].astype(jnp.bfloat16)
+    to_lower, to_upper = pick_rows(sends, tangent)
     for step in range(SUBSTEPS):
         from_lower = passed_along(to_upper, "grains", 1)
         from_upper = passed_along(to_lower, "grains", -1)

time: 174 us -> 165 us (0.948)
  local copies, waits for them, and re-layouts: 12.9 us -> 6.77 us
  waiting for transfers between devices: 47.8 us -> 42.8 us
  Pallas kernels: 49.5 us -> 53 us
    gather x2 -> x0, local copies, waits for them, and re-layouts: 5.64 us -> none  [the longest x1 2.82 us: local(): to_lower = tangent[send_lists[0, 0]].astype(jnp.bfloat16)]
    ppermute x6, waiting for transfers between devices: 19.2 us -> 14.2 us  [passed_along(): lax.ppermute(shard, axis, [(i, (i + by) % length) for i in range(length)])]
    pallas_call x0 -> x1, Pallas kernels: none -> 3.49 us  [pick_rows(): pl.pallas_call(pick_kernel, grid_spec=grid_spec, out_shape=[jax.ShapeDtyp...]
    unnamed x14 -> x16, local copies, waits for them, and re-layouts: 4.25 us -> 3.77 us
  transfers between devices with their start and end apart: 13 -> 13, of which waited for: 10 -> 10; matrix products, arithmetic and copies ran while one was open for 6% -> 4% of each run, Pallas kernels for 0% -> 0%
where the time goes in v7:
time: 165 us
  Pallas kernels  53 us (32%)
  waiting for transfers between devices  42.8 us (26%)
  other arithmetic  28.5 us (17%)
  starting transfers between devices  25.4 us (15%)
  matrix products  6.8 us (4%)
  local copies, waits for them, and re-layouts  6.77 us (4%)
    pallas_call x3, Pallas kernels, substep(): pl.pallas_call(kernel, grid_spec=grid_spec, out_shape=[jax.ShapeDtypeStru...  49.5 us
    ppermute x7, waiting for transfers between devices, tree_sum(): value = value + lax.ppermute(value, axis, partner)  28.6 us
    ppermute x6, starting transfers between devices, passed_along(): lax.ppermute(shard, axis, [(i, (i + by) % length) for i in range(length)])  22.8 us
    ppermute x6, waiting for transfers between devices, passed_along(): lax.ppermute(shard, axis, [(i, (i + by) % length) for i in range(length)])  14.2 us
    another operation x3, other arithmetic, local(): first_low = jnp.linalg.cholesky(tree_sum(gram, 'grains'))  12.4 us
    another operation x1, other arithmetic, local(): lax.linalg.triangular_solve(first_low, jnp.eye(vectors, dtype=jnp.float32...  9.81 us
    dot_general x1, matrix products, local(): basis = jnp.dot(flat, inverse.T, precision=lax.Precision.HIGHEST)  6.55 us
    convert_element_type x1, other arithmetic, local(): rounded = state.astype(jnp.bfloat16)  5.53 us
  transfers between devices with their start and end apart: 13, of which 10 were waited for; matrix products, arithmetic and copies ran while one was open for 4% of the time, Pallas kernels for 0%

profile of v7, /device:TPU:0, one launch (start us, length us, event | category | flops | bytes accessed | tf_op | source)
XLA Modules:
  0.0 164.7 jit_solution(9799546457452206616)
XLA Ops:
  0.6 1.4 reshape.29.sends_ref
  2.0 3.5 %shard_map.68 = (bf16[16,128,128]{2,1,0:T(8,128)(2,1)}, bf16[16,128,128]{2,1,0:T(8,128)(2,1)}) custom-call(s32[32]{0:T(128)} %reshape.29.sends_ref, f32[64,128,128]{2,1,0:T(8,128)} %tangent_hbm.1), custom_call_target="tpu_custom_call" | custom-call | tf_op jit(solution)/shard_map/pallas_call | solution.py:56
  5.5 0.1 collective-permute-start
  5.6 8.3 %collective-permute-start.1 = (bf16[16,128,128]{2,1,0:T(8,128)(2,1)}, bf16[16,128,128]{2,1,0:T(8,128)(2,1)S(1)}, u32[]{:S(2)}, u32[]{:S(2)}) collective-permute-start(bf16[16,128,128]{2,1,0:T(8,128)(2,1)} %get-tuple-element.15), channel_id=1, source_target_pairs={{0,127},{1,0},{2,1},{3,2},{4,3},{5,4},{6,5},{7,6},{8,7},{9,8},{10,... | collective-permute-start | bytes 1572872 | tf_op jit(solution)/shard_map/ppermute | solution.py:16
  14.5 0.1 copy.11
  14.6 0.6 reshape.28.cols_ref
  15.3 5.5 %fusion.3 = (bf16[64,128,128]{2,1,0:T(8,128)(2,1)}, f32[64,128,128]{2,1,0:T(8,128)}) fusion(f32[64,128,128]{2,1,0:T(8,128)} %tangent_hbm.1, f32[64]{0:T(128)S(1)} %compare_convert_fusion), kind=kLoop, calls=%fused_computation.13 | loop fusion | flops 2097152 | bytes 10486016 | tf_op jit(solution)/shard_map/convert_element_type | solution.py:160
  20.8 0.1 collective-permute-done.low_hbm
  20.9 0.0 collective-permute-done.1.high_hbm
  20.9 0.8 copy-done
  21.7 0.1 copy-done.1
  21.9 15.7 %shard_map.69 = (f32[64,128,128]{2,1,0:T(8,128)}, bf16[64,128,128]{2,1,0:T(8,128)(2,1)}, bf16[16,128,128]{2,1,0:T(8,128)(2,1)}, bf16[16,128,128]{2,1,0:T(8,128)(2,1)}) custom-call(s32[512]{0:T(512)} %reshape.28.cols_ref, s32[1]{0:T(128)} %copy.16.count_ref, s32[32]{0:T(128)} %reshape.29.sends_ref, bf16[64,128,128]{2,1,0:T(8,128)(2,1)} %get-tuple-element.30.own_hbm, ...), custom_call_target="tpu_custom_call" | custom-call | tf_op jit(solution)/shard_map/pallas_call | solution.py:144
  37.5 0.1 collective-permute-start.2
  37.6 7.2 %collective-permute-start.3 = (bf16[16,128,128]{2,1,0:T(8,128)(2,1)}, bf16[16,128,128]{2,1,0:T(8,128)(2,1)S(1)}, u32[]{:S(2)}, u32[]{:S(2)}) collective-permute-start(bf16[16,128,128]{2,1,0:T(8,128)(2,1)} %get-tuple-element.18), channel_id=1, source_target_pairs={{0,127},{1,0},{2,1},{3,2},{4,3},{5,4},{6,5},{7,6},{8,7},{9,8},{10,... | collective-permute-start | bytes 1572872 | tf_op jit(solution)/shard_map/ppermute | solution.py:16
  44.8 7.1 %collective-permute-done.2.low_hbm = bf16[16,128,128]{2,1,0:T(8,128)(2,1)S(1)} collective-permute-done((bf16[16,128,128]{2,1,0:T(8,128)(2,1)}, bf16[16,128,128]{2,1,0:T(8,128)(2,1)S(1)}, u32[]{:S(2)}, u32[]{:S(2)}) %collective-permute-start.2) | collective-permute-done | bytes 524320 | tf_op jit(solution)/shard_map/ppermute | solution.py:16
  51.9 0.0 collective-permute-done.3.high_hbm
  51.9 0.9 copy-done.3
  52.7 0.1 copy-done.5
  52.9 15.7 %shard_map.70 = (f32[64,128,128]{2,1,0:T(8,128)}, bf16[64,128,128]{2,1,0:T(8,128)(2,1)}, bf16[16,128,128]{2,1,0:T(8,128)(2,1)}, bf16[16,128,128]{2,1,0:T(8,128)(2,1)}) custom-call(s32[512]{0:T(512)} %reshape.28.cols_ref, s32[1]{0:T(128)} %copy.16.count_ref, s32[32]{0:T(128)} %reshape.29.sends_ref, bf16[64,128,128]{2,1,0:T(8,128)(2,1)} %get-tuple-element.16.own_hbm, ...), custom_call_target="tpu_custom_call" | custom-call | tf_op jit(solution)/shard_map/pallas_call | solution.py:144
  68.5 0.1 collective-permute-start.4
  68.6 7.2 %collective-permute-start.5 = (bf16[16,128,128]{2,1,0:T(8,128)(2,1)}, bf16[16,128,128]{2,1,0:T(8,128)(2,1)S(1)}, u32[]{:S(2)}, u32[]{:S(2)}) collective-permute-start(bf16[16,128,128]{2,1,0:T(8,128)(2,1)} %get-tuple-element.22), channel_id=1, source_target_pairs={{0,127},{1,0},{2,1},{3,2},{4,3},{5,4},{6,5},{7,6},{8,7},{9,8},{10,... | collective-permute-start | bytes 1572872 | tf_op jit(solution)/shard_map/ppermute | solution.py:16
  75.8 7.1 %collective-permute-done.4.low_hbm = bf16[16,128,128]{2,1,0:T(8,128)(2,1)S(1)} collective-permute-done((bf16[16,128,128]{2,1,0:T(8,128)(2,1)}, bf16[16,128,128]{2,1,0:T(8,128)(2,1)S(1)}, u32[]{:S(2)}, u32[]{:S(2)}) %collective-permute-start.4) | collective-permute-done | bytes 524320 | tf_op jit(solution)/shard_map/ppermute | solution.py:16
  82.8 0.8 copy-done.2
  83.6 0.2 copy-done.4
  83.8 18.1 %shard_map.71 = (f32[64,128,128]{2,1,0:T(8,128)}, f32[128,128]{1,0:T(8,128)}) custom-call(s32[512]{0:T(512)} %reshape.28.cols_ref, s32[1]{0:T(128)} %copy.16.count_ref, s32[32]{0:T(128)} %reshape.29.sends_ref, bf16[64,128,128]{2,1,0:T(8,128)(2,1)} %get-tuple-element.20.own_hbm, bf16[16,128,128]{2,1,0:T(8,128)(2,1)} %copy-done.2, ...), custom_call_target="tpu_custom_call" | custom-call | tf_op jit(solution)/shard_map/pallas_call | solution.py:144
  102.0 0.9 copy.13
  102.9 0.1 collective-permute-start.6
  103.0 1.2 collective-permute-done.6
  104.3 0.1 collective-permute-start.7
  104.3 4.3 %collective-permute-done.7 = f32[128,128]{0,1:T(8,128)S(1)} collective-permute-done((f32[128,128]{0,1:T(8,128)S(1)}, f32[128,128]{0,1:T(8,128)S(1)}, u32[]{:S(2)}, u32[]{:S(2)}) %collective-permute-start.7) | collective-permute-done | bytes 65568 | tf_op jit(solution)/shard_map/ppermute | solution.py:28
  108.6 0.1 collective-permute-start.8
  108.7 5.5 %collective-permute-done.8 = f32[128,128]{0,1:T(8,128)S(1)} collective-permute-done((f32[128,128]{0,1:T(8,128)S(1)}, f32[128,128]{0,1:T(8,128)S(1)}, u32[]{:S(2)}, u32[]{:S(2)}) %collective-permute-start.8) | collective-permute-done | bytes 65568 | tf_op jit(solution)/shard_map/ppermute | solution.py:28
  114.2 0.1 collective-permute-start.9
  114.3 4.3 %collective-permute-done.9 = f32[128,128]{0,1:T(8,128)S(1)} collective-permute-done((f32[128,128]{0,1:T(8,128)S(1)}, f32[128,128]{0,1:T(8,128)S(1)}, u32[]{:S(2)}, u32[]{:S(2)}) %collective-permute-start.9) | collective-permute-done | bytes 65568 | tf_op jit(solution)/shard_map/ppermute | solution.py:28
  118.5 0.1 collective-permute-start.10
  118.6 5.5 %collective-permute-done.10 = f32[128,128]{0,1:T(8,128)S(1)} collective-permute-done((f32[128,128]{0,1:T(8,128)S(1)}, f32[128,128]{0,1:T(8,128)S(1)}, u32[]{:S(2)}, u32[]{:S(2)}) %collective-permute-start.10) | collective-permute-done | bytes 65568 | tf_op jit(solution)/shard_map/ppermute | solution.py:28
  124.1 0.1 collective-permute-start.11
  124.2 4.3 %collective-permute-done.11 = f32[128,128]{0,1:T(8,128)S(1)} collective-permute-done((f32[128,128]{0,1:T(8,128)S(1)}, f32[128,128]{0,1:T(8,128)S(1)}, u32[]{:S(2)}, u32[]{:S(2)}) %collective-permute-start.11) | collective-permute-done | bytes 65568 | tf_op jit(solution)/shard_map/ppermute | solution.py:28
  128.5 2.1 %collective-permute-start.12 = (f32[128,128]{0,1:T(8,128)S(1)}, f32[128,128]{0,1:T(8,128)S(1)}, u32[]{:S(2)}, u32[]{:S(2)}) collective-permute-start(f32[128,128]{0,1:T(8,128)S(1)} %add.37), channel_id=1, source_target_pairs={{0,96},{1,97},{2,98},{3,99},{4,100},{5,101},{6,102},{7,103},{8,104... | collective-permute-start | bytes 196616 | tf_op jit(solution)/shard_map/ppermute | solution.py:28
  130.5 3.7 %collective-permute-done.12 = f32[128,128]{0,1:T(8,128)S(1)} collective-permute-done((f32[128,128]{0,1:T(8,128)S(1)}, f32[128,128]{0,1:T(8,128)S(1)}, u32[]{:S(2)}, u32[]{:S(2)}) %collective-permute-start.12) | collective-permute-done | bytes 65568 | tf_op jit(solution)/shard_map/ppermute | solution.py:28
  134.2 0.1 copy.14
  134.3 11.7 %cholesky.17 = f32[128,128]{1,0:T(8,128)S(1)} custom-call(f32[128,128]{1,0:T(8,128)S(1)} %fusion.1), custom_call_target="Cholesky" | custom-call | tf_op jit(solution)/shard_map/jit(cholesky)/cholesky | solution.py:173
  146.1 0.6 compare_reduce_fusion
  146.7 0.7 fusion.2
  147.4 0.7 copy.15
  148.1 9.8 %custom-call.6 = f32[1,128,128]{1,2,0:T(8,128)S(1)} custom-call(f32[1,128,128]{2,1,0:T(8,128)S(1)} %get-tuple-element.33), custom_call_target="InvertDiagBlocksLowerTriangular" | custom-call | tf_op jit(solution)/shard_map/triangular_solve | solution.py:174
  157.9 0.2 convolution_bitcast_fusion
  158.2 6.5 %fusion.4 = f32[64,128,128]{2,1,0:T(8,128)} fusion(f32[64,128,128]{2,1,0:T(8,128)} %get-tuple-element.24, f32[128,128,1]{1,0,2:T(8,128)S(1)} %convolution_bitcast_fusion), kind=kOutput, calls=%fused_computation.14 | convolution fusion | flops 1610612736 | bytes 8454144 | tf_op jit(solution)/shard_map/dot_general | solution.py:177
  (19 shorter events, 0.1 us)
Async XLA Ops:
  0.6 13.9 %copy-start.6 = (s32[64,8]{0,1:T(8,128)S(1)}, s32[64,8]{0,1:T(8,128)}, u32[]{:S(2)}) copy-start(s32[64,8]{0,1:T(8,128)} %param.7) | copy-start | bytes 6148
  5.5 15.4 %collective-permute-start = (bf16[16,128,128]{2,1,0:T(8,128)(2,1)}, bf16[16,128,128]{2,1,0:T(8,128)(2,1)S(1)}, u32[]{:S(2)}, u32[]{:S(2)}) collective-permute-start(bf16[16,128,128]{2,1,0:T(8,128)(2,1)} %get-tuple-element.14), channel_id=1, source_target_pairs={{0,1},{1,2},{2,3},{3,4},{4,5},{5,6},{6,7},{7,8},{8,9},{9,10},{10,1... | collective-permute-start | bytes 1572872 | tf_op jit(solution)/shard_map/ppermute | solution.py:16
  5.6 15.3 %collective-permute-start.1 = (bf16[16,128,128]{2,1,0:T(8,128)(2,1)}, bf16[16,128,128]{2,1,0:T(8,128)(2,1)S(1)}, u32[]{:S(2)}, u32[]{:S(2)}) collective-permute-start(bf16[16,128,128]{2,1,0:T(8,128)(2,1)} %get-tuple-element.15), channel_id=1, source_target_pairs={{0,127},{1,0},{2,1},{3,2},{4,3},{5,4},{6,5},{7,6},{8,7},{9,8},{10,... | collective-permute-start | bytes 1572872 | tf_op jit(solution)/shard_map/ppermute | solution.py:16
  20.9 0.9 copy-start
  20.9 1.0 copy-start.1
  37.5 14.3 %collective-permute-start.2 = (bf16[16,128,128]{2,1,0:T(8,128)(2,1)}, bf16[16,128,128]{2,1,0:T(8,128)(2,1)S(1)}, u32[]{:S(2)}, u32[]{:S(2)}) collective-permute-start(bf16[16,128,128]{2,1,0:T(8,128)(2,1)} %get-tuple-element.17), channel_id=1, source_target_pairs={{0,1},{1,2},{2,3},{3,4},{4,5},{5,6},{6,7},{7,8},{8,9},{9,10},{10,1... | collective-permute-start | bytes 1572872 | tf_op jit(solution)/shard_map/ppermute | solution.py:16
  37.6 14.2 %collective-permute-start.3 = (bf16[16,128,128]{2,1,0:T(8,128)(2,1)}, bf16[16,128,128]{2,1,0:T(8,128)(2,1)S(1)}, u32[]{:S(2)}, u32[]{:S(2)}) collective-permute-start(bf16[16,128,128]{2,1,0:T(8,128)(2,1)} %get-tuple-element.18), channel_id=1, source_target_pairs={{0,127},{1,0},{2,1},{3,2},{4,3},{5,4},{6,5},{7,6},{8,7},{9,8},{10,... | collective-permute-start | bytes 1572872 | tf_op jit(solution)/shard_map/ppermute | solution.py:16
  51.9 0.9 copy-start.3
  51.9 1.0 copy-start.5
  68.5 14.3 %collective-permute-start.4 = (bf16[16,128,128]{2,1,0:T(8,128)(2,1)}, bf16[16,128,128]{2,1,0:T(8,128)(2,1)S(1)}, u32[]{:S(2)}, u32[]{:S(2)}) collective-permute-start(bf16[16,128,128]{2,1,0:T(8,128)(2,1)} %get-tuple-element.21), channel_id=1, source_target_pairs={{0,1},{1,2},{2,3},{3,4},{4,5},{5,6},{6,7},{7,8},{8,9},{9,10},{10,1... | collective-permute-start | bytes 1572872 | tf_op jit(solution)/shard_map/ppermute | solution.py:16
  68.6 14.2 %collective-permute-start.5 = (bf16[16,128,128]{2,1,0:T(8,128)(2,1)}, bf16[16,128,128]{2,1,0:T(8,128)(2,1)S(1)}, u32[]{:S(2)}, u32[]{:S(2)}) collective-permute-start(bf16[16,128,128]{2,1,0:T(8,128)(2,1)} %get-tuple-element.22), channel_id=1, source_target_pairs={{0,127},{1,0},{2,1},{3,2},{4,3},{5,4},{6,5},{7,6},{8,7},{9,8},{10,... | collective-permute-start | bytes 1572872 | tf_op jit(solution)/shard_map/ppermute | solution.py:16
  82.8 0.8 copy-start.2
  82.8 1.0 copy-start.4
  102.9 1.3 collective-permute-start.6
  104.3 4.3 %collective-permute-start.7 = (f32[128,128]{0,1:T(8,128)S(1)}, f32[128,128]{0,1:T(8,128)S(1)}, u32[]{:S(2)}, u32[]{:S(2)}) collective-permute-start(f32[128,128]{0,1:T(8,128)S(1)} %add.32), channel_id=1, source_target_pairs={{0,2},{1,3},{2,0},{3,1},{4,6},{5,7},{6,4},{7,5},{8,10},{9,11},{10,... | collective-permute-start | bytes 196616 | tf_op jit(solution)/shard_map/ppermute | solution.py:28
  108.6 5.6 %collective-permute-start.8 = (f32[128,128]{0,1:T(8,128)S(1)}, f32[128,128]{0,1:T(8,128)S(1)}, u32[]{:S(2)}, u32[]{:S(2)}) collective-permute-start(f32[128,128]{0,1:T(8,128)S(1)} %add.33), channel_id=1, source_target_pairs={{0,6},{1,7},{2,4},{3,5},{4,2},{5,3},{6,0},{7,1},{8,14},{9,15},{10,... | collective-permute-start | bytes 196616 | tf_op jit(solution)/shard_map/ppermute | solution.py:28
  114.2 4.3 %collective-permute-start.9 = (f32[128,128]{0,1:T(8,128)S(1)}, f32[128,128]{0,1:T(8,128)S(1)}, u32[]{:S(2)}, u32[]{:S(2)}) collective-permute-start(f32[128,128]{0,1:T(8,128)S(1)} %add.34), channel_id=1, source_target_pairs={{0,8},{1,9},{2,10},{3,11},{4,12},{5,13},{6,14},{7,15},{8,0},{9,1},... | collective-permute-start | bytes 196616 | tf_op jit(solution)/shard_map/ppermute | solution.py:28
  118.5 5.6 %collective-permute-start.10 = (f32[128,128]{0,1:T(8,128)S(1)}, f32[128,128]{0,1:T(8,128)S(1)}, u32[]{:S(2)}, u32[]{:S(2)}) collective-permute-start(f32[128,128]{0,1:T(8,128)S(1)} %add.35), channel_id=1, source_target_pairs={{0,24},{1,25},{2,26},{3,27},{4,28},{5,29},{6,30},{7,31},{8,16},{9,... | collective-permute-start | bytes 196616 | tf_op jit(solution)/shard_map/ppermute | solution.py:28
  124.1 4.3 %collective-permute-start.11 = (f32[128,128]{0,1:T(8,128)S(1)}, f32[128,128]{0,1:T(8,128)S(1)}, u32[]{:S(2)}, u32[]{:S(2)}) collective-permute-start(f32[128,128]{0,1:T(8,128)S(1)} %add.36), channel_id=1, source_target_pairs={{0,32},{1,33},{2,34},{3,35},{4,36},{5,37},{6,38},{7,39},{8,40},{9,... | collective-permute-start | bytes 196616 | tf_op jit(solution)/shard_map/ppermute | solution.py:28
  128.5 5.7 %collective-permute-start.12 = (f32[128,128]{0,1:T(8,128)S(1)}, f32[128,128]{0,1:T(8,128)S(1)}, u32[]{:S(2)}, u32[]{:S(2)}) collective-permute-start(f32[128,128]{0,1:T(8,128)S(1)} %add.37), channel_id=1, source_target_pairs={{0,96},{1,97},{2,98},{3,99},{4,100},{5,101},{6,102},{7,103},{8,104... | collective-permute-start | bytes 196616 | tf_op jit(solution)/shard_map/ppermute | solution.py:28

commit v8 on v7

--- a/solution.py
+++ b/solution.py
@@ -32,7 +32,8 @@
 def pick_kernel(sends_ref, tangent_hbm, to_lower_ref, to_upper_ref, buf, sems):
     rows = buf.shape[0]
     half = rows // 2
-    copies = [pltpu.make_async_copy(tangent_hbm.at[sends_ref[j]], buf.at[j], sems.at[j]) for j in range(rows)]
+    copies = [pltpu.make_async_copy(tangent_hbm.at[sends_ref[0, j // half, j % half]], buf.at[j], sems.at[j])
+              for j in range(rows)]
     for copy in copies:
         copy.start()
     for j in range(rows):
@@ -44,7 +45,7 @@
 
 
 def pick_rows(sends, tangent):
-    rows = sends.shape[0]
+    rows = sends.shape[1] * sends.shape[2]
     slots, width, vectors = tangent.shape
     grid_spec = pltpu.PrefetchScalarGridSpec(
         num_scalar_prefetch=1,
@@ -87,7 +88,7 @@
         row = step * per_step + r
         acc = jnp.zeros(state_ref.shape[1:], jnp.float32)
         for k in range(nnz):
-            col = cols_ref[row * nnz + k]
+            col = cols_ref[row, k]
             acc = acc + jnp.dot(blocks_ref[r, k], extended[col], preferred_element_type=jnp.float32)
         new = state_ref[r] + jnp.where(row < count, acc, 0.0)
         new_state_ref[r] = new
@@ -105,7 +106,7 @@
         return
     half = to_lower_ref.shape[0]
     for j in range(2 * half):
-        local = sends_ref[j] - step * per_step
+        local = sends_ref[0, j // half, j % half] - step * per_step
 
         @pl.when((local >= 0) & (local < per_step))
         def _():
@@ -158,8 +159,8 @@
     live = (jnp.arange(slots, dtype=jnp.int32) < counts[0]).astype(jnp.float32)[:, None, None]
     state = tangent * live
     rounded = state.astype(jnp.bfloat16)
-    cols = columns.reshape(-1)
-    sends = send_lists.reshape(-1)
+    cols = columns
+    sends = send_lists
     to_lower, to_upper = pick_rows(sends, tangent)
     for step in range(SUBSTEPS):
         from_lower = passed_along(to_upper, "grains", 1)

time: 165 us -> 166 us (level)
  Pallas kernels: 53 us -> 54.7 us
    reshape x2 -> x0, local copies, waits for them, and re-layouts: 1.98 us -> none  [the longest x1 1.35 us: local(): sends = send_lists.reshape(-1)]
where the time goes in v8:
time: 166 us; the launch traced here: 165 us
  Pallas kernels  54.7 us (33%)
  waiting for transfers between devices  42.9 us (26%)
  other arithmetic  28.5 us (17%)
  starting transfers between devices  25.4 us (15%)
  matrix products  6.8 us (4%)
  local copies, waits for them, and re-layouts  5.45 us (3%)
    pallas_call x3, Pallas kernels, substep(): pl.pallas_call(kernel, grid_spec=grid_spec, out_shape=[jax.ShapeDtypeStru...  51.1 us
    ppermute x7, waiting for transfers between devices, tree_sum(): value = value + lax.ppermute(value, axis, partner)  28.7 us
    ppermute x6, starting transfers between devices, passed_along(): lax.ppermute(shard, axis, [(i, (i + by) % length) for i in range(length)])  22.8 us
    ppermute x6, waiting for transfers between devices, passed_along(): lax.ppermute(shard, axis, [(i, (i + by) % length) for i in range(length)])  14.3 us
    another operation x3, other arithmetic, local(): first_low = jnp.linalg.cholesky(tree_sum(gram, 'grains'))  12.4 us
    another operation x1, other arithmetic, local(): lax.linalg.triangular_solve(first_low, jnp.eye(vectors, dtype=jnp.float32...  9.81 us
    dot_general x1, matrix products, local(): basis = jnp.dot(flat, inverse.T, precision=lax.Precision.HIGHEST)  6.55 us
    convert_element_type x1, other arithmetic, local(): rounded = state.astype(jnp.bfloat16)  5.53 us
  transfers between devices with their start and end apart: 13, of which 10 were waited for; matrix products, arithmetic and copies ran while one was open for 4% of the time, Pallas kernels for 0%

profile of v8, /device:TPU:0, one launch (start us, length us, event | category | flops | bytes accessed | tf_op | source)
XLA Modules:
  0.0 165.2 jit_solution(9553056964938045606)
XLA Ops:
  0.6 0.0 copy-start.6
  0.6 3.7 %shard_map.68 = (bf16[16,128,128]{2,1,0:T(8,128)(2,1)}, bf16[16,128,128]{2,1,0:T(8,128)(2,1)}) custom-call(s32[1,2,16]{2,1,0:T(2,128)} %sends_ref.7, f32[64,128,128]{2,1,0:T(8,128)} %tangent_hbm.1), custom_call_target="tpu_custom_call" | custom-call | tf_op jit(solution)/shard_map/pallas_call | solution.py:57
  4.3 0.1 collective-permute-start
  4.4 8.3 %collective-permute-start.1 = (bf16[16,128,128]{2,1,0:T(8,128)(2,1)}, bf16[16,128,128]{2,1,0:T(8,128)(2,1)S(1)}, u32[]{:S(2)}, u32[]{:S(2)}) collective-permute-start(bf16[16,128,128]{2,1,0:T(8,128)(2,1)} %get-tuple-element.15), channel_id=1, source_target_pairs={{0,127},{1,0},{2,1},{3,2},{4,3},{5,4},{6,5},{7,6},{8,7},{9,8},{10,... | collective-permute-start | bytes 1572872 | tf_op jit(solution)/shard_map/ppermute | solution.py:16
  13.4 0.7 copy.9.cols_ref
  14.1 5.5 %fusion.3 = (bf16[64,128,128]{2,1,0:T(8,128)(2,1)}, f32[64,128,128]{2,1,0:T(8,128)}) fusion(f32[64,128,128]{2,1,0:T(8,128)} %tangent_hbm.1, f32[64]{0:T(128)S(1)} %compare_convert_fusion), kind=kLoop, calls=%fused_computation.13 | loop fusion | flops 2097152 | bytes 10486016 | tf_op jit(solution)/shard_map/convert_element_type | solution.py:161
  19.6 0.1 collective-permute-done.low_hbm
  19.7 0.0 collective-permute-done.1.high_hbm
  19.7 0.8 copy-done
  20.5 0.1 copy-done.1
  20.7 16.2 %shard_map.69 = (f32[64,128,128]{2,1,0:T(8,128)}, bf16[64,128,128]{2,1,0:T(8,128)(2,1)}, bf16[16,128,128]{2,1,0:T(8,128)(2,1)}, bf16[16,128,128]{2,1,0:T(8,128)(2,1)}) custom-call(s32[64,8]{1,0:T(8,128)} %copy.9.cols_ref, s32[1]{0:T(128)} %copy.14.count_ref, s32[1,2,16]{2,1,0:T(2,128)} %sends_ref.7, bf16[64,128,128]{2,1,0:T(8,128)(2,1)} %get-tuple-element.28.own_hbm, ...), custom_call_target="tpu_custom_call" | custom-call | tf_op jit(solution)/shard_map/pallas_call | solution.py:145
  36.9 0.1 collective-permute-start.2
  37.0 7.2 %collective-permute-start.3 = (bf16[16,128,128]{2,1,0:T(8,128)(2,1)}, bf16[16,128,128]{2,1,0:T(8,128)(2,1)S(1)}, u32[]{:S(2)}, u32[]{:S(2)}) collective-permute-start(bf16[16,128,128]{2,1,0:T(8,128)(2,1)} %get-tuple-element.18), channel_id=1, source_target_pairs={{0,127},{1,0},{2,1},{3,2},{4,3},{5,4},{6,5},{7,6},{8,7},{9,8},{10,... | collective-permute-start | bytes 1572872 | tf_op jit(solution)/shard_map/ppermute | solution.py:16
  44.1 7.1 %collective-permute-done.2.low_hbm = bf16[16,128,128]{2,1,0:T(8,128)(2,1)S(1)} collective-permute-done((bf16[16,128,128]{2,1,0:T(8,128)(2,1)}, bf16[16,128,128]{2,1,0:T(8,128)(2,1)S(1)}, u32[]{:S(2)}, u32[]{:S(2)}) %collective-permute-start.2) | collective-permute-done | bytes 524320 | tf_op jit(solution)/shard_map/ppermute | solution.py:16
  51.2 0.0 collective-permute-done.3.high_hbm
  51.2 0.9 copy-done.2
  52.1 0.1 copy-done.4
  52.2 16.2 %shard_map.70 = (f32[64,128,128]{2,1,0:T(8,128)}, bf16[64,128,128]{2,1,0:T(8,128)(2,1)}, bf16[16,128,128]{2,1,0:T(8,128)(2,1)}, bf16[16,128,128]{2,1,0:T(8,128)(2,1)}) custom-call(s32[64,8]{1,0:T(8,128)} %copy.9.cols_ref, s32[1]{0:T(128)} %copy.14.count_ref, s32[1,2,16]{2,1,0:T(2,128)} %sends_ref.7, bf16[64,128,128]{2,1,0:T(8,128)(2,1)} %get-tuple-element.16.own_hbm, ...), custom_call_target="tpu_custom_call" | custom-call | tf_op jit(solution)/shard_map/pallas_call | solution.py:145
  68.4 0.1 collective-permute-start.4
  68.5 7.2 %collective-permute-start.5 = (bf16[16,128,128]{2,1,0:T(8,128)(2,1)}, bf16[16,128,128]{2,1,0:T(8,128)(2,1)S(1)}, u32[]{:S(2)}, u32[]{:S(2)}) collective-permute-start(bf16[16,128,128]{2,1,0:T(8,128)(2,1)} %get-tuple-element.22), channel_id=1, source_target_pairs={{0,127},{1,0},{2,1},{3,2},{4,3},{5,4},{6,5},{7,6},{8,7},{9,8},{10,... | collective-permute-start | bytes 1572872 | tf_op jit(solution)/shard_map/ppermute | solution.py:16
  75.6 7.1 %collective-permute-done.4.low_hbm = bf16[16,128,128]{2,1,0:T(8,128)(2,1)S(1)} collective-permute-done((bf16[16,128,128]{2,1,0:T(8,128)(2,1)}, bf16[16,128,128]{2,1,0:T(8,128)(2,1)S(1)}, u32[]{:S(2)}, u32[]{:S(2)}) %collective-permute-start.4) | collective-permute-done | bytes 524320 | tf_op jit(solution)/shard_map/ppermute | solution.py:16
  82.7 0.0 collective-permute-done.5.high_hbm
  82.7 0.9 copy-done.3
  83.6 0.2 copy-done.5
  83.7 18.7 %shard_map.71 = (f32[64,128,128]{2,1,0:T(8,128)}, f32[128,128]{1,0:T(8,128)}) custom-call(s32[64,8]{1,0:T(8,128)} %copy.9.cols_ref, s32[1]{0:T(128)} %copy.14.count_ref, s32[1,2,16]{2,1,0:T(2,128)} %sends_ref.7, bf16[64,128,128]{2,1,0:T(8,128)(2,1)} %get-tuple-element.20.own_hbm, bf16[16,128,128]{2,1,0:T(8,128)(2,1)} %copy-done.3, ...), custom_call_target="tpu_custom_call" | custom-call | tf_op jit(solution)/shard_map/pallas_call | solution.py:145
  102.4 0.9 copy.11
  103.4 0.1 collective-permute-start.6
  103.5 1.2 collective-permute-done.6
  104.7 0.1 collective-permute-start.7
  104.8 4.3 %collective-permute-done.7 = f32[128,128]{0,1:T(8,128)S(1)} collective-permute-done((f32[128,128]{0,1:T(8,128)S(1)}, f32[128,128]{0,1:T(8,128)S(1)}, u32[]{:S(2)}, u32[]{:S(2)}) %collective-permute-start.7) | collective-permute-done | bytes 65568 | tf_op jit(solution)/shard_map/ppermute | solution.py:28
  109.1 0.1 collective-permute-start.8
  109.2 5.5 %collective-permute-done.8 = f32[128,128]{0,1:T(8,128)S(1)} collective-permute-done((f32[128,128]{0,1:T(8,128)S(1)}, f32[128,128]{0,1:T(8,128)S(1)}, u32[]{:S(2)}, u32[]{:S(2)}) %collective-permute-start.8) | collective-permute-done | bytes 65568 | tf_op jit(solution)/shard_map/ppermute | solution.py:28
  114.6 0.1 collective-permute-start.9
  114.7 4.3 %collective-permute-done.9 = f32[128,128]{0,1:T(8,128)S(1)} collective-permute-done((f32[128,128]{0,1:T(8,128)S(1)}, f32[128,128]{0,1:T(8,128)S(1)}, u32[]{:S(2)}, u32[]{:S(2)}) %collective-permute-start.9) | collective-permute-done | bytes 65568 | tf_op jit(solution)/shard_map/ppermute | solution.py:28
  119.0 0.1 collective-permute-start.10
  119.1 5.5 %collective-permute-done.10 = f32[128,128]{0,1:T(8,128)S(1)} collective-permute-done((f32[128,128]{0,1:T(8,128)S(1)}, f32[128,128]{0,1:T(8,128)S(1)}, u32[]{:S(2)}, u32[]{:S(2)}) %collective-permute-start.10) | collective-permute-done | bytes 65568 | tf_op jit(solution)/shard_map/ppermute | solution.py:28
  124.6 0.1 collective-permute-start.11
  124.7 4.3 %collective-permute-done.11 = f32[128,128]{0,1:T(8,128)S(1)} collective-permute-done((f32[128,128]{0,1:T(8,128)S(1)}, f32[128,128]{0,1:T(8,128)S(1)}, u32[]{:S(2)}, u32[]{:S(2)}) %collective-permute-start.11) | collective-permute-done | bytes 65568 | tf_op jit(solution)/shard_map/ppermute | solution.py:28
  128.9 2.0 %collective-permute-start.12 = (f32[128,128]{0,1:T(8,128)S(1)}, f32[128,128]{0,1:T(8,128)S(1)}, u32[]{:S(2)}, u32[]{:S(2)}) collective-permute-start(f32[128,128]{0,1:T(8,128)S(1)} %add.37), channel_id=1, source_target_pairs={{0,96},{1,97},{2,98},{3,99},{4,100},{5,101},{6,102},{7,103},{8,104... | collective-permute-start | bytes 196616 | tf_op jit(solution)/shard_map/ppermute | solution.py:28
  130.9 3.7 %collective-permute-done.12 = f32[128,128]{0,1:T(8,128)S(1)} collective-permute-done((f32[128,128]{0,1:T(8,128)S(1)}, f32[128,128]{0,1:T(8,128)S(1)}, u32[]{:S(2)}, u32[]{:S(2)}) %collective-permute-start.12) | collective-permute-done | bytes 65568 | tf_op jit(solution)/shard_map/ppermute | solution.py:28
  134.7 0.1 copy.12
  134.8 11.7 %cholesky.17 = f32[128,128]{1,0:T(8,128)S(1)} custom-call(f32[128,128]{1,0:T(8,128)S(1)} %fusion.1), custom_call_target="Cholesky" | custom-call | tf_op jit(solution)/shard_map/jit(cholesky)/cholesky | solution.py:174
  146.5 0.6 compare_reduce_fusion
  147.2 0.7 fusion.2
  147.8 0.7 copy.13
  148.6 9.8 %custom-call.6 = f32[1,128,128]{1,2,0:T(8,128)S(1)} custom-call(f32[1,128,128]{2,1,0:T(8,128)S(1)} %get-tuple-element.31), custom_call_target="InvertDiagBlocksLowerTriangular" | custom-call | tf_op jit(solution)/shard_map/triangular_solve | solution.py:175
  158.4 0.2 convolution_bitcast_fusion
  158.6 6.6 %fusion.4 = f32[64,128,128]{2,1,0:T(8,128)} fusion(f32[64,128,128]{2,1,0:T(8,128)} %get-tuple-element.24, f32[128,128,1]{1,0,2:T(8,128)S(1)} %convolution_bitcast_fusion), kind=kOutput, calls=%fused_computation.14 | convolution fusion | flops 1610612736 | bytes 8454144 | tf_op jit(solution)/shard_map/dot_general | solution.py:178
  (17 shorter events, 0.1 us)
Async XLA Ops:
  0.6 12.7 %copy-start.6 = (s32[64,8]{0,1:T(8,128)S(1)}, s32[64,8]{0,1:T(8,128)}, u32[]{:S(2)}) copy-start(s32[64,8]{0,1:T(8,128)} %param.7) | copy-start | bytes 6148
  4.3 15.4 %collective-permute-start = (bf16[16,128,128]{2,1,0:T(8,128)(2,1)}, bf16[16,128,128]{2,1,0:T(8,128)(2,1)S(1)}, u32[]{:S(2)}, u32[]{:S(2)}) collective-permute-start(bf16[16,128,128]{2,1,0:T(8,128)(2,1)} %get-tuple-element.14), channel_id=1, source_target_pairs={{0,1},{1,2},{2,3},{3,4},{4,5},{5,6},{6,7},{7,8},{8,9},{9,10},{10,1... | collective-permute-start | bytes 1572872 | tf_op jit(solution)/shard_map/ppermute | solution.py:16
  4.4 15.3 %collective-permute-start.1 = (bf16[16,128,128]{2,1,0:T(8,128)(2,1)}, bf16[16,128,128]{2,1,0:T(8,128)(2,1)S(1)}, u32[]{:S(2)}, u32[]{:S(2)}) collective-permute-start(bf16[16,128,128]{2,1,0:T(8,128)(2,1)} %get-tuple-element.15), channel_id=1, source_target_pairs={{0,127},{1,0},{2,1},{3,2},{4,3},{5,4},{6,5},{7,6},{8,7},{9,8},{10,... | collective-permute-start | bytes 1572872 | tf_op jit(solution)/shard_map/ppermute | solution.py:16
  19.7 0.9 copy-start
  19.7 1.0 copy-start.1
  36.9 14.3 %collective-permute-start.2 = (bf16[16,128,128]{2,1,0:T(8,128)(2,1)}, bf16[16,128,128]{2,1,0:T(8,128)(2,1)S(1)}, u32[]{:S(2)}, u32[]{:S(2)}) collective-permute-start(bf16[16,128,128]{2,1,0:T(8,128)(2,1)} %get-tuple-element.17), channel_id=1, source_target_pairs={{0,1},{1,2},{2,3},{3,4},{4,5},{5,6},{6,7},{7,8},{8,9},{9,10},{10,1... | collective-permute-start | bytes 1572872 | tf_op jit(solution)/shard_map/ppermute | solution.py:16
  37.0 14.2 %collective-permute-start.3 = (bf16[16,128,128]{2,1,0:T(8,128)(2,1)}, bf16[16,128,128]{2,1,0:T(8,128)(2,1)S(1)}, u32[]{:S(2)}, u32[]{:S(2)}) collective-permute-start(bf16[16,128,128]{2,1,0:T(8,128)(2,1)} %get-tuple-element.18), channel_id=1, source_target_pairs={{0,127},{1,0},{2,1},{3,2},{4,3},{5,4},{6,5},{7,6},{8,7},{9,8},{10,... | collective-permute-start | bytes 1572872 | tf_op jit(solution)/shard_map/ppermute | solution.py:16
  51.2 0.9 copy-start.2
  51.2 1.0 copy-start.4
  68.4 14.3 %collective-permute-start.4 = (bf16[16,128,128]{2,1,0:T(8,128)(2,1)}, bf16[16,128,128]{2,1,0:T(8,128)(2,1)S(1)}, u32[]{:S(2)}, u32[]{:S(2)}) collective-permute-start(bf16[16,128,128]{2,1,0:T(8,128)(2,1)} %get-tuple-element.21), channel_id=1, source_target_pairs={{0,1},{1,2},{2,3},{3,4},{4,5},{5,6},{6,7},{7,8},{8,9},{9,10},{10,1... | collective-permute-start | bytes 1572872 | tf_op jit(solution)/shard_map/ppermute | solution.py:16
  68.5 14.2 %collective-permute-start.5 = (bf16[16,128,128]{2,1,0:T(8,128)(2,1)}, bf16[16,128,128]{2,1,0:T(8,128)(2,1)S(1)}, u32[]{:S(2)}, u32[]{:S(2)}) collective-permute-start(bf16[16,128,128]{2,1,0:T(8,128)(2,1)} %get-tuple-element.22), channel_id=1, source_target_pairs={{0,127},{1,0},{2,1},{3,2},{4,3},{5,4},{6,5},{7,6},{8,7},{9,8},{10,... | collective-permute-start | bytes 1572872 | tf_op jit(solution)/shard_map/ppermute | solution.py:16
  82.7 0.9 copy-start.3
  82.7 1.0 copy-start.5
  103.4 1.3 collective-permute-start.6
  104.7 4.3 %collective-permute-start.7 = (f32[128,128]{0,1:T(8,128)S(1)}, f32[128,128]{0,1:T(8,128)S(1)}, u32[]{:S(2)}, u32[]{:S(2)}) collective-permute-start(f32[128,128]{0,1:T(8,128)S(1)} %add.32), channel_id=1, source_target_pairs={{0,2},{1,3},{2,0},{3,1},{4,6},{5,7},{6,4},{7,5},{8,10},{9,11},{10,... | collective-permute-start | bytes 196616 | tf_op jit(solution)/shard_map/ppermute | solution.py:28
  109.1 5.6 %collective-permute-start.8 = (f32[128,128]{0,1:T(8,128)S(1)}, f32[128,128]{0,1:T(8,128)S(1)}, u32[]{:S(2)}, u32[]{:S(2)}) collective-permute-start(f32[128,128]{0,1:T(8,128)S(1)} %add.33), channel_id=1, source_target_pairs={{0,6},{1,7},{2,4},{3,5},{4,2},{5,3},{6,0},{7,1},{8,14},{9,15},{10,... | collective-permute-start | bytes 196616 | tf_op jit(solution)/shard_map/ppermute | solution.py:28
  114.6 4.3 %collective-permute-start.9 = (f32[128,128]{0,1:T(8,128)S(1)}, f32[128,128]{0,1:T(8,128)S(1)}, u32[]{:S(2)}, u32[]{:S(2)}) collective-permute-start(f32[128,128]{0,1:T(8,128)S(1)} %add.34), channel_id=1, source_target_pairs={{0,8},{1,9},{2,10},{3,11},{4,12},{5,13},{6,14},{7,15},{8,0},{9,1},... | collective-permute-start | bytes 196616 | tf_op jit(solution)/shard_map/ppermute | solution.py:28
  119.0 5.6 %collective-permute-start.10 = (f32[128,128]{0,1:T(8,128)S(1)}, f32[128,128]{0,1:T(8,128)S(1)}, u32[]{:S(2)}, u32[]{:S(2)}) collective-permute-start(f32[128,128]{0,1:T(8,128)S(1)} %add.35), channel_id=1, source_target_pairs={{0,24},{1,25},{2,26},{3,27},{4,28},{5,29},{6,30},{7,31},{8,16},{9,... | collective-permute-start | bytes 196616 | tf_op jit(solution)/shard_map/ppermute | solution.py:28
  124.6 4.3 %collective-permute-start.11 = (f32[128,128]{0,1:T(8,128)S(1)}, f32[128,128]{0,1:T(8,128)S(1)}, u32[]{:S(2)}, u32[]{:S(2)}) collective-permute-start(f32[128,128]{0,1:T(8,128)S(1)} %add.36), channel_id=1, source_target_pairs={{0,32},{1,33},{2,34},{3,35},{4,36},{5,37},{6,38},{7,39},{8,40},{9,... | collective-permute-start | bytes 196616 | tf_op jit(solution)/shard_map/ppermute | solution.py:28
  128.9 5.7 %collective-permute-start.12 = (f32[128,128]{0,1:T(8,128)S(1)}, f32[128,128]{0,1:T(8,128)S(1)}, u32[]{:S(2)}, u32[]{:S(2)}) collective-permute-start(f32[128,128]{0,1:T(8,128)S(1)} %add.37), channel_id=1, source_target_pairs={{0,96},{1,97},{2,98},{3,99},{4,100},{5,101},{6,102},{7,103},{8,104... | collective-permute-start | bytes 196616 | tf_op jit(solution)/shard_map/ppermute | solution.py:28

commit v9 on v7

--- a/solution.py
+++ b/solution.py
@@ -94,7 +94,7 @@
         if not last:
             out_ref[r] = new.astype(jnp.bfloat16)
             continue
-        part = lax.dot_general(new, new, (((0,), (0,)), ((), ())), precision=lax.Precision.HIGHEST,
+        part = lax.dot_general(new, new, (((0,), (0,)), ((), ())), precision=lax.Precision.HIGH,
                                preferred_element_type=jnp.float32)
         if r == 0:
             @pl.when(step == 0)
@@ -174,7 +174,7 @@
     inverse = lax.linalg.triangular_solve(
         first_low, jnp.eye(vectors, dtype=jnp.float32), left_side=True, lower=True
     )
-    basis = jnp.dot(flat, inverse.T, precision=lax.Precision.HIGHEST)
+    basis = jnp.dot(flat, inverse.T, precision=lax.Precision.HIGH)
     r_factor = first_low.T
     return (basis.reshape(slots, width, vectors), r_factor)
 

time: 165 us -> 165 us (level)
  no operation moved by 1% of the time
where the time goes in v9:
time: 165 us; the launch traced here: 164 us
  Pallas kernels  53.2 us (32%)
  waiting for transfers between devices  42.8 us (26%)
  other arithmetic  28.5 us (17%)
  starting transfers between devices  25.4 us (15%)
  local copies, waits for them, and re-layouts  6.77 us (4%)
  matrix products  6.26 us (4%)
    pallas_call x3, Pallas kernels, substep(): pl.pallas_call(kernel, grid_spec=grid_spec, out_shape=[jax.ShapeDtypeStru...  49.7 us
    ppermute x7, waiting for transfers between devices, tree_sum(): value = value + lax.ppermute(value, axis, partner)  28.6 us
    ppermute x6, starting transfers between devices, passed_along(): lax.ppermute(shard, axis, [(i, (i + by) % length) for i in range(length)])  22.8 us
    ppermute x6, waiting for transfers between devices, passed_along(): lax.ppermute(shard, axis, [(i, (i + by) % length) for i in range(length)])  14.2 us
    another operation x3, other arithmetic, local(): first_low = jnp.linalg.cholesky(tree_sum(gram, 'grains'))  12.4 us
    another operation x1, other arithmetic, local(): lax.linalg.triangular_solve(first_low, jnp.eye(vectors, dtype=jnp.float32...  9.81 us
    dot_general x1, matrix products, local(): basis = jnp.dot(flat, inverse.T, precision=lax.Precision.HIGH)  6.01 us
    convert_element_type x1, other arithmetic, local(): rounded = state.astype(jnp.bfloat16)  5.53 us
  transfers between devices with their start and end apart: 13, of which 10 were waited for; matrix products, arithmetic and copies ran while one was open for 4% of the time, Pallas kernels for 0%

profile of v9, /device:TPU:0, one launch (start us, length us, event | category | flops | bytes accessed | tf_op | source)
XLA Modules:
  0.0 164.4 jit_solution(11128420723065901696)
XLA Ops:
  0.6 1.4 reshape.29.sends_ref
  2.0 3.5 %shard_map.68 = (bf16[16,128,128]{2,1,0:T(8,128)(2,1)}, bf16[16,128,128]{2,1,0:T(8,128)(2,1)}) custom-call(s32[32]{0:T(128)} %reshape.29.sends_ref, f32[64,128,128]{2,1,0:T(8,128)} %tangent_hbm.1), custom_call_target="tpu_custom_call" | custom-call | tf_op jit(solution)/shard_map/pallas_call | solution.py:56
  5.5 0.1 collective-permute-start
  5.6 8.3 %collective-permute-start.1 = (bf16[16,128,128]{2,1,0:T(8,128)(2,1)}, bf16[16,128,128]{2,1,0:T(8,128)(2,1)S(1)}, u32[]{:S(2)}, u32[]{:S(2)}) collective-permute-start(bf16[16,128,128]{2,1,0:T(8,128)(2,1)} %get-tuple-element.15), channel_id=1, source_target_pairs={{0,127},{1,0},{2,1},{3,2},{4,3},{5,4},{6,5},{7,6},{8,7},{9,8},{10,... | collective-permute-start | bytes 1572872 | tf_op jit(solution)/shard_map/ppermute | solution.py:16
  14.5 0.1 copy.11
  14.6 0.6 reshape.28.cols_ref
  15.3 5.5 %fusion.3 = (bf16[64,128,128]{2,1,0:T(8,128)(2,1)}, f32[64,128,128]{2,1,0:T(8,128)}) fusion(f32[64,128,128]{2,1,0:T(8,128)} %tangent_hbm.1, f32[64]{0:T(128)S(1)} %compare_convert_fusion), kind=kLoop, calls=%fused_computation.13 | loop fusion | flops 2097152 | bytes 10486016 | tf_op jit(solution)/shard_map/convert_element_type | solution.py:160
  20.8 0.1 collective-permute-done.low_hbm
  20.9 0.0 collective-permute-done.1.high_hbm
  20.9 0.8 copy-done
  21.7 0.1 copy-done.1
  21.9 15.7 %shard_map.69 = (f32[64,128,128]{2,1,0:T(8,128)}, bf16[64,128,128]{2,1,0:T(8,128)(2,1)}, bf16[16,128,128]{2,1,0:T(8,128)(2,1)}, bf16[16,128,128]{2,1,0:T(8,128)(2,1)}) custom-call(s32[512]{0:T(512)} %reshape.28.cols_ref, s32[1]{0:T(128)} %copy.16.count_ref, s32[32]{0:T(128)} %reshape.29.sends_ref, bf16[64,128,128]{2,1,0:T(8,128)(2,1)} %get-tuple-element.30.own_hbm, ...), custom_call_target="tpu_custom_call" | custom-call | tf_op jit(solution)/shard_map/pallas_call | solution.py:144
  37.5 0.1 collective-permute-start.2
  37.6 7.2 %collective-permute-start.3 = (bf16[16,128,128]{2,1,0:T(8,128)(2,1)}, bf16[16,128,128]{2,1,0:T(8,128)(2,1)S(1)}, u32[]{:S(2)}, u32[]{:S(2)}) collective-permute-start(bf16[16,128,128]{2,1,0:T(8,128)(2,1)} %get-tuple-element.18), channel_id=1, source_target_pairs={{0,127},{1,0},{2,1},{3,2},{4,3},{5,4},{6,5},{7,6},{8,7},{9,8},{10,... | collective-permute-start | bytes 1572872 | tf_op jit(solution)/shard_map/ppermute | solution.py:16
  44.8 7.1 %collective-permute-done.2.low_hbm = bf16[16,128,128]{2,1,0:T(8,128)(2,1)S(1)} collective-permute-done((bf16[16,128,128]{2,1,0:T(8,128)(2,1)}, bf16[16,128,128]{2,1,0:T(8,128)(2,1)S(1)}, u32[]{:S(2)}, u32[]{:S(2)}) %collective-permute-start.2) | collective-permute-done | bytes 524320 | tf_op jit(solution)/shard_map/ppermute | solution.py:16
  51.9 0.0 collective-permute-done.3.high_hbm
  51.9 0.9 copy-done.3
  52.7 0.1 copy-done.5
  52.9 15.7 %shard_map.70 = (f32[64,128,128]{2,1,0:T(8,128)}, bf16[64,128,128]{2,1,0:T(8,128)(2,1)}, bf16[16,128,128]{2,1,0:T(8,128)(2,1)}, bf16[16,128,128]{2,1,0:T(8,128)(2,1)}) custom-call(s32[512]{0:T(512)} %reshape.28.cols_ref, s32[1]{0:T(128)} %copy.16.count_ref, s32[32]{0:T(128)} %reshape.29.sends_ref, bf16[64,128,128]{2,1,0:T(8,128)(2,1)} %get-tuple-element.16.own_hbm, ...), custom_call_target="tpu_custom_call" | custom-call | tf_op jit(solution)/shard_map/pallas_call | solution.py:144
  68.5 0.1 collective-permute-start.4
  68.6 7.2 %collective-permute-start.5 = (bf16[16,128,128]{2,1,0:T(8,128)(2,1)}, bf16[16,128,128]{2,1,0:T(8,128)(2,1)S(1)}, u32[]{:S(2)}, u32[]{:S(2)}) collective-permute-start(bf16[16,128,128]{2,1,0:T(8,128)(2,1)} %get-tuple-element.22), channel_id=1, source_target_pairs={{0,127},{1,0},{2,1},{3,2},{4,3},{5,4},{6,5},{7,6},{8,7},{9,8},{10,... | collective-permute-start | bytes 1572872 | tf_op jit(solution)/shard_map/ppermute | solution.py:16
  75.8 7.1 %collective-permute-done.4.low_hbm = bf16[16,128,128]{2,1,0:T(8,128)(2,1)S(1)} collective-permute-done((bf16[16,128,128]{2,1,0:T(8,128)(2,1)}, bf16[16,128,128]{2,1,0:T(8,128)(2,1)S(1)}, u32[]{:S(2)}, u32[]{:S(2)}) %collective-permute-start.4) | collective-permute-done | bytes 524320 | tf_op jit(solution)/shard_map/ppermute | solution.py:16
  82.8 0.8 copy-done.2
  83.6 0.2 copy-done.4
  83.8 18.4 %shard_map.71 = (f32[64,128,128]{2,1,0:T(8,128)}, f32[128,128]{1,0:T(8,128)}) custom-call(s32[512]{0:T(512)} %reshape.28.cols_ref, s32[1]{0:T(128)} %copy.16.count_ref, s32[32]{0:T(128)} %reshape.29.sends_ref, bf16[64,128,128]{2,1,0:T(8,128)(2,1)} %get-tuple-element.20.own_hbm, bf16[16,128,128]{2,1,0:T(8,128)(2,1)} %copy-done.2, ...), custom_call_target="tpu_custom_call" | custom-call | tf_op jit(solution)/shard_map/pallas_call | solution.py:144
  102.2 0.9 copy.13
  103.1 0.1 collective-permute-start.6
  103.2 1.2 collective-permute-done.6
  104.5 0.1 collective-permute-start.7
  104.6 4.3 %collective-permute-done.7 = f32[128,128]{0,1:T(8,128)S(1)} collective-permute-done((f32[128,128]{0,1:T(8,128)S(1)}, f32[128,128]{0,1:T(8,128)S(1)}, u32[]{:S(2)}, u32[]{:S(2)}) %collective-permute-start.7) | collective-permute-done | bytes 65568 | tf_op jit(solution)/shard_map/ppermute | solution.py:28
  108.8 0.1 collective-permute-start.8
  108.9 5.5 %collective-permute-done.8 = f32[128,128]{0,1:T(8,128)S(1)} collective-permute-done((f32[128,128]{0,1:T(8,128)S(1)}, f32[128,128]{0,1:T(8,128)S(1)}, u32[]{:S(2)}, u32[]{:S(2)}) %collective-permute-start.8) | collective-permute-done | bytes 65568 | tf_op jit(solution)/shard_map/ppermute | solution.py:28
  114.4 0.1 collective-permute-start.9
  114.5 4.3 %collective-permute-done.9 = f32[128,128]{0,1:T(8,128)S(1)} collective-permute-done((f32[128,128]{0,1:T(8,128)S(1)}, f32[128,128]{0,1:T(8,128)S(1)}, u32[]{:S(2)}, u32[]{:S(2)}) %collective-permute-start.9) | collective-permute-done | bytes 65568 | tf_op jit(solution)/shard_map/ppermute | solution.py:28
  118.8 0.1 collective-permute-start.10
  118.9 5.5 %collective-permute-done.10 = f32[128,128]{0,1:T(8,128)S(1)} collective-permute-done((f32[128,128]{0,1:T(8,128)S(1)}, f32[128,128]{0,1:T(8,128)S(1)}, u32[]{:S(2)}, u32[]{:S(2)}) %collective-permute-start.10) | collective-permute-done | bytes 65568 | tf_op jit(solution)/shard_map/ppermute | solution.py:28
  124.3 0.1 collective-permute-start.11
  124.4 4.3 %collective-permute-done.11 = f32[128,128]{0,1:T(8,128)S(1)} collective-permute-done((f32[128,128]{0,1:T(8,128)S(1)}, f32[128,128]{0,1:T(8,128)S(1)}, u32[]{:S(2)}, u32[]{:S(2)}) %collective-permute-start.11) | collective-permute-done | bytes 65568 | tf_op jit(solution)/shard_map/ppermute | solution.py:28
  128.7 2.1 %collective-permute-start.12 = (f32[128,128]{0,1:T(8,128)S(1)}, f32[128,128]{0,1:T(8,128)S(1)}, u32[]{:S(2)}, u32[]{:S(2)}) collective-permute-start(f32[128,128]{0,1:T(8,128)S(1)} %add.37), channel_id=1, source_target_pairs={{0,96},{1,97},{2,98},{3,99},{4,100},{5,101},{6,102},{7,103},{8,104... | collective-permute-start | bytes 196616 | tf_op jit(solution)/shard_map/ppermute | solution.py:28
  130.8 3.7 %collective-permute-done.12 = f32[128,128]{0,1:T(8,128)S(1)} collective-permute-done((f32[128,128]{0,1:T(8,128)S(1)}, f32[128,128]{0,1:T(8,128)S(1)}, u32[]{:S(2)}, u32[]{:S(2)}) %collective-permute-start.12) | collective-permute-done | bytes 65568 | tf_op jit(solution)/shard_map/ppermute | solution.py:28
  134.5 0.1 copy.14
  134.6 11.7 %cholesky.17 = f32[128,128]{1,0:T(8,128)S(1)} custom-call(f32[128,128]{1,0:T(8,128)S(1)} %fusion.1), custom_call_target="Cholesky" | custom-call | tf_op jit(solution)/shard_map/jit(cholesky)/cholesky | solution.py:173
  146.3 0.6 compare_reduce_fusion
  147.0 0.7 fusion.2
  147.6 0.7 copy.15
  148.4 9.8 %custom-call.6 = f32[1,128,128]{1,2,0:T(8,128)S(1)} custom-call(f32[1,128,128]{2,1,0:T(8,128)S(1)} %get-tuple-element.33), custom_call_target="InvertDiagBlocksLowerTriangular" | custom-call | tf_op jit(solution)/shard_map/triangular_solve | solution.py:174
  158.2 0.2 convolution_bitcast_fusion
  158.4 6.0 %fusion.4 = f32[64,128,128]{2,1,0:T(8,128)} fusion(f32[64,128,128]{2,1,0:T(8,128)} %get-tuple-element.24, f32[128,128,1]{1,0,2:T(8,128)S(1)} %convolution_bitcast_fusion), kind=kOutput, calls=%fused_computation.14 | convolution fusion | flops 805306368 | bytes 8454144 | tf_op jit(solution)/shard_map/dot_general | solution.py:177
  (19 shorter events, 0.1 us)
Async XLA Ops:
  0.6 13.9 %copy-start.6 = (s32[64,8]{0,1:T(8,128)S(1)}, s32[64,8]{0,1:T(8,128)}, u32[]{:S(2)}) copy-start(s32[64,8]{0,1:T(8,128)} %param.7) | copy-start | bytes 6148
  5.5 15.4 %collective-permute-start = (bf16[16,128,128]{2,1,0:T(8,128)(2,1)}, bf16[16,128,128]{2,1,0:T(8,128)(2,1)S(1)}, u32[]{:S(2)}, u32[]{:S(2)}) collective-permute-start(bf16[16,128,128]{2,1,0:T(8,128)(2,1)} %get-tuple-element.14), channel_id=1, source_target_pairs={{0,1},{1,2},{2,3},{3,4},{4,5},{5,6},{6,7},{7,8},{8,9},{9,10},{10,1... | collective-permute-start | bytes 1572872 | tf_op jit(solution)/shard_map/ppermute | solution.py:16
  5.6 15.3 %collective-permute-start.1 = (bf16[16,128,128]{2,1,0:T(8,128)(2,1)}, bf16[16,128,128]{2,1,0:T(8,128)(2,1)S(1)}, u32[]{:S(2)}, u32[]{:S(2)}) collective-permute-start(bf16[16,128,128]{2,1,0:T(8,128)(2,1)} %get-tuple-element.15), channel_id=1, source_target_pairs={{0,127},{1,0},{2,1},{3,2},{4,3},{5,4},{6,5},{7,6},{8,7},{9,8},{10,... | collective-permute-start | bytes 1572872 | tf_op jit(solution)/shard_map/ppermute | solution.py:16
  20.9 0.9 copy-start
  20.9 1.0 copy-start.1
  37.5 14.3 %collective-permute-start.2 = (bf16[16,128,128]{2,1,0:T(8,128)(2,1)}, bf16[16,128,128]{2,1,0:T(8,128)(2,1)S(1)}, u32[]{:S(2)}, u32[]{:S(2)}) collective-permute-start(bf16[16,128,128]{2,1,0:T(8,128)(2,1)} %get-tuple-element.17), channel_id=1, source_target_pairs={{0,1},{1,2},{2,3},{3,4},{4,5},{5,6},{6,7},{7,8},{8,9},{9,10},{10,1... | collective-permute-start | bytes 1572872 | tf_op jit(solution)/shard_map/ppermute | solution.py:16
  37.6 14.2 %collective-permute-start.3 = (bf16[16,128,128]{2,1,0:T(8,128)(2,1)}, bf16[16,128,128]{2,1,0:T(8,128)(2,1)S(1)}, u32[]{:S(2)}, u32[]{:S(2)}) collective-permute-start(bf16[16,128,128]{2,1,0:T(8,128)(2,1)} %get-tuple-element.18), channel_id=1, source_target_pairs={{0,127},{1,0},{2,1},{3,2},{4,3},{5,4},{6,5},{7,6},{8,7},{9,8},{10,... | collective-permute-start | bytes 1572872 | tf_op jit(solution)/shard_map/ppermute | solution.py:16
  51.9 0.9 copy-start.3
  51.9 1.0 copy-start.5
  68.5 14.3 %collective-permute-start.4 = (bf16[16,128,128]{2,1,0:T(8,128)(2,1)}, bf16[16,128,128]{2,1,0:T(8,128)(2,1)S(1)}, u32[]{:S(2)}, u32[]{:S(2)}) collective-permute-start(bf16[16,128,128]{2,1,0:T(8,128)(2,1)} %get-tuple-element.21), channel_id=1, source_target_pairs={{0,1},{1,2},{2,3},{3,4},{4,5},{5,6},{6,7},{7,8},{8,9},{9,10},{10,1... | collective-permute-start | bytes 1572872 | tf_op jit(solution)/shard_map/ppermute | solution.py:16
  68.6 14.2 %collective-permute-start.5 = (bf16[16,128,128]{2,1,0:T(8,128)(2,1)}, bf16[16,128,128]{2,1,0:T(8,128)(2,1)S(1)}, u32[]{:S(2)}, u32[]{:S(2)}) collective-permute-start(bf16[16,128,128]{2,1,0:T(8,128)(2,1)} %get-tuple-element.22), channel_id=1, source_target_pairs={{0,127},{1,0},{2,1},{3,2},{4,3},{5,4},{6,5},{7,6},{8,7},{9,8},{10,... | collective-permute-start | bytes 1572872 | tf_op jit(solution)/shard_map/ppermute | solution.py:16
  82.8 0.8 copy-start.2
  82.8 1.0 copy-start.4
  103.1 1.3 collective-permute-start.6
  104.5 4.3 %collective-permute-start.7 = (f32[128,128]{0,1:T(8,128)S(1)}, f32[128,128]{0,1:T(8,128)S(1)}, u32[]{:S(2)}, u32[]{:S(2)}) collective-permute-start(f32[128,128]{0,1:T(8,128)S(1)} %add.32), channel_id=1, source_target_pairs={{0,2},{1,3},{2,0},{3,1},{4,6},{5,7},{6,4},{7,5},{8,10},{9,11},{10,... | collective-permute-start | bytes 196616 | tf_op jit(solution)/shard_map/ppermute | solution.py:28
  108.8 5.6 %collective-permute-start.8 = (f32[128,128]{0,1:T(8,128)S(1)}, f32[128,128]{0,1:T(8,128)S(1)}, u32[]{:S(2)}, u32[]{:S(2)}) collective-permute-start(f32[128,128]{0,1:T(8,128)S(1)} %add.33), channel_id=1, source_target_pairs={{0,6},{1,7},{2,4},{3,5},{4,2},{5,3},{6,0},{7,1},{8,14},{9,15},{10,... | collective-permute-start | bytes 196616 | tf_op jit(solution)/shard_map/ppermute | solution.py:28
  114.4 4.3 %collective-permute-start.9 = (f32[128,128]{0,1:T(8,128)S(1)}, f32[128,128]{0,1:T(8,128)S(1)}, u32[]{:S(2)}, u32[]{:S(2)}) collective-permute-start(f32[128,128]{0,1:T(8,128)S(1)} %add.34), channel_id=1, source_target_pairs={{0,8},{1,9},{2,10},{3,11},{4,12},{5,13},{6,14},{7,15},{8,0},{9,1},... | collective-permute-start | bytes 196616 | tf_op jit(solution)/shard_map/ppermute | solution.py:28
  118.8 5.6 %collective-permute-start.10 = (f32[128,128]{0,1:T(8,128)S(1)}, f32[128,128]{0,1:T(8,128)S(1)}, u32[]{:S(2)}, u32[]{:S(2)}) collective-permute-start(f32[128,128]{0,1:T(8,128)S(1)} %add.35), channel_id=1, source_target_pairs={{0,24},{1,25},{2,26},{3,27},{4,28},{5,29},{6,30},{7,31},{8,16},{9,... | collective-permute-start | bytes 196616 | tf_op jit(solution)/shard_map/ppermute | solution.py:28
  124.3 4.3 %collective-permute-start.11 = (f32[128,128]{0,1:T(8,128)S(1)}, f32[128,128]{0,1:T(8,128)S(1)}, u32[]{:S(2)}, u32[]{:S(2)}) collective-permute-start(f32[128,128]{0,1:T(8,128)S(1)} %add.36), channel_id=1, source_target_pairs={{0,32},{1,33},{2,34},{3,35},{4,36},{5,37},{6,38},{7,39},{8,40},{9,... | collective-permute-start | bytes 196616 | tf_op jit(solution)/shard_map/ppermute | solution.py:28
  128.7 5.7 %collective-permute-start.12 = (f32[128,128]{0,1:T(8,128)S(1)}, f32[128,128]{0,1:T(8,128)S(1)}, u32[]{:S(2)}, u32[]{:S(2)}) collective-permute-start(f32[128,128]{0,1:T(8,128)S(1)} %add.37), channel_id=1, source_target_pairs={{0,96},{1,97},{2,98},{3,99},{4,100},{5,101},{6,102},{7,103},{8,104... | collective-permute-start | bytes 196616 | tf_op jit(solution)/shard_map/ppermute | solution.py:28

commit v10 on v7

--- a/solution.py
+++ b/solution.py
@@ -23,10 +23,11 @@
     while bit < length:
         masks += [bit, 3 * bit] if 4 * bit <= length else [bit]
         bit *= 4
+    halves = jnp.split(value, 2, axis=0)
     for mask in masks:
         partner = [(i, i ^ mask) for i in range(length)]
-        value = value + lax.ppermute(value, axis, partner)
-    return value
+        halves = [half + lax.ppermute(half, axis, partner) for half in halves]
+    return jnp.concatenate(halves, axis=0)
 
 
 def pick_kernel(sends_ref, tangent_hbm, to_lower_ref, to_upper_ref, buf, sems):

time: 165 us -> 169 us (1.024)
  starting transfers between devices: 25.4 us -> 39.6 us
  waiting for transfers between devices: 42.8 us -> 32.4 us
    ppermute x7 -> x14, starting transfers between devices: 2.57 us -> 16.7 us  [tree_sum(): halves = [half + lax.ppermute(half, axis, partner) for half in halves]]
    ppermute x7 -> x14, waiting for transfers between devices: 28.6 us -> 18.2 us  [tree_sum(): halves = [half + lax.ppermute(half, axis, partner) for half in halves]]
  transfers between devices with their start and end apart: 13 -> 20, of which waited for: 10 -> 16; matrix products, arithmetic and copies ran while one was open for 4% -> 4% of each run, Pallas kernels for 0% -> 0%
where the time goes in v10:
time: 169 us
  Pallas kernels  53 us (31%)
  starting transfers between devices  39.6 us (23%)
  waiting for transfers between devices  32.4 us (19%)
  other arithmetic  28.7 us (17%)
  matrix products  6.8 us (4%)
  local copies, waits for them, and re-layouts  6.76 us (4%)
    pallas_call x3, Pallas kernels, substep(): pl.pallas_call(kernel, grid_spec=grid_spec, out_shape=[jax.ShapeDtypeStru...  49.5 us
    ppermute x6, starting transfers between devices, passed_along(): lax.ppermute(shard, axis, [(i, (i + by) % length) for i in range(length)])  22.9 us
    ppermute x14, waiting for transfers between devices, tree_sum(): halves = [half + lax.ppermute(half, axis, partner) for half in halves]  18.2 us
    ppermute x14, starting transfers between devices, tree_sum(): halves = [half + lax.ppermute(half, axis, partner) for half in halves]  16.7 us
    ppermute x6, waiting for transfers between devices, passed_along(): lax.ppermute(shard, axis, [(i, (i + by) % length) for i in range(length)])  14.2 us
    another operation x3, other arithmetic, local(): first_low = jnp.linalg.cholesky(tree_sum(gram, 'grains'))  12.4 us
    another operation x1, other arithmetic, local(): lax.linalg.triangular_solve(first_low, jnp.eye(vectors, dtype=jnp.float32...  9.81 us
    dot_general x1, matrix products, local(): basis = jnp.dot(flat, inverse.T, precision=lax.Precision.HIGHEST)  6.55 us
  transfers between devices with their start and end apart: 20, of which 16 were waited for; matrix products, arithmetic and copies ran while one was open for 4% of the time, Pallas kernels for 0%

profile of v10, /device:TPU:0, one launch (start us, length us, event | category | flops | bytes accessed | tf_op | source)
XLA Modules:
  0.0 168.7 jit_solution(16770678714292048060)
XLA Ops:
  0.6 1.3 reshape.29.sends_ref
  1.9 3.5 %shard_map.68 = (bf16[16,128,128]{2,1,0:T(8,128)(2,1)}, bf16[16,128,128]{2,1,0:T(8,128)(2,1)}) custom-call(s32[32]{0:T(128)} %reshape.29.sends_ref, f32[64,128,128]{2,1,0:T(8,128)} %tangent_hbm.1), custom_call_target="tpu_custom_call" | custom-call | tf_op jit(solution)/shard_map/pallas_call | solution.py:57
  5.5 8.3 %collective-permute-start.1 = (bf16[16,128,128]{2,1,0:T(8,128)(2,1)}, bf16[16,128,128]{2,1,0:T(8,128)(2,1)S(1)}, u32[]{:S(2)}, u32[]{:S(2)}) collective-permute-start(bf16[16,128,128]{2,1,0:T(8,128)(2,1)} %get-tuple-element.15), channel_id=1, source_target_pairs={{0,127},{1,0},{2,1},{3,2},{4,3},{5,4},{6,5},{7,6},{8,7},{9,8},{10,... | collective-permute-start | bytes 1572872 | tf_op jit(solution)/shard_map/ppermute | solution.py:16
  14.6 0.6 reshape.28.cols_ref
  15.2 5.5 %fusion.3 = (bf16[64,128,128]{2,1,0:T(8,128)(2,1)}, f32[64,128,128]{2,1,0:T(8,128)}) fusion(f32[64,128,128]{2,1,0:T(8,128)} %tangent_hbm.1, f32[64]{0:T(128)S(1)} %compare_convert_fusion), kind=kLoop, calls=%fused_computation.16 | loop fusion | flops 2097152 | bytes 10486016 | tf_op jit(solution)/shard_map/convert_element_type | solution.py:161
  20.8 0.8 copy-done
  21.7 0.1 copy-done.1
  21.8 15.7 %shard_map.69 = (f32[64,128,128]{2,1,0:T(8,128)}, bf16[64,128,128]{2,1,0:T(8,128)(2,1)}, bf16[16,128,128]{2,1,0:T(8,128)(2,1)}, bf16[16,128,128]{2,1,0:T(8,128)(2,1)}) custom-call(s32[512]{0:T(512)} %reshape.28.cols_ref, s32[1]{0:T(128)} %copy.16.count_ref, s32[32]{0:T(128)} %reshape.29.sends_ref, bf16[64,128,128]{2,1,0:T(8,128)(2,1)} %get-tuple-element.30.own_hbm, ...), custom_call_target="tpu_custom_call" | custom-call | tf_op jit(solution)/shard_map/pallas_call | solution.py:145
  37.6 7.2 %collective-permute-start.3 = (bf16[16,128,128]{2,1,0:T(8,128)(2,1)}, bf16[16,128,128]{2,1,0:T(8,128)(2,1)S(1)}, u32[]{:S(2)}, u32[]{:S(2)}) collective-permute-start(bf16[16,128,128]{2,1,0:T(8,128)(2,1)} %get-tuple-element.18), channel_id=1, source_target_pairs={{0,127},{1,0},{2,1},{3,2},{4,3},{5,4},{6,5},{7,6},{8,7},{9,8},{10,... | collective-permute-start | bytes 1572872 | tf_op jit(solution)/shard_map/ppermute | solution.py:16
  44.7 7.1 %collective-permute-done.2.low_hbm = bf16[16,128,128]{2,1,0:T(8,128)(2,1)S(1)} collective-permute-done((bf16[16,128,128]{2,1,0:T(8,128)(2,1)}, bf16[16,128,128]{2,1,0:T(8,128)(2,1)S(1)}, u32[]{:S(2)}, u32[]{:S(2)}) %collective-permute-start.2) | collective-permute-done | bytes 524320 | tf_op jit(solution)/shard_map/ppermute | solution.py:16
  51.8 0.9 copy-done.3
  52.7 0.1 copy-done.5
  52.8 15.7 %shard_map.70 = (f32[64,128,128]{2,1,0:T(8,128)}, bf16[64,128,128]{2,1,0:T(8,128)(2,1)}, bf16[16,128,128]{2,1,0:T(8,128)(2,1)}, bf16[16,128,128]{2,1,0:T(8,128)(2,1)}) custom-call(s32[512]{0:T(512)} %reshape.28.cols_ref, s32[1]{0:T(128)} %copy.16.count_ref, s32[32]{0:T(128)} %reshape.29.sends_ref, bf16[64,128,128]{2,1,0:T(8,128)(2,1)} %get-tuple-element.16.own_hbm, ...), custom_call_target="tpu_custom_call" | custom-call | tf_op jit(solution)/shard_map/pallas_call | solution.py:145
  68.5 7.2 %collective-permute-start.5 = (bf16[16,128,128]{2,1,0:T(8,128)(2,1)}, bf16[16,128,128]{2,1,0:T(8,128)(2,1)S(1)}, u32[]{:S(2)}, u32[]{:S(2)}) collective-permute-start(bf16[16,128,128]{2,1,0:T(8,128)(2,1)} %get-tuple-element.22), channel_id=1, source_target_pairs={{0,127},{1,0},{2,1},{3,2},{4,3},{5,4},{6,5},{7,6},{8,7},{9,8},{10,... | collective-permute-start | bytes 1572872 | tf_op jit(solution)/shard_map/ppermute | solution.py:16
  75.7 7.1 %collective-permute-done.4.low_hbm = bf16[16,128,128]{2,1,0:T(8,128)(2,1)S(1)} collective-permute-done((bf16[16,128,128]{2,1,0:T(8,128)(2,1)}, bf16[16,128,128]{2,1,0:T(8,128)(2,1)S(1)}, u32[]{:S(2)}, u32[]{:S(2)}) %collective-permute-start.4) | collective-permute-done | bytes 524320 | tf_op jit(solution)/shard_map/ppermute | solution.py:16
  82.8 0.8 copy-done.2
  83.6 0.1 copy-done.4
  83.7 18.1 %shard_map.71 = (f32[64,128,128]{2,1,0:T(8,128)}, f32[128,128]{1,0:T(8,128)}) custom-call(s32[512]{0:T(512)} %reshape.28.cols_ref, s32[1]{0:T(128)} %copy.16.count_ref, s32[32]{0:T(128)} %reshape.29.sends_ref, bf16[64,128,128]{2,1,0:T(8,128)(2,1)} %get-tuple-element.20.own_hbm, bf16[16,128,128]{2,1,0:T(8,128)(2,1)} %copy-done.2, ...), custom_call_target="tpu_custom_call" | custom-call | tf_op jit(solution)/shard_map/pallas_call | solution.py:145
  101.9 0.9 copy.12
  103.0 0.5 collective-permute-start.13
  103.5 0.7 collective-permute-done.6
  104.2 0.2 collective-permute-done.13
  104.6 2.0 %collective-permute-start.14 = (f32[64,128]{0,1:T(8,128)S(1)}, f32[64,128]{0,1:T(8,128)S(1)}, u32[]{:S(2)}, u32[]{:S(2)}) collective-permute-start(f32[64,128]{0,1:T(8,128)S(1)} %get-tuple-element.35), channel_id=1, source_target_pairs={{0,2},{1,3},{2,0},{3,1},{4,6},{5,7},{6,4},{7,5},{8,10},{9,11},{10,... | collective-permute-start | bytes 98312 | tf_op jit(solution)/shard_map/ppermute | solution.py:29
  106.6 2.9 %collective-permute-done.7 = f32[64,128]{0,1:T(8,128)S(1)} collective-permute-done((f32[64,128]{0,1:T(8,128)S(1)}, f32[64,128]{0,1:T(8,128)S(1)}, u32[]{:S(2)}, u32[]{:S(2)}) %collective-permute-start.7) | collective-permute-done | bytes 32800 | tf_op jit(solution)/shard_map/ppermute | solution.py:29
  109.6 0.7 collective-permute-done.14
  110.3 2.6 %collective-permute-start.15 = (f32[64,128]{0,1:T(8,128)S(1)}, f32[64,128]{0,1:T(8,128)S(1)}, u32[]{:S(2)}, u32[]{:S(2)}) collective-permute-start(f32[64,128]{0,1:T(8,128)S(1)} %add.61), channel_id=1, source_target_pairs={{0,6},{1,7},{2,4},{3,5},{4,2},{5,3},{6,0},{7,1},{8,14},{9,15},{10,... | collective-permute-start | bytes 98312 | tf_op jit(solution)/shard_map/ppermute | solution.py:29
  112.9 2.2 %collective-permute-done.8 = f32[64,128]{0,1:T(8,128)S(1)} collective-permute-done((f32[64,128]{0,1:T(8,128)S(1)}, f32[64,128]{0,1:T(8,128)S(1)}, u32[]{:S(2)}, u32[]{:S(2)}) %collective-permute-start.8) | collective-permute-done | bytes 32800 | tf_op jit(solution)/shard_map/ppermute | solution.py:29
  115.2 0.7 collective-permute-done.15
  115.9 1.4 collective-permute-start.16
  117.3 2.1 %collective-permute-done.9 = f32[64,128]{0,1:T(8,128)S(1)} collective-permute-done((f32[64,128]{0,1:T(8,128)S(1)}, f32[64,128]{0,1:T(8,128)S(1)}, u32[]{:S(2)}, u32[]{:S(2)}) %collective-permute-start.9) | collective-permute-done | bytes 32800 | tf_op jit(solution)/shard_map/ppermute | solution.py:29
  119.6 0.7 collective-permute-done.16
  120.2 2.6 %collective-permute-start.17 = (f32[64,128]{0,1:T(8,128)S(1)}, f32[64,128]{0,1:T(8,128)S(1)}, u32[]{:S(2)}, u32[]{:S(2)}) collective-permute-start(f32[64,128]{0,1:T(8,128)S(1)} %add.63), channel_id=1, source_target_pairs={{0,24},{1,25},{2,26},{3,27},{4,28},{5,29},{6,30},{7,31},{8,16},{9,... | collective-permute-start | bytes 98312 | tf_op jit(solution)/shard_map/ppermute | solution.py:29
  122.9 2.1 %collective-permute-done.10 = f32[64,128]{0,1:T(8,128)S(1)} collective-permute-done((f32[64,128]{0,1:T(8,128)S(1)}, f32[64,128]{0,1:T(8,128)S(1)}, u32[]{:S(2)}, u32[]{:S(2)}) %collective-permute-start.10) | collective-permute-done | bytes 32800 | tf_op jit(solution)/shard_map/ppermute | solution.py:29
  125.0 0.3 collective-permute-start.11
  125.3 0.5 collective-permute-done.17
  125.8 1.6 collective-permute-start.18
  127.4 2.1 %collective-permute-done.11 = f32[64,128]{0,1:T(8,128)S(1)} collective-permute-done((f32[64,128]{0,1:T(8,128)S(1)}, f32[64,128]{0,1:T(8,128)S(1)}, u32[]{:S(2)}, u32[]{:S(2)}) %collective-permute-start.11) | collective-permute-done | bytes 32800 | tf_op jit(solution)/shard_map/ppermute | solution.py:29
  129.6 3.0 %collective-permute-start.12 = (f32[64,128]{0,1:T(8,128)S(1)}, f32[64,128]{0,1:T(8,128)S(1)}, u32[]{:S(2)}, u32[]{:S(2)}) collective-permute-start(f32[64,128]{0,1:T(8,128)S(1)} %add.58), channel_id=1, source_target_pairs={{0,96},{1,97},{2,98},{3,99},{4,100},{5,101},{6,102},{7,103},{8,104... | collective-permute-start | bytes 98312 | tf_op jit(solution)/shard_map/ppermute | solution.py:29
  132.6 2.3 %collective-permute-start.19 = (f32[64,128]{0,1:T(8,128)S(1)}, f32[64,128]{0,1:T(8,128)S(1)}, u32[]{:S(2)}, u32[]{:S(2)}) collective-permute-start(f32[64,128]{0,1:T(8,128)S(1)} %add.65), channel_id=1, source_target_pairs={{0,96},{1,97},{2,98},{3,99},{4,100},{5,101},{6,102},{7,103},{8,104... | collective-permute-start | bytes 98312 | tf_op jit(solution)/shard_map/ppermute | solution.py:29
  134.9 0.3 collective-permute-done.12
  135.1 3.0 %collective-permute-done.19 = f32[64,128]{0,1:T(8,128)S(1)} collective-permute-done((f32[64,128]{0,1:T(8,128)S(1)}, f32[64,128]{0,1:T(8,128)S(1)}, u32[]{:S(2)}, u32[]{:S(2)}) %collective-permute-start.19) | collective-permute-done | bytes 32800 | tf_op jit(solution)/shard_map/ppermute | solution.py:29
  138.3 11.7 %cholesky.17 = f32[128,128]{1,0:T(8,128)S(1)} custom-call(f32[128,128]{1,0:T(8,128)S(1)} %fusion.1), custom_call_target="Cholesky" | custom-call | tf_op jit(solution)/shard_map/jit(cholesky)/cholesky | solution.py:174
  150.1 0.6 compare_reduce_fusion
  150.7 0.7 fusion.2
  151.4 0.7 copy.15
  152.1 9.8 %custom-call.6 = f32[1,128,128]{1,2,0:T(8,128)S(1)} custom-call(f32[1,128,128]{2,1,0:T(8,128)S(1)} %get-tuple-element.33), custom_call_target="InvertDiagBlocksLowerTriangular" | custom-call | tf_op jit(solution)/shard_map/triangular_solve | solution.py:175
  161.9 0.2 convolution_bitcast_fusion
  162.2 6.5 %fusion.5 = f32[64,128,128]{2,1,0:T(8,128)} fusion(f32[64,128,128]{2,1,0:T(8,128)} %get-tuple-element.24, f32[128,128,1]{1,0,2:T(8,128)S(1)} %convolution_bitcast_fusion), kind=kOutput, calls=%fused_computation.18 | convolution fusion | flops 1610612736 | bytes 8454144 | tf_op jit(solution)/shard_map/dot_general | solution.py:178
  (41 shorter events, 1.3 us)
Async XLA Ops:
  0.6 13.8 %copy-start.6 = (s32[64,8]{0,1:T(8,128)S(1)}, s32[64,8]{0,1:T(8,128)}, u32[]{:S(2)}) copy-start(s32[64,8]{0,1:T(8,128)} %param.7) | copy-start | bytes 6148
  5.4 15.4 %collective-permute-start = (bf16[16,128,128]{2,1,0:T(8,128)(2,1)}, bf16[16,128,128]{2,1,0:T(8,128)(2,1)S(1)}, u32[]{:S(2)}, u32[]{:S(2)}) collective-permute-start(bf16[16,128,128]{2,1,0:T(8,128)(2,1)} %get-tuple-element.14), channel_id=1, source_target_pairs={{0,1},{1,2},{2,3},{3,4},{4,5},{5,6},{6,7},{7,8},{8,9},{9,10},{10,1... | collective-permute-start | bytes 1572872 | tf_op jit(solution)/shard_map/ppermute | solution.py:16
  5.5 15.3 %collective-permute-start.1 = (bf16[16,128,128]{2,1,0:T(8,128)(2,1)}, bf16[16,128,128]{2,1,0:T(8,128)(2,1)S(1)}, u32[]{:S(2)}, u32[]{:S(2)}) collective-permute-start(bf16[16,128,128]{2,1,0:T(8,128)(2,1)} %get-tuple-element.15), channel_id=1, source_target_pairs={{0,127},{1,0},{2,1},{3,2},{4,3},{5,4},{6,5},{7,6},{8,7},{9,8},{10,... | collective-permute-start | bytes 1572872 | tf_op jit(solution)/shard_map/ppermute | solution.py:16
  20.8 0.9 copy-start
  20.8 1.0 copy-start.1
  37.5 14.3 %collective-permute-start.2 = (bf16[16,128,128]{2,1,0:T(8,128)(2,1)}, bf16[16,128,128]{2,1,0:T(8,128)(2,1)S(1)}, u32[]{:S(2)}, u32[]{:S(2)}) collective-permute-start(bf16[16,128,128]{2,1,0:T(8,128)(2,1)} %get-tuple-element.17), channel_id=1, source_target_pairs={{0,1},{1,2},{2,3},{3,4},{4,5},{5,6},{6,7},{7,8},{8,9},{9,10},{10,1... | collective-permute-start | bytes 1572872 | tf_op jit(solution)/shard_map/ppermute | solution.py:16
  37.6 14.2 %collective-permute-start.3 = (bf16[16,128,128]{2,1,0:T(8,128)(2,1)}, bf16[16,128,128]{2,1,0:T(8,128)(2,1)S(1)}, u32[]{:S(2)}, u32[]{:S(2)}) collective-permute-start(bf16[16,128,128]{2,1,0:T(8,128)(2,1)} %get-tuple-element.18), channel_id=1, source_target_pairs={{0,127},{1,0},{2,1},{3,2},{4,3},{5,4},{6,5},{7,6},{8,7},{9,8},{10,... | collective-permute-start | bytes 1572872 | tf_op jit(solution)/shard_map/ppermute | solution.py:16
  51.8 0.9 copy-start.3
  51.8 1.0 copy-start.5
  68.5 14.3 %collective-permute-start.4 = (bf16[16,128,128]{2,1,0:T(8,128)(2,1)}, bf16[16,128,128]{2,1,0:T(8,128)(2,1)S(1)}, u32[]{:S(2)}, u32[]{:S(2)}) collective-permute-start(bf16[16,128,128]{2,1,0:T(8,128)(2,1)} %get-tuple-element.21), channel_id=1, source_target_pairs={{0,1},{1,2},{2,3},{3,4},{4,5},{5,6},{6,7},{7,8},{8,9},{9,10},{10,1... | collective-permute-start | bytes 1572872 | tf_op jit(solution)/shard_map/ppermute | solution.py:16
  68.5 14.2 %collective-permute-start.5 = (bf16[16,128,128]{2,1,0:T(8,128)(2,1)}, bf16[16,128,128]{2,1,0:T(8,128)(2,1)S(1)}, u32[]{:S(2)}, u32[]{:S(2)}) collective-permute-start(bf16[16,128,128]{2,1,0:T(8,128)(2,1)} %get-tuple-element.22), channel_id=1, source_target_pairs={{0,127},{1,0},{2,1},{3,2},{4,3},{5,4},{6,5},{7,6},{8,7},{9,8},{10,... | collective-permute-start | bytes 1572872 | tf_op jit(solution)/shard_map/ppermute | solution.py:16
  82.8 0.8 copy-start.2
  82.8 1.0 copy-start.4
  102.9 1.3 collective-permute-start.6
  103.0 1.4 collective-permute-start.13
  104.5 5.0 %collective-permute-start.7 = (f32[64,128]{0,1:T(8,128)S(1)}, f32[64,128]{0,1:T(8,128)S(1)}, u32[]{:S(2)}, u32[]{:S(2)}) collective-permute-start(f32[64,128]{0,1:T(8,128)S(1)} %get-tuple-element.34), channel_id=1, source_target_pairs={{0,2},{1,3},{2,0},{3,1},{4,6},{5,7},{6,4},{7,5},{8,10},{9,11},{10,... | collective-permute-start | bytes 98312 | tf_op jit(solution)/shard_map/ppermute | solution.py:29
  104.6 5.7 %collective-permute-start.14 = (f32[64,128]{0,1:T(8,128)S(1)}, f32[64,128]{0,1:T(8,128)S(1)}, u32[]{:S(2)}, u32[]{:S(2)}) collective-permute-start(f32[64,128]{0,1:T(8,128)S(1)} %get-tuple-element.35), channel_id=1, source_target_pairs={{0,2},{1,3},{2,0},{3,1},{4,6},{5,7},{6,4},{7,5},{8,10},{9,11},{10,... | collective-permute-start | bytes 98312 | tf_op jit(solution)/shard_map/ppermute | solution.py:29
  109.5 5.6 %collective-permute-start.8 = (f32[64,128]{0,1:T(8,128)S(1)}, f32[64,128]{0,1:T(8,128)S(1)}, u32[]{:S(2)}, u32[]{:S(2)}) collective-permute-start(f32[64,128]{0,1:T(8,128)S(1)} %add.54), channel_id=1, source_target_pairs={{0,6},{1,7},{2,4},{3,5},{4,2},{5,3},{6,0},{7,1},{8,14},{9,15},{10,... | collective-permute-start | bytes 98312 | tf_op jit(solution)/shard_map/ppermute | solution.py:29
  110.3 5.6 %collective-permute-start.15 = (f32[64,128]{0,1:T(8,128)S(1)}, f32[64,128]{0,1:T(8,128)S(1)}, u32[]{:S(2)}, u32[]{:S(2)}) collective-permute-start(f32[64,128]{0,1:T(8,128)S(1)} %add.61), channel_id=1, source_target_pairs={{0,6},{1,7},{2,4},{3,5},{4,2},{5,3},{6,0},{7,1},{8,14},{9,15},{10,... | collective-permute-start | bytes 98312 | tf_op jit(solution)/shard_map/ppermute | solution.py:29
  115.1 4.3 %collective-permute-start.9 = (f32[64,128]{0,1:T(8,128)S(1)}, f32[64,128]{0,1:T(8,128)S(1)}, u32[]{:S(2)}, u32[]{:S(2)}) collective-permute-start(f32[64,128]{0,1:T(8,128)S(1)} %add.55), channel_id=1, source_target_pairs={{0,8},{1,9},{2,10},{3,11},{4,12},{5,13},{6,14},{7,15},{8,0},{9,1},... | collective-permute-start | bytes 98312 | tf_op jit(solution)/shard_map/ppermute | solution.py:29
  115.9 4.3 %collective-permute-start.16 = (f32[64,128]{0,1:T(8,128)S(1)}, f32[64,128]{0,1:T(8,128)S(1)}, u32[]{:S(2)}, u32[]{:S(2)}) collective-permute-start(f32[64,128]{0,1:T(8,128)S(1)} %add.62), channel_id=1, source_target_pairs={{0,8},{1,9},{2,10},{3,11},{4,12},{5,13},{6,14},{7,15},{8,0},{9,1},... | collective-permute-start | bytes 98312 | tf_op jit(solution)/shard_map/ppermute | solution.py:29
  119.5 5.6 %collective-permute-start.10 = (f32[64,128]{0,1:T(8,128)S(1)}, f32[64,128]{0,1:T(8,128)S(1)}, u32[]{:S(2)}, u32[]{:S(2)}) collective-permute-start(f32[64,128]{0,1:T(8,128)S(1)} %add.56), channel_id=1, source_target_pairs={{0,24},{1,25},{2,26},{3,27},{4,28},{5,29},{6,30},{7,31},{8,16},{9,... | collective-permute-start | bytes 98312 | tf_op jit(solution)/shard_map/ppermute | solution.py:29
  120.2 5.6 %collective-permute-start.17 = (f32[64,128]{0,1:T(8,128)S(1)}, f32[64,128]{0,1:T(8,128)S(1)}, u32[]{:S(2)}, u32[]{:S(2)}) collective-permute-start(f32[64,128]{0,1:T(8,128)S(1)} %add.63), channel_id=1, source_target_pairs={{0,24},{1,25},{2,26},{3,27},{4,28},{5,29},{6,30},{7,31},{8,16},{9,... | collective-permute-start | bytes 98312 | tf_op jit(solution)/shard_map/ppermute | solution.py:29
  125.0 4.5 %collective-permute-start.11 = (f32[64,128]{0,1:T(8,128)S(1)}, f32[64,128]{0,1:T(8,128)S(1)}, u32[]{:S(2)}, u32[]{:S(2)}) collective-permute-start(f32[64,128]{0,1:T(8,128)S(1)} %add.57), channel_id=1, source_target_pairs={{0,32},{1,33},{2,34},{3,35},{4,36},{5,37},{6,38},{7,39},{8,40},{9,... | collective-permute-start | bytes 98312 | tf_op jit(solution)/shard_map/ppermute | solution.py:29
  125.8 6.7 %collective-permute-start.18 = (f32[64,128]{0,1:T(8,128)S(1)}, f32[64,128]{0,1:T(8,128)S(1)}, u32[]{:S(2)}, u32[]{:S(2)}) collective-permute-start(f32[64,128]{0,1:T(8,128)S(1)} %add.64), channel_id=1, source_target_pairs={{0,32},{1,33},{2,34},{3,35},{4,36},{5,37},{6,38},{7,39},{8,40},{9,... | collective-permute-start | bytes 98312 | tf_op jit(solution)/shard_map/ppermute | solution.py:29
  129.6 5.6 %collective-permute-start.12 = (f32[64,128]{0,1:T(8,128)S(1)}, f32[64,128]{0,1:T(8,128)S(1)}, u32[]{:S(2)}, u32[]{:S(2)}) collective-permute-start(f32[64,128]{0,1:T(8,128)S(1)} %add.58), channel_id=1, source_target_pairs={{0,96},{1,97},{2,98},{3,99},{4,100},{5,101},{6,102},{7,103},{8,104... | collective-permute-start | bytes 98312 | tf_op jit(solution)/shard_map/ppermute | solution.py:29
  132.6 5.6 %collective-permute-start.19 = (f32[64,128]{0,1:T(8,128)S(1)}, f32[64,128]{0,1:T(8,128)S(1)}, u32[]{:S(2)}, u32[]{:S(2)}) collective-permute-start(f32[64,128]{0,1:T(8,128)S(1)} %add.65), channel_id=1, source_target_pairs={{0,96},{1,97},{2,98},{3,99},{4,100},{5,101},{6,102},{7,103},{8,104... | collective-permute-start | bytes 98312 | tf_op jit(solution)/shard_map/ppermute | solution.py:29

commit v11 on v8

--- a/solution.py
+++ b/solution.py
@@ -88,9 +88,9 @@
         row = step * per_step + r
         acc = jnp.zeros(state_ref.shape[1:], jnp.float32)
         for k in range(nnz):
-            col = cols_ref[row, k]
+            col = cols_ref[row * nnz + k]
             acc = acc + jnp.dot(blocks_ref[r, k], extended[col], preferred_element_type=jnp.float32)
-        new = state_ref[r] + jnp.where(row < count, acc, 0.0)
+        new = jnp.where(row < count, state_ref[r] + acc, 0.0)
         new_state_ref[r] = new
         if not last:
             out_ref[r] = new.astype(jnp.bfloat16)
@@ -157,9 +157,9 @@
 def local(tangent, blocks, columns, counts, send_lists):
     slots, width, vectors = tangent.shape
     live = (jnp.arange(slots, dtype=jnp.int32) < counts[0]).astype(jnp.float32)[:, None, None]
-    state = tangent * live
-    rounded = state.astype(jnp.bfloat16)
-    cols = columns
+    state = tangent
+    rounded = (tangent * live).astype(jnp.bfloat16)
+    cols = columns.reshape(-1)
     sends = send_lists
     to_lower, to_upper = pick_rows(sends, tangent)
     for step in range(SUBSTEPS):
@@ -171,7 +171,7 @@
         else:
             state, gram = substep(cols, counts, sends, rounded, from_lower, from_upper, blocks, state, True)
     flat = state.reshape(slots * width, vectors)
-    first_low = jnp.linalg.cholesky(tree_sum(gram, "grains"))
+    first_low = lax.linalg.cholesky(tree_sum(gram, "grains"), symmetrize_input=False)
     inverse = lax.linalg.triangular_solve(
         first_low, jnp.eye(vectors, dtype=jnp.float32), left_side=True, lower=True
     )

time: 166 us -> 165 us (level)
  waiting for transfers between devices: 42.9 us -> 44.6 us
  transfers between devices with their start and end apart: 13 -> 13, of which waited for: 10 -> 10; matrix products, arithmetic and copies ran while one was open for 4% -> 3% of each run, Pallas kernels for 0% -> 0%
where the time goes in v11:
time: 165 us; the launch traced here: 164 us
  Pallas kernels  53.1 us (32%)
  waiting for transfers between devices  44.6 us (27%)
  other arithmetic  27.7 us (17%)
  starting transfers between devices  25.4 us (15%)
  matrix products  6.8 us (4%)
  local copies, waits for them, and re-layouts  5 us (3%)
    pallas_call x3, Pallas kernels, substep(): pl.pallas_call(kernel, grid_spec=grid_spec, out_shape=[jax.ShapeDtypeStru...  49.5 us
    ppermute x7, waiting for transfers between devices, tree_sum(): value = value + lax.ppermute(value, axis, partner)  28.8 us
    ppermute x6, starting transfers between devices, passed_along(): lax.ppermute(shard, axis, [(i, (i + by) % length) for i in range(length)])  22.8 us
    ppermute x6, waiting for transfers between devices, passed_along(): lax.ppermute(shard, axis, [(i, (i + by) % length) for i in range(length)])  15.8 us
    another operation x3, other arithmetic, local(): lax.linalg.cholesky(tree_sum(gram, 'grains'), symmetrize_input=False)  12.4 us
    another operation x1, other arithmetic, local(): lax.linalg.triangular_solve(first_low, jnp.eye(vectors, dtype=jnp.float32...  9.81 us
    dot_general x1, matrix products, local(): basis = jnp.dot(flat, inverse.T, precision=lax.Precision.HIGHEST)  6.55 us
    unnamed x16, local copies, waits for them, and re-layouts  4.32 us
  transfers between devices with their start and end apart: 13, of which 10 were waited for; matrix products, arithmetic and copies ran while one was open for 3% of the time, Pallas kernels for 0%

profile of v11, /device:TPU:0, one launch (start us, length us, event | category | flops | bytes accessed | tf_op | source)
XLA Modules:
  0.0 164.1 jit_solution(12315958531786314304)
XLA Ops:
  0.6 0.0 copy-start.6
  0.6 3.6 %shard_map.68 = (bf16[16,128,128]{2,1,0:T(8,128)(2,1)}, bf16[16,128,128]{2,1,0:T(8,128)(2,1)}) custom-call(s32[1,2,16]{2,1,0:T(2,128)} %sends_ref.7, f32[64,128,128]{2,1,0:T(8,128)} %state_ref.1), custom_call_target="tpu_custom_call" | custom-call | tf_op jit(solution)/shard_map/pallas_call | solution.py:57
  4.3 0.1 collective-permute-start
  4.4 8.3 %collective-permute-start.1 = (bf16[16,128,128]{2,1,0:T(8,128)(2,1)}, bf16[16,128,128]{2,1,0:T(8,128)(2,1)S(1)}, u32[]{:S(2)}, u32[]{:S(2)}) collective-permute-start(bf16[16,128,128]{2,1,0:T(8,128)(2,1)} %get-tuple-element.15), channel_id=1, source_target_pairs={{0,127},{1,0},{2,1},{3,2},{4,3},{5,4},{6,5},{7,6},{8,7},{9,8},{10,... | collective-permute-start | bytes 1572872 | tf_op jit(solution)/shard_map/ppermute | solution.py:16
  13.3 0.1 copy.8
  13.4 0.7 reshape.24.cols_ref
  14.1 3.9 %multiply_convert_fusion.own_hbm = bf16[64,128,128]{2,1,0:T(8,128)(2,1)} fusion(f32[64,128,128]{2,1,0:T(8,128)} %state_ref.1, f32[64]{0:T(128)S(1)} %compare_convert_fusion), kind=kLoop, calls=%fused_computation | loop fusion | flops 2097152 | bytes 6291712 | tf_op jit(solution)/shard_map/convert_element_type | solution.py:161
  18.0 1.6 collective-permute-done.low_hbm
  19.7 0.0 collective-permute-done.1.high_hbm
  19.7 0.8 copy-done
  20.5 0.8 copy-done.1
  21.2 15.7 %shard_map.69 = (f32[64,128,128]{2,1,0:T(8,128)}, bf16[64,128,128]{2,1,0:T(8,128)(2,1)}, bf16[16,128,128]{2,1,0:T(8,128)(2,1)}, bf16[16,128,128]{2,1,0:T(8,128)(2,1)}) custom-call(s32[512]{0:T(512)} %reshape.24.cols_ref, s32[1]{0:T(128)} %copy.10.count_ref, s32[1,2,16]{2,1,0:T(2,128)} %sends_ref.7, bf16[64,128,128]{2,1,0:T(8,128)(2,1)} %multiply_convert_fusion.own_hbm, ...), custom_call_target="tpu_custom_call" | custom-call | tf_op jit(solution)/shard_map/pallas_call | solution.py:145
  36.9 0.1 collective-permute-start.2
  37.0 7.2 %collective-permute-start.3 = (bf16[16,128,128]{2,1,0:T(8,128)(2,1)}, bf16[16,128,128]{2,1,0:T(8,128)(2,1)S(1)}, u32[]{:S(2)}, u32[]{:S(2)}) collective-permute-start(bf16[16,128,128]{2,1,0:T(8,128)(2,1)} %get-tuple-element.18), channel_id=1, source_target_pairs={{0,127},{1,0},{2,1},{3,2},{4,3},{5,4},{6,5},{7,6},{8,7},{9,8},{10,... | collective-permute-start | bytes 1572872 | tf_op jit(solution)/shard_map/ppermute | solution.py:16
  44.2 7.1 %collective-permute-done.2.low_hbm = bf16[16,128,128]{2,1,0:T(8,128)(2,1)S(1)} collective-permute-done((bf16[16,128,128]{2,1,0:T(8,128)(2,1)}, bf16[16,128,128]{2,1,0:T(8,128)(2,1)S(1)}, u32[]{:S(2)}, u32[]{:S(2)}) %collective-permute-start.2) | collective-permute-done | bytes 524320 | tf_op jit(solution)/shard_map/ppermute | solution.py:16
  51.2 0.0 collective-permute-done.3.high_hbm
  51.2 0.8 copy-done.2
  52.0 0.2 copy-done.4
  52.2 15.7 %shard_map.70 = (f32[64,128,128]{2,1,0:T(8,128)}, bf16[64,128,128]{2,1,0:T(8,128)(2,1)}, bf16[16,128,128]{2,1,0:T(8,128)(2,1)}, bf16[16,128,128]{2,1,0:T(8,128)(2,1)}) custom-call(s32[512]{0:T(512)} %reshape.24.cols_ref, s32[1]{0:T(128)} %copy.10.count_ref, s32[1,2,16]{2,1,0:T(2,128)} %sends_ref.7, bf16[64,128,128]{2,1,0:T(8,128)(2,1)} %get-tuple-element.16.own_hbm, ...), custom_call_target="tpu_custom_call" | custom-call | tf_op jit(solution)/shard_map/pallas_call | solution.py:145
  67.9 0.1 collective-permute-start.4
  68.0 7.2 %collective-permute-start.5 = (bf16[16,128,128]{2,1,0:T(8,128)(2,1)}, bf16[16,128,128]{2,1,0:T(8,128)(2,1)S(1)}, u32[]{:S(2)}, u32[]{:S(2)}) collective-permute-start(bf16[16,128,128]{2,1,0:T(8,128)(2,1)} %get-tuple-element.22), channel_id=1, source_target_pairs={{0,127},{1,0},{2,1},{3,2},{4,3},{5,4},{6,5},{7,6},{8,7},{9,8},{10,... | collective-permute-start | bytes 1572872 | tf_op jit(solution)/shard_map/ppermute | solution.py:16
  75.1 7.1 %collective-permute-done.4.low_hbm = bf16[16,128,128]{2,1,0:T(8,128)(2,1)S(1)} collective-permute-done((bf16[16,128,128]{2,1,0:T(8,128)(2,1)}, bf16[16,128,128]{2,1,0:T(8,128)(2,1)S(1)}, u32[]{:S(2)}, u32[]{:S(2)}) %collective-permute-start.4) | collective-permute-done | bytes 524320 | tf_op jit(solution)/shard_map/ppermute | solution.py:16
  82.2 0.0 collective-permute-done.5.high_hbm
  82.2 0.8 copy-done.3
  83.0 0.2 copy-done.5
  83.2 18.2 %shard_map.71 = (f32[64,128,128]{2,1,0:T(8,128)}, f32[128,128]{1,0:T(8,128)}) custom-call(s32[512]{0:T(512)} %reshape.24.cols_ref, s32[1]{0:T(128)} %copy.10.count_ref, s32[1,2,16]{2,1,0:T(2,128)} %sends_ref.7, bf16[64,128,128]{2,1,0:T(8,128)(2,1)} %get-tuple-element.20.own_hbm, bf16[16,128,128]{2,1,0:T(8,128)(2,1)} %copy-done.3, ...), custom_call_target="tpu_custom_call" | custom-call | tf_op jit(solution)/shard_map/pallas_call | solution.py:145
  101.4 0.1 collective-permute-start.6
  101.4 1.5 collective-permute-done.6
  102.9 0.9 add.27
  103.8 0.1 collective-permute-start.7
  103.8 4.3 %collective-permute-done.7 = f32[128,128]{1,0:T(8,128)S(1)} collective-permute-done((f32[128,128]{1,0:T(8,128)S(1)}, f32[128,128]{1,0:T(8,128)S(1)}, u32[]{:S(2)}, u32[]{:S(2)}) %collective-permute-start.7) | collective-permute-done | bytes 65568 | tf_op jit(solution)/shard_map/ppermute | solution.py:28
  108.1 0.1 collective-permute-start.8
  108.2 5.5 %collective-permute-done.8 = f32[128,128]{1,0:T(8,128)S(1)} collective-permute-done((f32[128,128]{1,0:T(8,128)S(1)}, f32[128,128]{1,0:T(8,128)S(1)}, u32[]{:S(2)}, u32[]{:S(2)}) %collective-permute-start.8) | collective-permute-done | bytes 65568 | tf_op jit(solution)/shard_map/ppermute | solution.py:28
  113.7 0.1 collective-permute-start.9
  113.8 4.3 %collective-permute-done.9 = f32[128,128]{1,0:T(8,128)S(1)} collective-permute-done((f32[128,128]{1,0:T(8,128)S(1)}, f32[128,128]{1,0:T(8,128)S(1)}, u32[]{:S(2)}, u32[]{:S(2)}) %collective-permute-start.9) | collective-permute-done | bytes 65568 | tf_op jit(solution)/shard_map/ppermute | solution.py:28
  118.0 0.1 collective-permute-start.10
  118.1 5.5 %collective-permute-done.10 = f32[128,128]{1,0:T(8,128)S(1)} collective-permute-done((f32[128,128]{1,0:T(8,128)S(1)}, f32[128,128]{1,0:T(8,128)S(1)}, u32[]{:S(2)}, u32[]{:S(2)}) %collective-permute-start.10) | collective-permute-done | bytes 65568 | tf_op jit(solution)/shard_map/ppermute | solution.py:28
  123.6 0.1 collective-permute-start.11
  123.7 4.3 %collective-permute-done.11 = f32[128,128]{1,0:T(8,128)S(1)} collective-permute-done((f32[128,128]{1,0:T(8,128)S(1)}, f32[128,128]{1,0:T(8,128)S(1)}, u32[]{:S(2)}, u32[]{:S(2)}) %collective-permute-start.11) | collective-permute-done | bytes 65568 | tf_op jit(solution)/shard_map/ppermute | solution.py:28
  128.0 2.1 %collective-permute-start.12 = (f32[128,128]{1,0:T(8,128)S(1)}, f32[128,128]{1,0:T(8,128)S(1)}, u32[]{:S(2)}, u32[]{:S(2)}) collective-permute-start(f32[128,128]{1,0:T(8,128)S(1)} %add.32), channel_id=1, source_target_pairs={{0,96},{1,97},{2,98},{3,99},{4,100},{5,101},{6,102},{7,103},{8,104... | collective-permute-start | bytes 196616 | tf_op jit(solution)/shard_map/ppermute | solution.py:28
  130.0 3.7 %collective-permute-done.12 = f32[128,128]{1,0:T(8,128)S(1)} collective-permute-done((f32[128,128]{1,0:T(8,128)S(1)}, f32[128,128]{1,0:T(8,128)S(1)}, u32[]{:S(2)}, u32[]{:S(2)}) %collective-permute-start.12) | collective-permute-done | bytes 65568 | tf_op jit(solution)/shard_map/ppermute | solution.py:28
  133.7 11.7 %cholesky.17 = f32[128,128]{1,0:T(8,128)S(1)} custom-call(f32[128,128]{1,0:T(8,128)S(1)} %add.33), custom_call_target="Cholesky" | custom-call | tf_op jit(solution)/shard_map/cholesky | solution.py:174
  145.5 0.6 compare_reduce_fusion
  146.1 0.7 fusion.1
  146.8 0.7 copy.9
  147.5 9.8 %custom-call.5 = f32[1,128,128]{1,2,0:T(8,128)S(1)} custom-call(f32[1,128,128]{2,1,0:T(8,128)S(1)} %get-tuple-element.31), custom_call_target="InvertDiagBlocksLowerTriangular" | custom-call | tf_op jit(solution)/shard_map/triangular_solve | solution.py:175
  157.3 0.2 convolution_bitcast_fusion
  157.6 6.6 %fusion.2 = f32[64,128,128]{2,1,0:T(8,128)} fusion(f32[64,128,128]{2,1,0:T(8,128)} %get-tuple-element.24, f32[128,128,1]{1,0,2:T(8,128)S(1)} %convolution_bitcast_fusion), kind=kOutput, calls=%fused_computation.11 | convolution fusion | flops 1610612736 | bytes 8454144 | tf_op jit(solution)/shard_map/dot_general | solution.py:178
  (15 shorter events, 0.1 us)
Async XLA Ops:
  0.6 12.7 %copy-start.6 = (s32[64,8]{0,1:T(8,128)S(1)}, s32[64,8]{0,1:T(8,128)}, u32[]{:S(2)}) copy-start(s32[64,8]{0,1:T(8,128)} %param.7) | copy-start | bytes 6148
  4.3 15.4 %collective-permute-start = (bf16[16,128,128]{2,1,0:T(8,128)(2,1)}, bf16[16,128,128]{2,1,0:T(8,128)(2,1)S(1)}, u32[]{:S(2)}, u32[]{:S(2)}) collective-permute-start(bf16[16,128,128]{2,1,0:T(8,128)(2,1)} %get-tuple-element.14), channel_id=1, source_target_pairs={{0,1},{1,2},{2,3},{3,4},{4,5},{5,6},{6,7},{7,8},{8,9},{9,10},{10,1... | collective-permute-start | bytes 1572872 | tf_op jit(solution)/shard_map/ppermute | solution.py:16
  4.4 15.3 %collective-permute-start.1 = (bf16[16,128,128]{2,1,0:T(8,128)(2,1)}, bf16[16,128,128]{2,1,0:T(8,128)(2,1)S(1)}, u32[]{:S(2)}, u32[]{:S(2)}) collective-permute-start(bf16[16,128,128]{2,1,0:T(8,128)(2,1)} %get-tuple-element.15), channel_id=1, source_target_pairs={{0,127},{1,0},{2,1},{3,2},{4,3},{5,4},{6,5},{7,6},{8,7},{9,8},{10,... | collective-permute-start | bytes 1572872 | tf_op jit(solution)/shard_map/ppermute | solution.py:16
  19.7 0.8 copy-start
  20.5 0.8 copy-start.1
  36.9 14.3 %collective-permute-start.2 = (bf16[16,128,128]{2,1,0:T(8,128)(2,1)}, bf16[16,128,128]{2,1,0:T(8,128)(2,1)S(1)}, u32[]{:S(2)}, u32[]{:S(2)}) collective-permute-start(bf16[16,128,128]{2,1,0:T(8,128)(2,1)} %get-tuple-element.17), channel_id=1, source_target_pairs={{0,1},{1,2},{2,3},{3,4},{4,5},{5,6},{6,7},{7,8},{8,9},{9,10},{10,1... | collective-permute-start | bytes 1572872 | tf_op jit(solution)/shard_map/ppermute | solution.py:16
  37.0 14.2 %collective-permute-start.3 = (bf16[16,128,128]{2,1,0:T(8,128)(2,1)}, bf16[16,128,128]{2,1,0:T(8,128)(2,1)S(1)}, u32[]{:S(2)}, u32[]{:S(2)}) collective-permute-start(bf16[16,128,128]{2,1,0:T(8,128)(2,1)} %get-tuple-element.18), channel_id=1, source_target_pairs={{0,127},{1,0},{2,1},{3,2},{4,3},{5,4},{6,5},{7,6},{8,7},{9,8},{10,... | collective-permute-start | bytes 1572872 | tf_op jit(solution)/shard_map/ppermute | solution.py:16
  51.2 0.8 copy-start.2
  51.2 1.0 copy-start.4
  67.9 14.3 %collective-permute-start.4 = (bf16[16,128,128]{2,1,0:T(8,128)(2,1)}, bf16[16,128,128]{2,1,0:T(8,128)(2,1)S(1)}, u32[]{:S(2)}, u32[]{:S(2)}) collective-permute-start(bf16[16,128,128]{2,1,0:T(8,128)(2,1)} %get-tuple-element.21), channel_id=1, source_target_pairs={{0,1},{1,2},{2,3},{3,4},{4,5},{5,6},{6,7},{7,8},{8,9},{9,10},{10,1... | collective-permute-start | bytes 1572872 | tf_op jit(solution)/shard_map/ppermute | solution.py:16
  68.0 14.2 %collective-permute-start.5 = (bf16[16,128,128]{2,1,0:T(8,128)(2,1)}, bf16[16,128,128]{2,1,0:T(8,128)(2,1)S(1)}, u32[]{:S(2)}, u32[]{:S(2)}) collective-permute-start(bf16[16,128,128]{2,1,0:T(8,128)(2,1)} %get-tuple-element.22), channel_id=1, source_target_pairs={{0,127},{1,0},{2,1},{3,2},{4,3},{5,4},{6,5},{7,6},{8,7},{9,8},{10,... | collective-permute-start | bytes 1572872 | tf_op jit(solution)/shard_map/ppermute | solution.py:16
  82.2 0.8 copy-start.3
  82.2 1.0 copy-start.5
  101.4 1.5 collective-permute-start.6
  103.8 4.3 %collective-permute-start.7 = (f32[128,128]{1,0:T(8,128)S(1)}, f32[128,128]{1,0:T(8,128)S(1)}, u32[]{:S(2)}, u32[]{:S(2)}) collective-permute-start(f32[128,128]{1,0:T(8,128)S(1)} %add.27), channel_id=1, source_target_pairs={{0,2},{1,3},{2,0},{3,1},{4,6},{5,7},{6,4},{7,5},{8,10},{9,11},{10,... | collective-permute-start | bytes 196616 | tf_op jit(solution)/shard_map/ppermute | solution.py:28
  108.1 5.6 %collective-permute-start.8 = (f32[128,128]{1,0:T(8,128)S(1)}, f32[128,128]{1,0:T(8,128)S(1)}, u32[]{:S(2)}, u32[]{:S(2)}) collective-permute-start(f32[128,128]{1,0:T(8,128)S(1)} %add.28), channel_id=1, source_target_pairs={{0,6},{1,7},{2,4},{3,5},{4,2},{5,3},{6,0},{7,1},{8,14},{9,15},{10,... | collective-permute-start | bytes 196616 | tf_op jit(solution)/shard_map/ppermute | solution.py:28
  113.7 4.3 %collective-permute-start.9 = (f32[128,128]{1,0:T(8,128)S(1)}, f32[128,128]{1,0:T(8,128)S(1)}, u32[]{:S(2)}, u32[]{:S(2)}) collective-permute-start(f32[128,128]{1,0:T(8,128)S(1)} %add.29), channel_id=1, source_target_pairs={{0,8},{1,9},{2,10},{3,11},{4,12},{5,13},{6,14},{7,15},{8,0},{9,1},... | collective-permute-start | bytes 196616 | tf_op jit(solution)/shard_map/ppermute | solution.py:28
  118.0 5.6 %collective-permute-start.10 = (f32[128,128]{1,0:T(8,128)S(1)}, f32[128,128]{1,0:T(8,128)S(1)}, u32[]{:S(2)}, u32[]{:S(2)}) collective-permute-start(f32[128,128]{1,0:T(8,128)S(1)} %add.30), channel_id=1, source_target_pairs={{0,24},{1,25},{2,26},{3,27},{4,28},{5,29},{6,30},{7,31},{8,16},{9,... | collective-permute-start | bytes 196616 | tf_op jit(solution)/shard_map/ppermute | solution.py:28
  123.6 4.3 %collective-permute-start.11 = (f32[128,128]{1,0:T(8,128)S(1)}, f32[128,128]{1,0:T(8,128)S(1)}, u32[]{:S(2)}, u32[]{:S(2)}) collective-permute-start(f32[128,128]{1,0:T(8,128)S(1)} %add.31), channel_id=1, source_target_pairs={{0,32},{1,33},{2,34},{3,35},{4,36},{5,37},{6,38},{7,39},{8,40},{9,... | collective-permute-start | bytes 196616 | tf_op jit(solution)/shard_map/ppermute | solution.py:28
  128.0 5.7 %collective-permute-start.12 = (f32[128,128]{1,0:T(8,128)S(1)}, f32[128,128]{1,0:T(8,128)S(1)}, u32[]{:S(2)}, u32[]{:S(2)}) collective-permute-start(f32[128,128]{1,0:T(8,128)S(1)} %add.32), channel_id=1, source_target_pairs={{0,96},{1,97},{2,98},{3,99},{4,100},{5,101},{6,102},{7,103},{8,104... | collective-permute-start | bytes 196616 | tf_op jit(solution)/shard_map/ppermute | solution.py:28

commit v12 on v11

--- a/solution.py
+++ b/solution.py
@@ -172,10 +172,10 @@
             state, gram = substep(cols, counts, sends, rounded, from_lower, from_upper, blocks, state, True)
     flat = state.reshape(slots * width, vectors)
     first_low = lax.linalg.cholesky(tree_sum(gram, "grains"), symmetrize_input=False)
-    inverse = lax.linalg.triangular_solve(
-        first_low, jnp.eye(vectors, dtype=jnp.float32), left_side=True, lower=True
+    inverse_t = lax.linalg.triangular_solve(
+        first_low, jnp.eye(vectors, dtype=jnp.float32), left_side=True, lower=True, transpose_a=True
     )
-    basis = jnp.dot(flat, inverse.T, precision=lax.Precision.HIGHEST)
+    basis = jnp.dot(flat, inverse_t, precision=lax.Precision.HIGHEST)
     r_factor = first_low.T
     return (basis.reshape(slots, width, vectors), r_factor)
 

time: 165 us -> 164 us (level)
  no operation moved by 1% of the time
where the time goes in v12:
time: 164 us
  Pallas kernels  53.1 us (32%)
  waiting for transfers between devices  44.6 us (27%)
  other arithmetic  27.7 us (17%)
  starting transfers between devices  25.4 us (15%)
  matrix products  6.7 us (4%)
  local copies, waits for them, and re-layouts  5 us (3%)
    pallas_call x3, Pallas kernels, substep(): pl.pallas_call(kernel, grid_spec=grid_spec, out_shape=[jax.ShapeDtypeStru...  49.5 us
    ppermute x7, waiting for transfers between devices, tree_sum(): value = value + lax.ppermute(value, axis, partner)  28.8 us
    ppermute x6, starting transfers between devices, passed_along(): lax.ppermute(shard, axis, [(i, (i + by) % length) for i in range(length)])  22.8 us
    ppermute x6, waiting for transfers between devices, passed_along(): lax.ppermute(shard, axis, [(i, (i + by) % length) for i in range(length)])  15.8 us
    another operation x3, other arithmetic, local(): lax.linalg.cholesky(tree_sum(gram, 'grains'), symmetrize_input=False)  12.4 us
    another operation x1, other arithmetic, local(): lax.linalg.triangular_solve(first_low, jnp.eye(vectors, dtype=jnp.float32...  9.81 us
    dot_general x1, matrix products, local(): basis = jnp.dot(flat, inverse_t, precision=lax.Precision.HIGHEST)  6.52 us
    unnamed x16, local copies, waits for them, and re-layouts  4.32 us
  transfers between devices with their start and end apart: 13, of which 10 were waited for; matrix products, arithmetic and copies ran while one was open for 3% of the time, Pallas kernels for 0%

profile of v12, /device:TPU:0, one launch (start us, length us, event | category | flops | bytes accessed | tf_op | source)
XLA Modules:
  0.0 164.0 jit_solution(18148039964906720243)
XLA Ops:
  0.6 0.0 copy-start.6
  0.6 3.6 %shard_map.68 = (bf16[16,128,128]{2,1,0:T(8,128)(2,1)}, bf16[16,128,128]{2,1,0:T(8,128)(2,1)}) custom-call(s32[1,2,16]{2,1,0:T(2,128)} %sends_ref.7, f32[64,128,128]{2,1,0:T(8,128)} %state_ref.1), custom_call_target="tpu_custom_call" | custom-call | tf_op jit(solution)/shard_map/pallas_call | solution.py:57
  4.3 0.1 collective-permute-start
  4.4 8.3 %collective-permute-start.1 = (bf16[16,128,128]{2,1,0:T(8,128)(2,1)}, bf16[16,128,128]{2,1,0:T(8,128)(2,1)S(1)}, u32[]{:S(2)}, u32[]{:S(2)}) collective-permute-start(bf16[16,128,128]{2,1,0:T(8,128)(2,1)} %get-tuple-element.15), channel_id=1, source_target_pairs={{0,127},{1,0},{2,1},{3,2},{4,3},{5,4},{6,5},{7,6},{8,7},{9,8},{10,... | collective-permute-start | bytes 1572872 | tf_op jit(solution)/shard_map/ppermute | solution.py:16
  13.3 0.1 copy.8
  13.4 0.7 reshape.24.cols_ref
  14.1 3.9 %multiply_convert_fusion.own_hbm = bf16[64,128,128]{2,1,0:T(8,128)(2,1)} fusion(f32[64,128,128]{2,1,0:T(8,128)} %state_ref.1, f32[64]{0:T(128)S(1)} %compare_convert_fusion), kind=kLoop, calls=%fused_computation | loop fusion | flops 2097152 | bytes 6291712 | tf_op jit(solution)/shard_map/convert_element_type | solution.py:161
  18.0 1.6 collective-permute-done.low_hbm
  19.7 0.0 collective-permute-done.1.high_hbm
  19.7 0.8 copy-done
  20.5 0.8 copy-done.1
  21.2 15.7 %shard_map.69 = (f32[64,128,128]{2,1,0:T(8,128)}, bf16[64,128,128]{2,1,0:T(8,128)(2,1)}, bf16[16,128,128]{2,1,0:T(8,128)(2,1)}, bf16[16,128,128]{2,1,0:T(8,128)(2,1)}) custom-call(s32[512]{0:T(512)} %reshape.24.cols_ref, s32[1]{0:T(128)} %copy.10.count_ref, s32[1,2,16]{2,1,0:T(2,128)} %sends_ref.7, bf16[64,128,128]{2,1,0:T(8,128)(2,1)} %multiply_convert_fusion.own_hbm, ...), custom_call_target="tpu_custom_call" | custom-call | tf_op jit(solution)/shard_map/pallas_call | solution.py:145
  36.9 0.1 collective-permute-start.2
  37.0 7.2 %collective-permute-start.3 = (bf16[16,128,128]{2,1,0:T(8,128)(2,1)}, bf16[16,128,128]{2,1,0:T(8,128)(2,1)S(1)}, u32[]{:S(2)}, u32[]{:S(2)}) collective-permute-start(bf16[16,128,128]{2,1,0:T(8,128)(2,1)} %get-tuple-element.18), channel_id=1, source_target_pairs={{0,127},{1,0},{2,1},{3,2},{4,3},{5,4},{6,5},{7,6},{8,7},{9,8},{10,... | collective-permute-start | bytes 1572872 | tf_op jit(solution)/shard_map/ppermute | solution.py:16
  44.2 7.1 %collective-permute-done.2.low_hbm = bf16[16,128,128]{2,1,0:T(8,128)(2,1)S(1)} collective-permute-done((bf16[16,128,128]{2,1,0:T(8,128)(2,1)}, bf16[16,128,128]{2,1,0:T(8,128)(2,1)S(1)}, u32[]{:S(2)}, u32[]{:S(2)}) %collective-permute-start.2) | collective-permute-done | bytes 524320 | tf_op jit(solution)/shard_map/ppermute | solution.py:16
  51.2 0.0 collective-permute-done.3.high_hbm
  51.2 0.8 copy-done.2
  52.0 0.2 copy-done.4
  52.2 15.7 %shard_map.70 = (f32[64,128,128]{2,1,0:T(8,128)}, bf16[64,128,128]{2,1,0:T(8,128)(2,1)}, bf16[16,128,128]{2,1,0:T(8,128)(2,1)}, bf16[16,128,128]{2,1,0:T(8,128)(2,1)}) custom-call(s32[512]{0:T(512)} %reshape.24.cols_ref, s32[1]{0:T(128)} %copy.10.count_ref, s32[1,2,16]{2,1,0:T(2,128)} %sends_ref.7, bf16[64,128,128]{2,1,0:T(8,128)(2,1)} %get-tuple-element.16.own_hbm, ...), custom_call_target="tpu_custom_call" | custom-call | tf_op jit(solution)/shard_map/pallas_call | solution.py:145
  67.9 0.1 collective-permute-start.4
  68.0 7.2 %collective-permute-start.5 = (bf16[16,128,128]{2,1,0:T(8,128)(2,1)}, bf16[16,128,128]{2,1,0:T(8,128)(2,1)S(1)}, u32[]{:S(2)}, u32[]{:S(2)}) collective-permute-start(bf16[16,128,128]{2,1,0:T(8,128)(2,1)} %get-tuple-element.22), channel_id=1, source_target_pairs={{0,127},{1,0},{2,1},{3,2},{4,3},{5,4},{6,5},{7,6},{8,7},{9,8},{10,... | collective-permute-start | bytes 1572872 | tf_op jit(solution)/shard_map/ppermute | solution.py:16
  75.1 7.1 %collective-permute-done.4.low_hbm = bf16[16,128,128]{2,1,0:T(8,128)(2,1)S(1)} collective-permute-done((bf16[16,128,128]{2,1,0:T(8,128)(2,1)}, bf16[16,128,128]{2,1,0:T(8,128)(2,1)S(1)}, u32[]{:S(2)}, u32[]{:S(2)}) %collective-permute-start.4) | collective-permute-done | bytes 524320 | tf_op jit(solution)/shard_map/ppermute | solution.py:16
  82.2 0.0 collective-permute-done.5.high_hbm
  82.2 0.8 copy-done.3
  83.0 0.2 copy-done.5
  83.2 18.2 %shard_map.71 = (f32[64,128,128]{2,1,0:T(8,128)}, f32[128,128]{1,0:T(8,128)}) custom-call(s32[512]{0:T(512)} %reshape.24.cols_ref, s32[1]{0:T(128)} %copy.10.count_ref, s32[1,2,16]{2,1,0:T(2,128)} %sends_ref.7, bf16[64,128,128]{2,1,0:T(8,128)(2,1)} %get-tuple-element.20.own_hbm, bf16[16,128,128]{2,1,0:T(8,128)(2,1)} %copy-done.3, ...), custom_call_target="tpu_custom_call" | custom-call | tf_op jit(solution)/shard_map/pallas_call | solution.py:145
  101.4 0.1 collective-permute-start.6
  101.4 1.5 collective-permute-done.6
  102.9 0.9 add.27
  103.8 0.1 collective-permute-start.7
  103.8 4.3 %collective-permute-done.7 = f32[128,128]{1,0:T(8,128)S(1)} collective-permute-done((f32[128,128]{1,0:T(8,128)S(1)}, f32[128,128]{1,0:T(8,128)S(1)}, u32[]{:S(2)}, u32[]{:S(2)}) %collective-permute-start.7) | collective-permute-done | bytes 65568 | tf_op jit(solution)/shard_map/ppermute | solution.py:28
  108.1 0.1 collective-permute-start.8
  108.2 5.5 %collective-permute-done.8 = f32[128,128]{1,0:T(8,128)S(1)} collective-permute-done((f32[128,128]{1,0:T(8,128)S(1)}, f32[128,128]{1,0:T(8,128)S(1)}, u32[]{:S(2)}, u32[]{:S(2)}) %collective-permute-start.8) | collective-permute-done | bytes 65568 | tf_op jit(solution)/shard_map/ppermute | solution.py:28
  113.7 0.1 collective-permute-start.9
  113.8 4.3 %collective-permute-done.9 = f32[128,128]{1,0:T(8,128)S(1)} collective-permute-done((f32[128,128]{1,0:T(8,128)S(1)}, f32[128,128]{1,0:T(8,128)S(1)}, u32[]{:S(2)}, u32[]{:S(2)}) %collective-permute-start.9) | collective-permute-done | bytes 65568 | tf_op jit(solution)/shard_map/ppermute | solution.py:28
  118.0 0.1 collective-permute-start.10
  118.1 5.5 %collective-permute-done.10 = f32[128,128]{1,0:T(8,128)S(1)} collective-permute-done((f32[128,128]{1,0:T(8,128)S(1)}, f32[128,128]{1,0:T(8,128)S(1)}, u32[]{:S(2)}, u32[]{:S(2)}) %collective-permute-start.10) | collective-permute-done | bytes 65568 | tf_op jit(solution)/shard_map/ppermute | solution.py:28
  123.6 0.1 collective-permute-start.11
  123.7 4.3 %collective-permute-done.11 = f32[128,128]{1,0:T(8,128)S(1)} collective-permute-done((f32[128,128]{1,0:T(8,128)S(1)}, f32[128,128]{1,0:T(8,128)S(1)}, u32[]{:S(2)}, u32[]{:S(2)}) %collective-permute-start.11) | collective-permute-done | bytes 65568 | tf_op jit(solution)/shard_map/ppermute | solution.py:28
  128.0 2.1 %collective-permute-start.12 = (f32[128,128]{1,0:T(8,128)S(1)}, f32[128,128]{1,0:T(8,128)S(1)}, u32[]{:S(2)}, u32[]{:S(2)}) collective-permute-start(f32[128,128]{1,0:T(8,128)S(1)} %add.32), channel_id=1, source_target_pairs={{0,96},{1,97},{2,98},{3,99},{4,100},{5,101},{6,102},{7,103},{8,104... | collective-permute-start | bytes 196616 | tf_op jit(solution)/shard_map/ppermute | solution.py:28
  130.0 3.7 %collective-permute-done.12 = f32[128,128]{1,0:T(8,128)S(1)} collective-permute-done((f32[128,128]{1,0:T(8,128)S(1)}, f32[128,128]{1,0:T(8,128)S(1)}, u32[]{:S(2)}, u32[]{:S(2)}) %collective-permute-start.12) | collective-permute-done | bytes 65568 | tf_op jit(solution)/shard_map/ppermute | solution.py:28
  133.7 11.7 %cholesky.17 = f32[128,128]{1,0:T(8,128)S(1)} custom-call(f32[128,128]{1,0:T(8,128)S(1)} %add.33), custom_call_target="Cholesky" | custom-call | tf_op jit(solution)/shard_map/cholesky | solution.py:174
  145.5 0.6 compare_reduce_fusion
  146.1 0.7 fusion.1
  146.8 0.7 copy.9
  147.5 9.8 %custom-call.5 = f32[1,128,128]{1,2,0:T(8,128)S(1)} custom-call(f32[1,128,128]{2,1,0:T(8,128)S(1)} %get-tuple-element.31), custom_call_target="InvertDiagBlocksLowerTriangular" | custom-call | tf_op jit(solution)/shard_map/triangular_solve | solution.py:175
  157.3 0.2 convolution_bitcast_fusion
  157.5 6.5 %fusion.2 = f32[64,128,128]{2,1,0:T(8,128)} fusion(f32[64,128,128]{2,1,0:T(8,128)} %get-tuple-element.24, f32[128,128,1]{1,0,2:T(8,128)S(1)} %convolution_bitcast_fusion), kind=kOutput, calls=%fused_computation.11 | convolution fusion | flops 1610612736 | bytes 8454144 | tf_op jit(solution)/shard_map/dot_general | solution.py:178
  (15 shorter events, 0.1 us)
Async XLA Ops:
  0.6 12.7 %copy-start.6 = (s32[64,8]{0,1:T(8,128)S(1)}, s32[64,8]{0,1:T(8,128)}, u32[]{:S(2)}) copy-start(s32[64,8]{0,1:T(8,128)} %param.7) | copy-start | bytes 6148
  4.3 15.4 %collective-permute-start = (bf16[16,128,128]{2,1,0:T(8,128)(2,1)}, bf16[16,128,128]{2,1,0:T(8,128)(2,1)S(1)}, u32[]{:S(2)}, u32[]{:S(2)}) collective-permute-start(bf16[16,128,128]{2,1,0:T(8,128)(2,1)} %get-tuple-element.14), channel_id=1, source_target_pairs={{0,1},{1,2},{2,3},{3,4},{4,5},{5,6},{6,7},{7,8},{8,9},{9,10},{10,1... | collective-permute-start | bytes 1572872 | tf_op jit(solution)/shard_map/ppermute | solution.py:16
  4.4 15.3 %collective-permute-start.1 = (bf16[16,128,128]{2,1,0:T(8,128)(2,1)}, bf16[16,128,128]{2,1,0:T(8,128)(2,1)S(1)}, u32[]{:S(2)}, u32[]{:S(2)}) collective-permute-start(bf16[16,128,128]{2,1,0:T(8,128)(2,1)} %get-tuple-element.15), channel_id=1, source_target_pairs={{0,127},{1,0},{2,1},{3,2},{4,3},{5,4},{6,5},{7,6},{8,7},{9,8},{10,... | collective-permute-start | bytes 1572872 | tf_op jit(solution)/shard_map/ppermute | solution.py:16
  19.7 0.8 copy-start
  20.5 0.8 copy-start.1
  36.9 14.3 %collective-permute-start.2 = (bf16[16,128,128]{2,1,0:T(8,128)(2,1)}, bf16[16,128,128]{2,1,0:T(8,128)(2,1)S(1)}, u32[]{:S(2)}, u32[]{:S(2)}) collective-permute-start(bf16[16,128,128]{2,1,0:T(8,128)(2,1)} %get-tuple-element.17), channel_id=1, source_target_pairs={{0,1},{1,2},{2,3},{3,4},{4,5},{5,6},{6,7},{7,8},{8,9},{9,10},{10,1... | collective-permute-start | bytes 1572872 | tf_op jit(solution)/shard_map/ppermute | solution.py:16
  37.0 14.2 %collective-permute-start.3 = (bf16[16,128,128]{2,1,0:T(8,128)(2,1)}, bf16[16,128,128]{2,1,0:T(8,128)(2,1)S(1)}, u32[]{:S(2)}, u32[]{:S(2)}) collective-permute-start(bf16[16,128,128]{2,1,0:T(8,128)(2,1)} %get-tuple-element.18), channel_id=1, source_target_pairs={{0,127},{1,0},{2,1},{3,2},{4,3},{5,4},{6,5},{7,6},{8,7},{9,8},{10,... | collective-permute-start | bytes 1572872 | tf_op jit(solution)/shard_map/ppermute | solution.py:16
  51.2 0.8 copy-start.2
  51.2 1.0 copy-start.4
  67.9 14.3 %collective-permute-start.4 = (bf16[16,128,128]{2,1,0:T(8,128)(2,1)}, bf16[16,128,128]{2,1,0:T(8,128)(2,1)S(1)}, u32[]{:S(2)}, u32[]{:S(2)}) collective-permute-start(bf16[16,128,128]{2,1,0:T(8,128)(2,1)} %get-tuple-element.21), channel_id=1, source_target_pairs={{0,1},{1,2},{2,3},{3,4},{4,5},{5,6},{6,7},{7,8},{8,9},{9,10},{10,1... | collective-permute-start | bytes 1572872 | tf_op jit(solution)/shard_map/ppermute | solution.py:16
  68.0 14.2 %collective-permute-start.5 = (bf16[16,128,128]{2,1,0:T(8,128)(2,1)}, bf16[16,128,128]{2,1,0:T(8,128)(2,1)S(1)}, u32[]{:S(2)}, u32[]{:S(2)}) collective-permute-start(bf16[16,128,128]{2,1,0:T(8,128)(2,1)} %get-tuple-element.22), channel_id=1, source_target_pairs={{0,127},{1,0},{2,1},{3,2},{4,3},{5,4},{6,5},{7,6},{8,7},{9,8},{10,... | collective-permute-start | bytes 1572872 | tf_op jit(solution)/shard_map/ppermute | solution.py:16
  82.2 0.8 copy-start.3
  82.2 1.0 copy-start.5
  101.4 1.5 collective-permute-start.6
  103.8 4.3 %collective-permute-start.7 = (f32[128,128]{1,0:T(8,128)S(1)}, f32[128,128]{1,0:T(8,128)S(1)}, u32[]{:S(2)}, u32[]{:S(2)}) collective-permute-start(f32[128,128]{1,0:T(8,128)S(1)} %add.27), channel_id=1, source_target_pairs={{0,2},{1,3},{2,0},{3,1},{4,6},{5,7},{6,4},{7,5},{8,10},{9,11},{10,... | collective-permute-start | bytes 196616 | tf_op jit(solution)/shard_map/ppermute | solution.py:28
  108.1 5.6 %collective-permute-start.8 = (f32[128,128]{1,0:T(8,128)S(1)}, f32[128,128]{1,0:T(8,128)S(1)}, u32[]{:S(2)}, u32[]{:S(2)}) collective-permute-start(f32[128,128]{1,0:T(8,128)S(1)} %add.28), channel_id=1, source_target_pairs={{0,6},{1,7},{2,4},{3,5},{4,2},{5,3},{6,0},{7,1},{8,14},{9,15},{10,... | collective-permute-start | bytes 196616 | tf_op jit(solution)/shard_map/ppermute | solution.py:28
  113.7 4.3 %collective-permute-start.9 = (f32[128,128]{1,0:T(8,128)S(1)}, f32[128,128]{1,0:T(8,128)S(1)}, u32[]{:S(2)}, u32[]{:S(2)}) collective-permute-start(f32[128,128]{1,0:T(8,128)S(1)} %add.29), channel_id=1, source_target_pairs={{0,8},{1,9},{2,10},{3,11},{4,12},{5,13},{6,14},{7,15},{8,0},{9,1},... | collective-permute-start | bytes 196616 | tf_op jit(solution)/shard_map/ppermute | solution.py:28
  118.0 5.6 %collective-permute-start.10 = (f32[128,128]{1,0:T(8,128)S(1)}, f32[128,128]{1,0:T(8,128)S(1)}, u32[]{:S(2)}, u32[]{:S(2)}) collective-permute-start(f32[128,128]{1,0:T(8,128)S(1)} %add.30), channel_id=1, source_target_pairs={{0,24},{1,25},{2,26},{3,27},{4,28},{5,29},{6,30},{7,31},{8,16},{9,... | collective-permute-start | bytes 196616 | tf_op jit(solution)/shard_map/ppermute | solution.py:28
  123.6 4.3 %collective-permute-start.11 = (f32[128,128]{1,0:T(8,128)S(1)}, f32[128,128]{1,0:T(8,128)S(1)}, u32[]{:S(2)}, u32[]{:S(2)}) collective-permute-start(f32[128,128]{1,0:T(8,128)S(1)} %add.31), channel_id=1, source_target_pairs={{0,32},{1,33},{2,34},{3,35},{4,36},{5,37},{6,38},{7,39},{8,40},{9,... | collective-permute-start | bytes 196616 | tf_op jit(solution)/shard_map/ppermute | solution.py:28
  128.0 5.7 %collective-permute-start.12 = (f32[128,128]{1,0:T(8,128)S(1)}, f32[128,128]{1,0:T(8,128)S(1)}, u32[]{:S(2)}, u32[]{:S(2)}) collective-permute-start(f32[128,128]{1,0:T(8,128)S(1)} %add.32), channel_id=1, source_target_pairs={{0,96},{1,97},{2,98},{3,99},{4,100},{5,101},{6,102},{7,103},{8,104... | collective-permute-start | bytes 196616 | tf_op jit(solution)/shard_map/ppermute | solution.py:28

commit v13 on v11

--- a/solution.py
+++ b/solution.py
@@ -84,6 +84,7 @@
             copy.wait()
 
     count = count_ref[0]
+    gram = None
     for r in range(per_step):
         row = step * per_step + r
         acc = jnp.zeros(state_ref.shape[1:], jnp.float32)
@@ -97,12 +98,13 @@
             continue
         part = lax.dot_general(new, new, (((0,), (0,)), ((), ())), precision=lax.Precision.HIGHEST,
                                preferred_element_type=jnp.float32)
-        if r == 0:
-            @pl.when(step == 0)
-            def _():
-                out_ref[...] = jnp.zeros_like(out_ref)
-        out_ref[...] += part
+        gram = part if gram is None else gram + part
     if last:
+        @pl.when(step == 0)
+        def _():
+            out_ref[...] = jnp.zeros_like(out_ref)
+
+        out_ref[...] += gram
         return
     half = to_lower_ref.shape[0]
     for j in range(2 * half):

time: 165 us -> 164 us (level)
  no operation moved by 1% of the time
where the time goes in v13:
time: 164 us; the launch traced here: 163 us
  Pallas kernels  52.5 us (32%)
  waiting for transfers between devices  44.6 us (27%)
  other arithmetic  27.7 us (17%)
  starting transfers between devices  25.4 us (15%)
  matrix products  6.8 us (4%)
  local copies, waits for them, and re-layouts  5 us (3%)
    pallas_call x3, Pallas kernels, substep(): pl.pallas_call(kernel, grid_spec=grid_spec, out_shape=[jax.ShapeDtypeStru...  48.9 us
    ppermute x7, waiting for transfers between devices, tree_sum(): value = value + lax.ppermute(value, axis, partner)  28.8 us
    ppermute x6, starting transfers between devices, passed_along(): lax.ppermute(shard, axis, [(i, (i + by) % length) for i in range(length)])  22.8 us
    ppermute x6, waiting for transfers between devices, passed_along(): lax.ppermute(shard, axis, [(i, (i + by) % length) for i in range(length)])  15.8 us
    another operation x3, other arithmetic, local(): lax.linalg.cholesky(tree_sum(gram, 'grains'), symmetrize_input=False)  12.4 us
    another operation x1, other arithmetic, local(): lax.linalg.triangular_solve(first_low, jnp.eye(vectors, dtype=jnp.float32...  9.81 us
    dot_general x1, matrix products, local(): basis = jnp.dot(flat, inverse.T, precision=lax.Precision.HIGHEST)  6.55 us
    unnamed x16, local copies, waits for them, and re-layouts  4.32 us
  transfers between devices with their start and end apart: 13, of which 10 were waited for; matrix products, arithmetic and copies ran while one was open for 3% of the time, Pallas kernels for 0%

profile of v13, /device:TPU:0, one launch (start us, length us, event | category | flops | bytes accessed | tf_op | source)
XLA Modules:
  0.0 163.5 jit_solution(837985723477818397)
XLA Ops:
  0.6 0.0 copy-start.6
  0.6 3.7 %shard_map.68 = (bf16[16,128,128]{2,1,0:T(8,128)(2,1)}, bf16[16,128,128]{2,1,0:T(8,128)(2,1)}) custom-call(s32[1,2,16]{2,1,0:T(2,128)} %sends_ref.7, f32[64,128,128]{2,1,0:T(8,128)} %state_ref.1), custom_call_target="tpu_custom_call" | custom-call | tf_op jit(solution)/shard_map/pallas_call | solution.py:57
  4.3 0.1 collective-permute-start
  4.4 8.3 %collective-permute-start.1 = (bf16[16,128,128]{2,1,0:T(8,128)(2,1)}, bf16[16,128,128]{2,1,0:T(8,128)(2,1)S(1)}, u32[]{:S(2)}, u32[]{:S(2)}) collective-permute-start(bf16[16,128,128]{2,1,0:T(8,128)(2,1)} %get-tuple-element.15), channel_id=1, source_target_pairs={{0,127},{1,0},{2,1},{3,2},{4,3},{5,4},{6,5},{7,6},{8,7},{9,8},{10,... | collective-permute-start | bytes 1572872 | tf_op jit(solution)/shard_map/ppermute | solution.py:16
  13.3 0.1 copy.8
  13.4 0.7 reshape.24.cols_ref
  14.1 3.9 %multiply_convert_fusion.own_hbm = bf16[64,128,128]{2,1,0:T(8,128)(2,1)} fusion(f32[64,128,128]{2,1,0:T(8,128)} %state_ref.1, f32[64]{0:T(128)S(1)} %compare_convert_fusion), kind=kLoop, calls=%fused_computation | loop fusion | flops 2097152 | bytes 6291712 | tf_op jit(solution)/shard_map/convert_element_type | solution.py:163
  18.0 1.6 collective-permute-done.low_hbm
  19.7 0.0 collective-permute-done.1.high_hbm
  19.7 0.8 copy-done
  20.5 0.8 copy-done.1
  21.2 15.7 %shard_map.69 = (f32[64,128,128]{2,1,0:T(8,128)}, bf16[64,128,128]{2,1,0:T(8,128)(2,1)}, bf16[16,128,128]{2,1,0:T(8,128)(2,1)}, bf16[16,128,128]{2,1,0:T(8,128)(2,1)}) custom-call(s32[512]{0:T(512)} %reshape.24.cols_ref, s32[1]{0:T(128)} %copy.10.count_ref, s32[1,2,16]{2,1,0:T(2,128)} %sends_ref.7, bf16[64,128,128]{2,1,0:T(8,128)(2,1)} %multiply_convert_fusion.own_hbm, ...), custom_call_target="tpu_custom_call" | custom-call | tf_op jit(solution)/shard_map/pallas_call | solution.py:147
  36.9 0.1 collective-permute-start.2
  37.0 7.2 %collective-permute-start.3 = (bf16[16,128,128]{2,1,0:T(8,128)(2,1)}, bf16[16,128,128]{2,1,0:T(8,128)(2,1)S(1)}, u32[]{:S(2)}, u32[]{:S(2)}) collective-permute-start(bf16[16,128,128]{2,1,0:T(8,128)(2,1)} %get-tuple-element.18), channel_id=1, source_target_pairs={{0,127},{1,0},{2,1},{3,2},{4,3},{5,4},{6,5},{7,6},{8,7},{9,8},{10,... | collective-permute-start | bytes 1572872 | tf_op jit(solution)/shard_map/ppermute | solution.py:16
  44.2 7.1 %collective-permute-done.2.low_hbm = bf16[16,128,128]{2,1,0:T(8,128)(2,1)S(1)} collective-permute-done((bf16[16,128,128]{2,1,0:T(8,128)(2,1)}, bf16[16,128,128]{2,1,0:T(8,128)(2,1)S(1)}, u32[]{:S(2)}, u32[]{:S(2)}) %collective-permute-start.2) | collective-permute-done | bytes 524320 | tf_op jit(solution)/shard_map/ppermute | solution.py:16
  51.2 0.0 collective-permute-done.3.high_hbm
  51.2 0.8 copy-done.2
  52.0 0.2 copy-done.4
  52.2 15.7 %shard_map.70 = (f32[64,128,128]{2,1,0:T(8,128)}, bf16[64,128,128]{2,1,0:T(8,128)(2,1)}, bf16[16,128,128]{2,1,0:T(8,128)(2,1)}, bf16[16,128,128]{2,1,0:T(8,128)(2,1)}) custom-call(s32[512]{0:T(512)} %reshape.24.cols_ref, s32[1]{0:T(128)} %copy.10.count_ref, s32[1,2,16]{2,1,0:T(2,128)} %sends_ref.7, bf16[64,128,128]{2,1,0:T(8,128)(2,1)} %get-tuple-element.16.own_hbm, ...), custom_call_target="tpu_custom_call" | custom-call | tf_op jit(solution)/shard_map/pallas_call | solution.py:147
  67.9 0.1 collective-permute-start.4
  68.0 7.2 %collective-permute-start.5 = (bf16[16,128,128]{2,1,0:T(8,128)(2,1)}, bf16[16,128,128]{2,1,0:T(8,128)(2,1)S(1)}, u32[]{:S(2)}, u32[]{:S(2)}) collective-permute-start(bf16[16,128,128]{2,1,0:T(8,128)(2,1)} %get-tuple-element.22), channel_id=1, source_target_pairs={{0,127},{1,0},{2,1},{3,2},{4,3},{5,4},{6,5},{7,6},{8,7},{9,8},{10,... | collective-permute-start | bytes 1572872 | tf_op jit(solution)/shard_map/ppermute | solution.py:16
  75.1 7.1 %collective-permute-done.4.low_hbm = bf16[16,128,128]{2,1,0:T(8,128)(2,1)S(1)} collective-permute-done((bf16[16,128,128]{2,1,0:T(8,128)(2,1)}, bf16[16,128,128]{2,1,0:T(8,128)(2,1)S(1)}, u32[]{:S(2)}, u32[]{:S(2)}) %collective-permute-start.4) | collective-permute-done | bytes 524320 | tf_op jit(solution)/shard_map/ppermute | solution.py:16
  82.2 0.0 collective-permute-done.5.high_hbm
  82.2 0.8 copy-done.3
  83.0 0.2 copy-done.5
  83.2 17.5 %shard_map.71 = (f32[64,128,128]{2,1,0:T(8,128)}, f32[128,128]{1,0:T(8,128)}) custom-call(s32[512]{0:T(512)} %reshape.24.cols_ref, s32[1]{0:T(128)} %copy.10.count_ref, s32[1,2,16]{2,1,0:T(2,128)} %sends_ref.7, bf16[64,128,128]{2,1,0:T(8,128)(2,1)} %get-tuple-element.20.own_hbm, bf16[16,128,128]{2,1,0:T(8,128)(2,1)} %copy-done.3, ...), custom_call_target="tpu_custom_call" | custom-call | tf_op jit(solution)/shard_map/pallas_call | solution.py:147
  100.7 0.1 collective-permute-start.6
  100.8 1.5 collective-permute-done.6
  102.3 0.9 add.27
  103.1 0.1 collective-permute-start.7
  103.2 4.3 %collective-permute-done.7 = f32[128,128]{1,0:T(8,128)S(1)} collective-permute-done((f32[128,128]{1,0:T(8,128)S(1)}, f32[128,128]{1,0:T(8,128)S(1)}, u32[]{:S(2)}, u32[]{:S(2)}) %collective-permute-start.7) | collective-permute-done | bytes 65568 | tf_op jit(solution)/shard_map/ppermute | solution.py:28
  107.5 0.1 collective-permute-start.8
  107.6 5.5 %collective-permute-done.8 = f32[128,128]{1,0:T(8,128)S(1)} collective-permute-done((f32[128,128]{1,0:T(8,128)S(1)}, f32[128,128]{1,0:T(8,128)S(1)}, u32[]{:S(2)}, u32[]{:S(2)}) %collective-permute-start.8) | collective-permute-done | bytes 65568 | tf_op jit(solution)/shard_map/ppermute | solution.py:28
  113.0 0.1 collective-permute-start.9
  113.1 4.3 %collective-permute-done.9 = f32[128,128]{1,0:T(8,128)S(1)} collective-permute-done((f32[128,128]{1,0:T(8,128)S(1)}, f32[128,128]{1,0:T(8,128)S(1)}, u32[]{:S(2)}, u32[]{:S(2)}) %collective-permute-start.9) | collective-permute-done | bytes 65568 | tf_op jit(solution)/shard_map/ppermute | solution.py:28
  117.4 0.1 collective-permute-start.10
  117.5 5.5 %collective-permute-done.10 = f32[128,128]{1,0:T(8,128)S(1)} collective-permute-done((f32[128,128]{1,0:T(8,128)S(1)}, f32[128,128]{1,0:T(8,128)S(1)}, u32[]{:S(2)}, u32[]{:S(2)}) %collective-permute-start.10) | collective-permute-done | bytes 65568 | tf_op jit(solution)/shard_map/ppermute | solution.py:28
  123.0 0.1 collective-permute-start.11
  123.1 4.3 %collective-permute-done.11 = f32[128,128]{1,0:T(8,128)S(1)} collective-permute-done((f32[128,128]{1,0:T(8,128)S(1)}, f32[128,128]{1,0:T(8,128)S(1)}, u32[]{:S(2)}, u32[]{:S(2)}) %collective-permute-start.11) | collective-permute-done | bytes 65568 | tf_op jit(solution)/shard_map/ppermute | solution.py:28
  127.3 2.1 %collective-permute-start.12 = (f32[128,128]{1,0:T(8,128)S(1)}, f32[128,128]{1,0:T(8,128)S(1)}, u32[]{:S(2)}, u32[]{:S(2)}) collective-permute-start(f32[128,128]{1,0:T(8,128)S(1)} %add.32), channel_id=1, source_target_pairs={{0,96},{1,97},{2,98},{3,99},{4,100},{5,101},{6,102},{7,103},{8,104... | collective-permute-start | bytes 196616 | tf_op jit(solution)/shard_map/ppermute | solution.py:28
  129.4 3.7 %collective-permute-done.12 = f32[128,128]{1,0:T(8,128)S(1)} collective-permute-done((f32[128,128]{1,0:T(8,128)S(1)}, f32[128,128]{1,0:T(8,128)S(1)}, u32[]{:S(2)}, u32[]{:S(2)}) %collective-permute-start.12) | collective-permute-done | bytes 65568 | tf_op jit(solution)/shard_map/ppermute | solution.py:28
  133.1 11.7 %cholesky.17 = f32[128,128]{1,0:T(8,128)S(1)} custom-call(f32[128,128]{1,0:T(8,128)S(1)} %add.33), custom_call_target="Cholesky" | custom-call | tf_op jit(solution)/shard_map/cholesky | solution.py:176
  144.8 0.6 compare_reduce_fusion
  145.5 0.7 fusion.1
  146.1 0.7 copy.9
  146.9 9.8 %custom-call.5 = f32[1,128,128]{1,2,0:T(8,128)S(1)} custom-call(f32[1,128,128]{2,1,0:T(8,128)S(1)} %get-tuple-element.31), custom_call_target="InvertDiagBlocksLowerTriangular" | custom-call | tf_op jit(solution)/shard_map/triangular_solve | solution.py:177
  156.7 0.2 convolution_bitcast_fusion
  156.9 6.6 %fusion.2 = f32[64,128,128]{2,1,0:T(8,128)} fusion(f32[64,128,128]{2,1,0:T(8,128)} %get-tuple-element.24, f32[128,128,1]{1,0,2:T(8,128)S(1)} %convolution_bitcast_fusion), kind=kOutput, calls=%fused_computation.11 | convolution fusion | flops 1610612736 | bytes 8454144 | tf_op jit(solution)/shard_map/dot_general | solution.py:180
  (15 shorter events, 0.1 us)
Async XLA Ops:
  0.6 12.7 %copy-start.6 = (s32[64,8]{0,1:T(8,128)S(1)}, s32[64,8]{0,1:T(8,128)}, u32[]{:S(2)}) copy-start(s32[64,8]{0,1:T(8,128)} %param.7) | copy-start | bytes 6148
  4.3 15.3 %collective-permute-start = (bf16[16,128,128]{2,1,0:T(8,128)(2,1)}, bf16[16,128,128]{2,1,0:T(8,128)(2,1)S(1)}, u32[]{:S(2)}, u32[]{:S(2)}) collective-permute-start(bf16[16,128,128]{2,1,0:T(8,128)(2,1)} %get-tuple-element.14), channel_id=1, source_target_pairs={{0,1},{1,2},{2,3},{3,4},{4,5},{5,6},{6,7},{7,8},{8,9},{9,10},{10,1... | collective-permute-start | bytes 1572872 | tf_op jit(solution)/shard_map/ppermute | solution.py:16
  4.4 15.3 %collective-permute-start.1 = (bf16[16,128,128]{2,1,0:T(8,128)(2,1)}, bf16[16,128,128]{2,1,0:T(8,128)(2,1)S(1)}, u32[]{:S(2)}, u32[]{:S(2)}) collective-permute-start(bf16[16,128,128]{2,1,0:T(8,128)(2,1)} %get-tuple-element.15), channel_id=1, source_target_pairs={{0,127},{1,0},{2,1},{3,2},{4,3},{5,4},{6,5},{7,6},{8,7},{9,8},{10,... | collective-permute-start | bytes 1572872 | tf_op jit(solution)/shard_map/ppermute | solution.py:16
  19.7 0.8 copy-start
  20.5 0.8 copy-start.1
  36.9 14.3 %collective-permute-start.2 = (bf16[16,128,128]{2,1,0:T(8,128)(2,1)}, bf16[16,128,128]{2,1,0:T(8,128)(2,1)S(1)}, u32[]{:S(2)}, u32[]{:S(2)}) collective-permute-start(bf16[16,128,128]{2,1,0:T(8,128)(2,1)} %get-tuple-element.17), channel_id=1, source_target_pairs={{0,1},{1,2},{2,3},{3,4},{4,5},{5,6},{6,7},{7,8},{8,9},{9,10},{10,1... | collective-permute-start | bytes 1572872 | tf_op jit(solution)/shard_map/ppermute | solution.py:16
  37.0 14.2 %collective-permute-start.3 = (bf16[16,128,128]{2,1,0:T(8,128)(2,1)}, bf16[16,128,128]{2,1,0:T(8,128)(2,1)S(1)}, u32[]{:S(2)}, u32[]{:S(2)}) collective-permute-start(bf16[16,128,128]{2,1,0:T(8,128)(2,1)} %get-tuple-element.18), channel_id=1, source_target_pairs={{0,127},{1,0},{2,1},{3,2},{4,3},{5,4},{6,5},{7,6},{8,7},{9,8},{10,... | collective-permute-start | bytes 1572872 | tf_op jit(solution)/shard_map/ppermute | solution.py:16
  51.2 0.8 copy-start.2
  51.2 1.0 copy-start.4
  67.9 14.3 %collective-permute-start.4 = (bf16[16,128,128]{2,1,0:T(8,128)(2,1)}, bf16[16,128,128]{2,1,0:T(8,128)(2,1)S(1)}, u32[]{:S(2)}, u32[]{:S(2)}) collective-permute-start(bf16[16,128,128]{2,1,0:T(8,128)(2,1)} %get-tuple-element.21), channel_id=1, source_target_pairs={{0,1},{1,2},{2,3},{3,4},{4,5},{5,6},{6,7},{7,8},{8,9},{9,10},{10,1... | collective-permute-start | bytes 1572872 | tf_op jit(solution)/shard_map/ppermute | solution.py:16
  68.0 14.2 %collective-permute-start.5 = (bf16[16,128,128]{2,1,0:T(8,128)(2,1)}, bf16[16,128,128]{2,1,0:T(8,128)(2,1)S(1)}, u32[]{:S(2)}, u32[]{:S(2)}) collective-permute-start(bf16[16,128,128]{2,1,0:T(8,128)(2,1)} %get-tuple-element.22), channel_id=1, source_target_pairs={{0,127},{1,0},{2,1},{3,2},{4,3},{5,4},{6,5},{7,6},{8,7},{9,8},{10,... | collective-permute-start | bytes 1572872 | tf_op jit(solution)/shard_map/ppermute | solution.py:16
  82.2 0.8 copy-start.3
  82.2 1.0 copy-start.5
  100.7 1.5 collective-permute-start.6
  103.1 4.3 %collective-permute-start.7 = (f32[128,128]{1,0:T(8,128)S(1)}, f32[128,128]{1,0:T(8,128)S(1)}, u32[]{:S(2)}, u32[]{:S(2)}) collective-permute-start(f32[128,128]{1,0:T(8,128)S(1)} %add.27), channel_id=1, source_target_pairs={{0,2},{1,3},{2,0},{3,1},{4,6},{5,7},{6,4},{7,5},{8,10},{9,11},{10,... | collective-permute-start | bytes 196616 | tf_op jit(solution)/shard_map/ppermute | solution.py:28
  107.5 5.6 %collective-permute-start.8 = (f32[128,128]{1,0:T(8,128)S(1)}, f32[128,128]{1,0:T(8,128)S(1)}, u32[]{:S(2)}, u32[]{:S(2)}) collective-permute-start(f32[128,128]{1,0:T(8,128)S(1)} %add.28), channel_id=1, source_target_pairs={{0,6},{1,7},{2,4},{3,5},{4,2},{5,3},{6,0},{7,1},{8,14},{9,15},{10,... | collective-permute-start | bytes 196616 | tf_op jit(solution)/shard_map/ppermute | solution.py:28
  113.0 4.3 %collective-permute-start.9 = (f32[128,128]{1,0:T(8,128)S(1)}, f32[128,128]{1,0:T(8,128)S(1)}, u32[]{:S(2)}, u32[]{:S(2)}) collective-permute-start(f32[128,128]{1,0:T(8,128)S(1)} %add.29), channel_id=1, source_target_pairs={{0,8},{1,9},{2,10},{3,11},{4,12},{5,13},{6,14},{7,15},{8,0},{9,1},... | collective-permute-start | bytes 196616 | tf_op jit(solution)/shard_map/ppermute | solution.py:28
  117.4 5.6 %collective-permute-start.10 = (f32[128,128]{1,0:T(8,128)S(1)}, f32[128,128]{1,0:T(8,128)S(1)}, u32[]{:S(2)}, u32[]{:S(2)}) collective-permute-start(f32[128,128]{1,0:T(8,128)S(1)} %add.30), channel_id=1, source_target_pairs={{0,24},{1,25},{2,26},{3,27},{4,28},{5,29},{6,30},{7,31},{8,16},{9,... | collective-permute-start | bytes 196616 | tf_op jit(solution)/shard_map/ppermute | solution.py:28
  123.0 4.3 %collective-permute-start.11 = (f32[128,128]{1,0:T(8,128)S(1)}, f32[128,128]{1,0:T(8,128)S(1)}, u32[]{:S(2)}, u32[]{:S(2)}) collective-permute-start(f32[128,128]{1,0:T(8,128)S(1)} %add.31), channel_id=1, source_target_pairs={{0,32},{1,33},{2,34},{3,35},{4,36},{5,37},{6,38},{7,39},{8,40},{9,... | collective-permute-start | bytes 196616 | tf_op jit(solution)/shard_map/ppermute | solution.py:28
  127.3 5.7 %collective-permute-start.12 = (f32[128,128]{1,0:T(8,128)S(1)}, f32[128,128]{1,0:T(8,128)S(1)}, u32[]{:S(2)}, u32[]{:S(2)}) collective-permute-start(f32[128,128]{1,0:T(8,128)S(1)} %add.32), channel_id=1, source_target_pairs={{0,96},{1,97},{2,98},{3,99},{4,100},{5,101},{6,102},{7,103},{8,104... | collective-permute-start | bytes 196616 | tf_op jit(solution)/shard_map/ppermute | solution.py:28
